TPU v7x, 256 devices: a whole 4x4x8 slice. The times are simulated.
256 devices in a mesh: pool: 32 (over y, z), tp: 8 (over x, core).
Axes of the slice: x: 4, y: 4, z: 8, core: 2. Of those that a mesh axis runs over, the one named last changes fastest.
Arguments:
- pool_kv: bfloat16 [8192, 8, 2, 16, 128], P('pool', 'tp')
- span_pages: int32 [64, 128], replicated, may hold values from 0 to 8191, as said below
- req_spans: int32 [64, 4], replicated, may hold values from 0 to 63, as said below
- span_offsets: int32 [64, 4], replicated, may hold values from 0 to 6144, as said below
- recompute_rows: int32 [64, 4, 104], replicated, may hold values from 0 to 2047, as said below
- question_lengths: int32 [64], replicated, may hold values from 32 to 64
- question_q: bfloat16 [64, 64, 40, 128], P('pool', None, 'tp')
- question_kv: bfloat16 [64, 64, 2, 8, 128], P('pool', None, None, 'tp')
- recompute_hidden: bfloat16 [64, 4, 104, 5120], P('pool', None, None, 'tp')
- w_kv: bfloat16 [5120, 2, 8, 128], P(None, None, 'tp'), may hold values from -0.25 to 0.25
- w_out: bfloat16 [5120, 5120], P('tp'), may hold values from -0.078125 to 0.078125
Outputs:
- attn_out: bfloat16 [64, 64, 5120], P('pool', None, 'tp')
Inputs may be any that keep to these rules, and one draw needn't show every extreme that they name: `span_pages`: page ids are distinct; page p is slot p mod 256 of pool index p // 256; every span has exactly 4 of its pages on each pool index. `req_spans`: the spans of one request are distinct. `span_offsets`: each request's offsets are 2048 times 0 to 3 in some order. `recompute_rows`: the rows of one request's slot are distinct.
All inputs are finite; a program needn't handle non-finite values.
Results may differ from a plain program's by a relative error of at most 0.012.
Values may be sent and summed in bfloat16 or wider, within the bound.
No kernel may reach another device: no remote copies, remote signals or barrier semaphores. Data moves between devices by JAX's collectives and lax.ppermute only.
A program may use at most 192 MiB of HBM per device.

v0:
```python
import jax
import jax.numpy as jnp
from jax import lax
from jax.sharding import PartitionSpec as P

THETA = 1000000.0
NEGATIVE = -1e30


def rotate(vectors, position):
    halfway = vectors.shape[-1] // 2
    frequency = THETA ** (-(jnp.arange(halfway, dtype=jnp.float32) * 2.0) / vectors.shape[-1])
    angles = position[..., None] * frequency
    cosine_part = jnp.cos(angles)
    sine_part = jnp.sin(angles)
    leading = vectors[..., :halfway]
    trailing = vectors[..., halfway:]
    return jnp.concatenate(
        [
            leading * cosine_part - trailing * sine_part,
            trailing * cosine_part + leading * sine_part,
        ],
        axis=-1,
    )


def summarize(scores, valid):
    masked = jnp.where(valid, scores, NEGATIVE)
    peak = jnp.max(masked, axis=-1)
    powers = jnp.where(valid, jnp.exp(masked - peak[..., None]), 0.0)
    return (peak, jnp.sum(powers, axis=-1), powers.astype(jnp.bfloat16))


def combine(former, latter):
    peak = jnp.maximum(former[0], latter[0])
    former_factor = jnp.exp(former[0] - peak)
    latter_factor = jnp.exp(latter[0] - peak)
    return (
        peak,
        former[1] * former_factor + latter[1] * latter_factor,
        former[2] * former_factor[..., None] + latter[2] * latter_factor[..., None],
    )


def merge_normalised(peaks, sums, normalised, axis):
    merged_peak = jnp.max(peaks, axis=axis)
    weight = sums * jnp.exp(peaks - jnp.expand_dims(merged_peak, axis))
    return (
        merged_peak,
        jnp.sum(weight, axis=axis),
        jnp.sum(normalised.astype(jnp.float32) * weight[..., None], axis=axis),
    )


def local_pages(pages, device, pages_dev, peer_pages):
    here = pages // pages_dev == device
    ranking = jnp.cumsum(here.astype(jnp.int32), axis=-1) - 1
    picks = here[..., None, :] & (
        ranking[..., None, :] == jnp.arange(peer_pages, dtype=jnp.int32)[:, None]
    )
    slot_ids = jnp.sum(jnp.where(picks, (pages % pages_dev)[..., None, :], 0), axis=-1)
    page_index = jnp.sum(jnp.where(picks, jnp.arange(pages.shape[-1], dtype=jnp.int32), 0), axis=-1)
    return (slot_ids, page_index)


def shards(
    pool_kv,
    span_pages,
    req_spans,
    span_offsets,
    recompute_rows,
    question_lengths,
    question_q,
    question_kv,
    recompute_hidden,
    w_kv,
    w_out,
):
    pool_count = lax.axis_size("pool")
    device = lax.axis_index("pool")
    req_dev = question_q.shape[0]
    qlen = question_q.shape[1]
    heads = question_q.shape[2]
    head_dim = question_q.shape[3]
    pages_dev = pool_kv.shape[0]
    kv_heads = pool_kv.shape[1]
    page_rows = pool_kv.shape[3]
    group_size = heads // kv_heads
    n_slots = req_spans.shape[1]
    pages_span = span_pages.shape[1]
    span_rows = pages_span * page_rows
    peer_pages = pages_span // pool_count
    score_scale = head_dim ** (-0.5)
    first_request = device * req_dev
    own_spans = lax.dynamic_slice_in_dim(req_spans, first_request, req_dev, 0)
    own_offsets = lax.dynamic_slice_in_dim(span_offsets, first_request, req_dev, 0).astype(
        jnp.float32
    )
    own_rows = lax.dynamic_slice_in_dim(recompute_rows, first_request, req_dev, 0)
    own_lengths = lax.dynamic_slice_in_dim(question_lengths, first_request, req_dev, 0)
    steps_q = jnp.arange(qlen, dtype=jnp.int32)
    qpos = (n_slots * span_rows + steps_q).astype(jnp.float32)
    queries = rotate(question_q.astype(jnp.float32), qpos[None, :, None]).astype(jnp.bfloat16)
    grouped = queries.reshape(req_dev, qlen, kv_heads, group_size, head_dim)
    own_keys = rotate(question_kv[:, :, 0].astype(jnp.float32), qpos[None, :, None]).astype(
        jnp.bfloat16
    )
    own_values = question_kv[:, :, 1]
    hidden = lax.all_gather(recompute_hidden, "tp", axis=3, tiled=True)
    widened = hidden.astype(jnp.float32)
    normed = (
        widened * lax.rsqrt(jnp.mean(widened * widened, axis=-1, keepdims=True) + 1e-06)
    ).astype(jnp.bfloat16)
    fresh = jnp.einsum("rcnd,dskh->rcnskh", normed, w_kv, preferred_element_type=jnp.float32)
    fresh_pos = own_offsets[:, :, None] + own_rows.astype(jnp.float32)
    fresh_keys = rotate(fresh[:, :, :, 0], fresh_pos[..., None]).astype(jnp.bfloat16)
    fresh_values = fresh[:, :, :, 1].astype(jnp.bfloat16)
    fresh_scores = (
        jnp.einsum("rqkgd,rcnkd->rqkgcn", grouped, fresh_keys, preferred_element_type=jnp.float32)
        * score_scale
    )
    fresh_scores = fresh_scores.reshape(req_dev, qlen, kv_heads, group_size, -1)
    fresh_peak, fresh_sum, fresh_weights = summarize(fresh_scores, True)
    fresh_acc = jnp.einsum(
        "rqkgn,rnkd->rqkgd",
        fresh_weights,
        fresh_values.reshape(req_dev, -1, kv_heads, head_dim),
        preferred_element_type=jnp.float32,
    )
    visible = (steps_q[None, None, :] <= steps_q[None, :, None]) & (
        steps_q[None, None, :] < own_lengths[:, None, None]
    )
    own_scores = (
        jnp.einsum("rqkgd,rjkd->rqkgj", grouped, own_keys, preferred_element_type=jnp.float32)
        * score_scale
    )
    own_peak, own_sum, own_weights = summarize(own_scores, visible[:, :, None, None, :])
    own_acc = jnp.einsum(
        "rqkgj,rjkd->rqkgd", own_weights, own_values, preferred_element_type=jnp.float32
    )
    all_pages = span_pages[req_spans]
    slot_ids, unused_index = local_pages(all_pages, device, pages_dev, peer_pages)
    outgoing = pool_kv[slot_ids]
    outgoing = outgoing.reshape((pool_count, req_dev) + outgoing.shape[1:])
    arrived = lax.all_to_all(outgoing, "pool", split_axis=0, concat_axis=0, tiled=True)
    mine = span_pages[own_spans]
    unused_slots, page_index = local_pages(
        mine[:, :, None, :], jnp.arange(pool_count, dtype=jnp.int32)[:, None], pages_dev, peer_pages
    )
    row_ids = page_index[..., None] * page_rows + jnp.arange(page_rows, dtype=jnp.int32)
    replaced = jnp.any(row_ids[..., None] == own_rows[:, :, None, None, None, :], axis=-1)
    key_rows = rotate(
        arrived[:, :, :, :, :, 0].astype(jnp.float32), own_offsets[None, :, :, None, None, None]
    ).astype(jnp.bfloat16)
    cached_scores = (
        jnp.einsum("rqkgd,srcpktd->rqkgscpt", grouped, key_rows, preferred_element_type=jnp.float32)
        * score_scale
    )
    flat_scores = cached_scores.reshape(req_dev, qlen, kv_heads, group_size, pool_count, -1)
    flat_valid = (
        jnp.logical_not(replaced).transpose(0, 2, 1, 3, 4).reshape(req_dev, 1, 1, 1, pool_count, -1)
    )
    part_peak, part_sum, part_weights = summarize(flat_scores, flat_valid)
    part_weights = part_weights.reshape(cached_scores.shape)
    part_acc = jnp.einsum(
        "rqkgscpt,srcpktd->rqkgsd",
        part_weights,
        arrived[:, :, :, :, :, 1],
        preferred_element_type=jnp.float32,
    )
    part_norm = (part_acc / jnp.maximum(part_sum, 1.0)[..., None]).astype(jnp.bfloat16)
    cached = merge_normalised(part_peak, part_sum, part_norm, 4)
    total = combine(
        combine(cached, (fresh_peak, fresh_sum, fresh_acc)), (own_peak, own_sum, own_acc)
    )
    attn = total[2] / total[1][..., None]
    live = steps_q[None, :] < own_lengths[:, None]
    attn = (
        jnp.where(live[:, :, None, None, None], attn, 0.0)
        .astype(jnp.bfloat16)
        .reshape(req_dev, qlen, heads * head_dim)
    )
    partial_out = jnp.einsum("rqh,hm->rqm", attn, w_out, preferred_element_type=jnp.float32)
    return lax.psum_scatter(partial_out, "tp", scatter_dimension=2, tiled=True).astype(jnp.bfloat16)


def solution(mesh):
    return jax.shard_map(
        shards,
        mesh=mesh,
        in_specs=(
            P("pool", "tp", None, None, None),
            P(),
            P(),
            P(),
            P(),
            P(),
            P("pool", None, "tp", None),
            P("pool", None, None, "tp", None),
            P("pool", None, None, "tp"),
            P(None, None, "tp", None),
            P("tp", None),
        ),
        out_specs=P("pool", None, "tp"),
        check_vma=False,
    )
```

profile of v0, /device:TPU:1, one launch (start us, length us, event | category | flops | bytes accessed | tf_op | source)
XLA Modules:
  0.0 386.6 jit_solution(1894640211045437952)
XLA Ops:
  8.2 1.5 gather_fusion
  9.8 1.2 reduce_window_sum.22
  11.8 11.5 %gather_fusion.1 = bf16[1024,2,16,128]{3,2,1,0:T(8,128)(2,1)} fusion(bf16[256,2,16,128]{3,2,1,0:T(8,128)(2,1)} %bitcast.232, s32[1024]{0:T(1024)S(1)} %broadcast_clamp_fusion), kind=kCustom, calls=%fused_computation.1 | custom fusion | bytes 16781312 | tf_op jit(solution)/shard_map/gather | solution.py:143
  23.3 9.9 %copy.69 = bf16[32,2,4,4,1,2,16,128]{7,6,3,2,1,5,4,0:T(8,128)(2,1)} copy(bf16[32,2,4,4,1,2,16,128]{7,6,5,3,2,1,0,4:T(8,128)(2,1)} %bitcast.231) | data formatting | bytes 16777216 | tf_op jit(solution)/shard_map/reshape | solution.py:144
  33.2 12.4 %all-to-all-start = ((bf16[32,2,4,4,1,2,16,128]{7,6,3,2,1,5,4,0:T(8,128)(2,1)}), bf16[32,2,4,4,1,2,16,128]{7,6,3,2,1,5,4,0:T(8,128)(2,1)}, u32[]{:S(2)}, u32[]{:S(2)}) async-start(bf16[32,2,4,4,1,2,16,128]{7,6,3,2,1,5,4,0:T(8,128)(2,1)} %copy.69), calls=%async_computation | async-start | bytes 16777216 | tf_op jit(solution)/shard_map/all_to_all | solution.py:145
  47.1 2.3 reduce_window_sum.23
  55.8 21.0 %compare_reduce_fusion = pred[2,4,32,4,16]{4,3,2,1,0:T(4,128)(4,1)} fusion(s32[2,4,104]{2,1,0:T(4,128)S(1)} %get-tuple-element.15, s32[2,4,32,4,16]{4,3,2,1,0:T(4,128)S(1)} %iota_add_fusion), kind=kLoop, calls=%fused_computation.27 | loop fusion | flops 3391488 | bytes 85248 | tf_op jit(solution)/shard_map/reduce_or | solution.py:151
  76.9 5.3 %fusion.9 = f32[2,4,104]{2,1,0:T(4,128)S(1)} fusion(bf16[2,4,104,5120]{3,2,1,0:T(8,128)(2,1)} %all-gather.2.cloned.1.call-done), kind=kLoop, calls=%fused_computation.17 | loop fusion | flops 12778688 | bytes 8523008 | tf_op jit(solution)/shard_map/reduce_sum | solution.py:112
  82.7 2.6 fusion.28
  86.1 1.8 fusion.61
  89.3 1.6 reshape.640
  91.3 142.8 %all-to-all-done = bf16[32,2,4,4,1,2,16,128]{7,6,3,2,1,5,4,0:T(8,128)(2,1)} async-done(((bf16[32,2,4,4,1,2,16,128]{7,6,3,2,1,5,4,0:T(8,128)(2,1)}), bf16[32,2,4,4,1,2,16,128]{7,6,3,2,1,5,4,0:T(8,128)(2,1)}, u32[]{:S(2)}, u32[]{:S(2)}) %all-to-all-start) | async-done | bytes 8388640 | tf_op jit(solution)/shard_map/all_to_all | solution.py:145
  234.2 6.3 %fusion.94 = (bf16[32,2,4,4,1,1,16,128]{7,6,3,2,1,5,4,0:T(8,128)(2,1)}, bf16[32,2,4,4,1,1,16,128]{7,6,3,2,1,5,4,0:T(8,128)(2,1)S(1)}) fusion(bf16[32,2,4,4,1,2,16,128]{7,6,3,2,1,5,4,0:T(8,128)(2,1)} %all-to-all-done), kind=kLoop, calls=%fused_computation.169 | loop fusion | bytes 16777216 | tf_op jit(solution)/shard_map/slice | solution.py:168
  240.4 1.1 fusion.24
  241.6 4.2 %fusion.18 = (bf16[32,2,4,4,16,64]{5,4,3,2,0,1:T(8,128)(2,1)S(1)}, bf16[32,2,4,4,16,64]{5,4,3,2,0,1:T(8,128)(2,1)}) fusion(f32[32,2,4,4,1,16,128]{6,5,3,2,0,1,4:T(8,128)S(1)} %fusion.24, f32[2,4,64]{2,1,0:T(4,128)S(1)} %get-tuple-element.34, f32[2,4,64]{2,1,0:T(4,128)S(1)} %get-tuple-element.33), kind=kLoop, calls=%fused_computation.30 | loop fusion | flops 8388608 | bytes 12587008 | tf_op jit(solution)/shard_map/concatenate | solution.py:18
  245.7 20.7 %bitcast_reduce_fusion.1 = (f32[2,64,5,32]{1,2,3,0:T(8,128)S(1)}, f32[2,32,4,4,16,64,5]{5,4,6,3,2,1,0:T(8,128)}) fusion(bf16[2,64,5,64]{3,1,2,0:T(8,128)(2,1)S(1)} %get-tuple-element.25, bf16[2,64,5,64]{3,1,2,0:T(8,128)(2,1)S(1)} %get-tuple-element.24, bf16[32,2,4,4,16,64]{5,4,3,2,0,1:T(8,128)(2,1)} %get-tuple-element.19, ...), kind=kOutput, calls=%fused_computation.5 | convolution fusion | flops 1366618112 | bytes 25427968 | tf_op jit(solution)/shard_map/rqkgd,srcpktd->rqkgscpt/dot_general | solution.py:156
  266.4 28.3 %fusion.2 = (f32[2,64,5,32]{1,2,3,0:T(8,128)S(1)}, f32[2,64,5]{1,2,0:T(8,128)S(1)}) fusion(f32[2,32,4,4,16,64,5]{5,4,6,3,2,1,0:T(8,128)} %get-tuple-element.42, f32[2,64,5,32]{1,2,3,0:T(8,128)S(1)} %get-tuple-element.41, pred[2,4,32,4,16]{4,3,2,1,0:T(4,128)(4,1)S(1)} %copy-done.4), kind=kLoop, calls=%fused_computation.9 | loop fusion | flops 31452544 | bytes 21154304 | tf_op jit(solution)/shard_map/reduce_sum | solution.py:31
  294.7 0.9 fusion.91
  295.7 1.0 fusion.42
  296.7 28.3 %multiply_reduce_fusion = f32[2,64,5,128]{3,1,2,0:T(8,128)} fusion(f32[2,64,5,32]{1,2,3,0:T(8,128)} %get-tuple-element.13, f32[2,64,5,32]{1,2,3,0:T(8,128)} %get-tuple-element.26, f32[2,32,4,4,16,64,5]{5,4,6,3,2,1,0:T(8,128)} %get-tuple-element.42, f32[2,64,5,32]{1,2,3,0:T(8,128)S(1)} %get-tuple-element.41, ...), kind=kOutput, calls=%fused_computation.21 | convolution fusion | flops 1381433344 | bytes 25755648 | tf_op jit(solution)/shard_map/rqkgscpt,srcpktd->rqkgsd/dot_general | solution.py:165
  325.0 1.9 fusion.43
  327.3 5.6 %fusion.16 = f32[2,64,5120]{2,1,0:T(8,128)} fusion(bf16[2,64,640]{2,1,0:T(8,128)(2,1)S(1)} %reshape.643, bf16[640,5120]{1,0:T(8,128)(2,1)} %param.21), kind=kOutput, calls=%fused_computation.28 | convolution fusion | flops 838860800 | bytes 9338880 | tf_op jit(solution)/shard_map/rqh,hm->rqm/dot_general | solution.py:183
  332.8 45.0 %reduce-scatter.2.cloned.1.call-done = f32[2,64,640]{2,1,0:T(8,128)} async-done(((f32[2,64,5120]{2,1,0:T(8,128)}), f32[2,64,640]{2,1,0:T(8,128)}) %reduce-scatter.2.cloned.1.call-update) | async-done | bytes 327696 | tf_op jit(solution)/shard_map/reduce_scatter | solution.py:184
  377.9 1.7 convert_element_type.149
  (98 shorter events, 13.7 us)
Async XLA Ops:
  6.5 75.6 %copy-start = (bf16[5120,2,1,128]{3,1,2,0:T(2,128)(2,1)S(1)}, bf16[5120,2,1,128]{3,1,2,0:T(2,128)(2,1)}, u32[]{:S(2)}) copy-start(bf16[5120,2,1,128]{3,1,2,0:T(2,128)(2,1)} %param.20) | copy-start | bytes 7864324
  6.5 70.3 %all-gather.2.cloned.1.call-start = ((), (), s32[]{:S(2)}) async-start(), calls=%async_computation.2 | async-start | bytes 9584640 | tf_op jit(solution)/shard_map/all_gather | solution.py:109
  33.2 13.0 %copy-start.15 = (s32[64,4]{0,1:T(4,128)S(1)}, s32[64,4]{0,1:T(4,128)}, u32[]{:S(2)}) copy-start(s32[64,4]{0,1:T(4,128)} %param.13) | copy-start | bytes 3076
  33.2 13.0 %copy-start.18 = (s32[64,4]{0,1:T(4,128)S(1)}, s32[64,4]{0,1:T(4,128)}, u32[]{:S(2)}) copy-start(s32[64,4]{0,1:T(4,128)} %param.14) | copy-start | bytes 3076
  33.2 13.3 %copy-start.2 = (s32[64,128]{1,0:T(8,128)S(1)}, s32[64,128]{1,0:T(8,128)}, u32[]{:S(2)}) copy-start(s32[64,128]{1,0:T(8,128)} %param.12) | copy-start | bytes 98308
  33.2 17.7 %copy-start.8 = (bf16[2,64,5,128]{3,1,2,0:T(8,128)(2,1)S(1)}, bf16[2,64,5,128]{3,1,2,0:T(8,128)(2,1)}, u32[]{:S(2)}) copy-start(bf16[2,64,5,128]{3,1,2,0:T(8,128)(2,1)} %param.17) | copy-start | bytes 491524
  33.2 17.7 %copy-start.21 = (s32[64]{0:T(128)S(1)}, s32[64]{0:T(128)}, u32[]{:S(2)}) copy-start(s32[64]{0:T(128)} %param.16) | copy-start | bytes 772
  33.2 18.6 %copy-start.7 = (bf16[2,64,2,1,128]{4,2,3,1,0:T(2,128)(2,1)S(1)}, bf16[2,64,2,1,128]{4,2,3,1,0:T(2,128)(2,1)}, u32[]{:S(2)}) copy-start(bf16[2,64,2,1,128]{4,2,3,1,0:T(2,128)(2,1)} %param.18) | copy-start | bytes 196612
  33.2 200.9 %all-to-all-start = ((bf16[32,2,4,4,1,2,16,128]{7,6,3,2,1,5,4,0:T(8,128)(2,1)}), bf16[32,2,4,4,1,2,16,128]{7,6,3,2,1,5,4,0:T(8,128)(2,1)}, u32[]{:S(2)}, u32[]{:S(2)}) async-start(bf16[32,2,4,4,1,2,16,128]{7,6,3,2,1,5,4,0:T(8,128)(2,1)} %copy.69), calls=%async_computation | async-start | bytes 16777216 | tf_op jit(solution)/shard_map/all_to_all | solution.py:145
  45.6 332.2 %reduce-scatter.2.cloned.1.call-start = ((), (), s32[]{:S(2)}) async-start(), calls=%async_computation.3 | async-start | bytes 2949120 | tf_op jit(solution)/shard_map/reduce_scatter | solution.py:184
  51.0 3.7 copy-start.16
  53.2 32.1 %copy-start.10 = (f32[2,64,5]{1,2,0:T(8,128)}, f32[2,64,5]{1,2,0:T(8,128)S(1)}, u32[]{:S(2)}) copy-start(f32[2,64,5]{1,2,0:T(8,128)S(1)} %get-tuple-element.37) | copy-start | bytes 7684
  76.9 5.8 %copy-start.3 = (bf16[2,4,104,5120]{3,2,1,0:T(8,128)(2,1)S(1)}, bf16[2,4,104,5120]{3,2,1,0:T(8,128)(2,1)}, u32[]{:S(2)}) copy-start(bf16[2,4,104,5120]{3,2,1,0:T(8,128)(2,1)} %all-gather.2.cloned.1.call-done) | copy-start | bytes 25559044
  82.7 3.4 copy-start.17
  88.4 152.0 %copy-start.12 = (f32[2,64,5]{1,2,0:T(8,128)}, f32[2,64,5]{1,2,0:T(8,128)S(1)}, u32[]{:S(2)}) copy-start(f32[2,64,5]{1,2,0:T(8,128)S(1)} %get-tuple-element.39) | copy-start | bytes 7684
  241.5 4.2 %copy-start.4 = (pred[2,4,32,4,16]{4,3,2,1,0:T(4,128)(4,1)S(1)}, pred[2,4,32,4,16]{4,3,2,1,0:T(4,128)(4,1)}, u32[]{:S(2)}) copy-start(pred[2,4,32,4,16]{4,3,2,1,0:T(4,128)(4,1)} %compare_reduce_fusion) | copy-start | bytes 49156
  266.4 29.2 %copy-start.11 = (f32[2,64,5]{1,2,0:T(8,128)S(1)}, f32[2,64,5]{1,2,0:T(8,128)}, u32[]{:S(2)}) copy-start(f32[2,64,5]{1,2,0:T(8,128)} %copy-done.10) | copy-start | bytes 7684
  266.4 29.2 %copy-start.13 = (f32[2,64,5]{1,2,0:T(8,128)S(1)}, f32[2,64,5]{1,2,0:T(8,128)}, u32[]{:S(2)}) copy-start(f32[2,64,5]{1,2,0:T(8,128)} %copy-done.12) | copy-start | bytes 7684
  266.4 29.2 %copy-start.14 = (f32[2,64,5]{1,2,0:T(8,128)S(1)}, f32[2,64,5]{1,2,0:T(8,128)}, u32[]{:S(2)}) copy-start(f32[2,64,5]{1,2,0:T(8,128)} %fusion.56) | copy-start | bytes 7684
  266.4 29.3 %copy-start.9 = (bf16[2,64,1,1,128]{4,2,3,1,0:T(2,128)(2,1)S(1)}, bf16[2,64,1,1,128]{4,2,3,1,0:T(2,128)(2,1)}, u32[]{:S(2)}) copy-start(bf16[2,64,1,1,128]{4,2,3,1,0:T(2,128)(2,1)} %get-tuple-element.29) | copy-start | bytes 98308
  266.4 30.3 %copy-start.5 = (pred[2,4,32,4,16]{4,3,2,1,0:T(4,128)(4,1)S(1)}, pred[2,4,32,4,16]{4,3,2,1,0:T(4,128)(4,1)}, u32[]{:S(2)}) copy-start(pred[2,4,32,4,16]{4,3,2,1,0:T(4,128)(4,1)} %compare_reduce_fusion) | copy-start | bytes 49156
  296.7 28.3 %copy-start.6 = (f32[2,64,1,5,128]{4,1,3,0,2:T(8,128)S(1)}, f32[2,64,1,5,128]{4,1,3,0,2:T(8,128)}, u32[]{:S(2)}) copy-start(f32[2,64,1,5,128]{4,1,3,0,2:T(8,128)} %fusion.42) | copy-start | bytes 983044
  296.7 28.3 %copy-start.20 = (pred[2,64]{1,0:T(4,128)(4,1)S(1)}, pred[2,64]{1,0:T(4,128)(4,1)}, u32[]{:S(2)}) copy-start(pred[2,64]{1,0:T(4,128)(4,1)} %copy-done.19) | copy-start | bytes 388
  296.7 82.9 %copy-start.1 = (bf16[5120,2,1,128]{3,1,2,0:T(2,128)(2,1)S(1)}, bf16[5120,2,1,128]{3,1,2,0:T(2,128)(2,1)}, u32[]{:S(2)}) copy-start(bf16[5120,2,1,128]{3,1,2,0:T(2,128)(2,1)} %param.20) | copy-start | bytes 7864324
  (1 other events, 0.6 us)
Sparse Core Ops, SparseCore 0:
  9.2 56.8 all-gather.1
  333.0 44.8 reduce-scatter.1
where the time goes:
time: 392 us; the launch traced here: 387 us
  waiting for transfers between devices  189 us (48%)
  other arithmetic  73.6 us (19%)
  matrix products  60.9 us (16%)
  local copies, waits for them, and re-layouts  36.6 us (9%)
  between operations  14 us (4%)
  starting transfers between devices  12.9 us (3%)
    all_to_all x1, waiting for transfers between devices, shards(): lax.all_to_all(outgoing, 'pool', split_axis=0, concat_axis=0, tiled=True)  143 us
    reduce_scatter x1, waiting for transfers between devices, shards(): lax.psum_scatter(partial_out, 'tp', scatter_dimension=2, tiled=True)  45 us
    reduce_sum x3, other arithmetic, summarize(): return (peak, jnp.sum(powers, axis=-1), powers.astype(jnp.bfloat16))  29.4 us
    dot_general x1, matrix products, shards(): jnp.einsum('rqkgscpt,srcpktd->rqkgsd', part_weights, arrived[:, :, :, :,...  28.3 us
    reduce_or x1, other arithmetic, shards(): jnp.any(row_ids[..., None] == own_rows[:, :, None, None, None, :], axis=-1)  21 us
    dot_general x1, matrix products, shards(): jnp.einsum('rqkgd,srcpktd->rqkgscpt', grouped, key_rows, preferred_elemen...  20.7 us
    all_to_all x1, starting transfers between devices, shards(): lax.all_to_all(outgoing, 'pool', split_axis=0, concat_axis=0, tiled=True)  12.4 us
    gather x1, local copies, waits for them, and re-layouts, shards(): outgoing = pool_kv[slot_ids]  11.5 us
  transfers between devices with their start and end apart: 3, of which 2 were waited for; matrix products, arithmetic and copies ran while one was open for 18% of the time, Pallas kernels for 0%

commit v1 on v0

--- a/solution.py
+++ b/solution.py
@@ -29,27 +29,6 @@
     peak = jnp.max(masked, axis=-1)
     powers = jnp.where(valid, jnp.exp(masked - peak[..., None]), 0.0)
     return (peak, jnp.sum(powers, axis=-1), powers.astype(jnp.bfloat16))
-
-
-def combine(former, latter):
-    peak = jnp.maximum(former[0], latter[0])
-    former_factor = jnp.exp(former[0] - peak)
-    latter_factor = jnp.exp(latter[0] - peak)
-    return (
-        peak,
-        former[1] * former_factor + latter[1] * latter_factor,
-        former[2] * former_factor[..., None] + latter[2] * latter_factor[..., None],
-    )
-
-
-def merge_normalised(peaks, sums, normalised, axis):
-    merged_peak = jnp.max(peaks, axis=axis)
-    weight = sums * jnp.exp(peaks - jnp.expand_dims(merged_peak, axis))
-    return (
-        merged_peak,
-        jnp.sum(weight, axis=axis),
-        jnp.sum(normalised.astype(jnp.float32) * weight[..., None], axis=axis),
-    )
 
 
 def local_pages(pages, device, pages_dev, peer_pages):
@@ -86,13 +65,13 @@
     kv_heads = pool_kv.shape[1]
     page_rows = pool_kv.shape[3]
     group_size = heads // kv_heads
+    n_req = req_spans.shape[0]
     n_slots = req_spans.shape[1]
     pages_span = span_pages.shape[1]
     span_rows = pages_span * page_rows
     peer_pages = pages_span // pool_count
     score_scale = head_dim ** (-0.5)
     first_request = device * req_dev
-    own_spans = lax.dynamic_slice_in_dim(req_spans, first_request, req_dev, 0)
     own_offsets = lax.dynamic_slice_in_dim(span_offsets, first_request, req_dev, 0).astype(
         jnp.float32
     )
@@ -102,6 +81,46 @@
     qpos = (n_slots * span_rows + steps_q).astype(jnp.float32)
     queries = rotate(question_q.astype(jnp.float32), qpos[None, :, None]).astype(jnp.bfloat16)
     grouped = queries.reshape(req_dev, qlen, kv_heads, group_size, head_dim)
+    all_queries = lax.all_gather(queries, "pool", axis=0, tiled=True)
+
+    all_pages = span_pages[req_spans]
+    slot_ids, page_index = local_pages(all_pages, device, pages_dev, peer_pages)
+    local_kv = pool_kv[slot_ids][:, :, :, 0]
+    all_offsets = span_offsets.astype(jnp.float32)
+    local_keys = rotate(
+        local_kv[:, :, :, 0].astype(jnp.float32), all_offsets[:, :, None, None]
+    ).astype(jnp.bfloat16)
+    local_keys = local_keys.reshape(n_req, -1, head_dim)
+    local_values = local_kv[:, :, :, 1].reshape(n_req, -1, head_dim)
+    marks = jnp.zeros((n_req, n_slots, span_rows), jnp.bool_)
+    marks = marks.at[
+        jnp.arange(n_req)[:, None, None], jnp.arange(n_slots)[None, :, None], recompute_rows
+    ].set(True)
+    row_ids = page_index[..., None] * page_rows + jnp.arange(page_rows, dtype=jnp.int32)
+    replaced = jnp.take_along_axis(
+        marks, row_ids.reshape(n_req, n_slots, -1), axis=2
+    ).reshape(n_req, 1, 1, -1)
+    cached_scores = (
+        jnp.einsum("rqhd,rkd->rqhk", all_queries, local_keys, preferred_element_type=jnp.float32)
+        * score_scale
+    )
+    part_peak, part_sum, part_weights = summarize(cached_scores, jnp.logical_not(replaced))
+    part_acc = jnp.einsum(
+        "rqhk,rkd->rqhd", part_weights, local_values, preferred_element_type=jnp.float32
+    )
+    part_norm = (part_acc / jnp.maximum(part_sum, 1.0)[..., None]).astype(jnp.bfloat16)
+    cached_peak = lax.pmax(part_peak, "pool")
+    part_weight = part_sum * jnp.exp(part_peak - cached_peak)
+    part_num = part_norm.astype(jnp.float32) * part_weight[..., None]
+    cached_num = lax.psum_scatter(part_num, "pool", scatter_dimension=0, tiled=True)
+    cached_sum = lax.psum_scatter(part_weight, "pool", scatter_dimension=0, tiled=True)
+    cached_peak = lax.dynamic_slice_in_dim(cached_peak, first_request, req_dev, 0)
+    cached = (
+        cached_peak.reshape(req_dev, qlen, kv_heads, group_size),
+        cached_sum.reshape(req_dev, qlen, kv_heads, group_size),
+        cached_num.reshape(req_dev, qlen, kv_heads, group_size, head_dim),
+    )
+
     own_keys = rotate(question_kv[:, :, 0].astype(jnp.float32), qpos[None, :, None]).astype(
         jnp.bfloat16
     )
@@ -138,42 +157,18 @@
     own_acc = jnp.einsum(
         "rqkgj,rjkd->rqkgd", own_weights, own_values, preferred_element_type=jnp.float32
     )
-    all_pages = span_pages[req_spans]
-    slot_ids, unused_index = local_pages(all_pages, device, pages_dev, peer_pages)
-    outgoing = pool_kv[slot_ids]
-    outgoing = outgoing.reshape((pool_count, req_dev) + outgoing.shape[1:])
-    arrived = lax.all_to_all(outgoing, "pool", split_axis=0, concat_axis=0, tiled=True)
-    mine = span_pages[own_spans]
-    unused_slots, page_index = local_pages(
-        mine[:, :, None, :], jnp.arange(pool_count, dtype=jnp.int32)[:, None], pages_dev, peer_pages
-    )
-    row_ids = page_index[..., None] * page_rows + jnp.arange(page_rows, dtype=jnp.int32)
-    replaced = jnp.any(row_ids[..., None] == own_rows[:, :, None, None, None, :], axis=-1)
-    key_rows = rotate(
-        arrived[:, :, :, :, :, 0].astype(jnp.float32), own_offsets[None, :, :, None, None, None]
-    ).astype(jnp.bfloat16)
-    cached_scores = (
-        jnp.einsum("rqkgd,srcpktd->rqkgscpt", grouped, key_rows, preferred_element_type=jnp.float32)
-        * score_scale
-    )
-    flat_scores = cached_scores.reshape(req_dev, qlen, kv_heads, group_size, pool_count, -1)
-    flat_valid = (
-        jnp.logical_not(replaced).transpose(0, 2, 1, 3, 4).reshape(req_dev, 1, 1, 1, pool_count, -1)
-    )
-    part_peak, part_sum, part_weights = summarize(flat_scores, flat_valid)
-    part_weights = part_weights.reshape(cached_scores.shape)
-    part_acc = jnp.einsum(
-        "rqkgscpt,srcpktd->rqkgsd",
-        part_weights,
-        arrived[:, :, :, :, :, 1],
-        preferred_element_type=jnp.float32,
-    )
-    part_norm = (part_acc / jnp.maximum(part_sum, 1.0)[..., None]).astype(jnp.bfloat16)
-    cached = merge_normalised(part_peak, part_sum, part_norm, 4)
-    total = combine(
-        combine(cached, (fresh_peak, fresh_sum, fresh_acc)), (own_peak, own_sum, own_acc)
-    )
-    attn = total[2] / total[1][..., None]
+
+    peak = jnp.maximum(jnp.maximum(cached[0], fresh_peak), own_peak)
+    cached_factor = jnp.exp(cached[0] - peak)
+    fresh_factor = jnp.exp(fresh_peak - peak)
+    own_factor = jnp.exp(own_peak - peak)
+    weight_sum = cached[1] * cached_factor + fresh_sum * fresh_factor + own_sum * own_factor
+    numerator = (
+        cached[2] * cached_factor[..., None]
+        + fresh_acc * fresh_factor[..., None]
+        + own_acc * own_factor[..., None]
+    )
+    attn = numerator / weight_sum[..., None]
     live = steps_q[None, :] < own_lengths[:, None]
     attn = (
         jnp.where(live[:, :, None, None, None], attn, 0.0)

time: 392 us -> 984 us (2.51)
  waiting for transfers between devices: 189 us -> 588 us
  local copies, waits for them, and re-layouts: 36.6 us -> 289 us
  other arithmetic: 73.6 us -> 47.1 us
  matrix products: 60.9 us -> 41.7 us
  starting transfers between devices: 12.9 us -> 0.44 us
    reduce_scatter x0 -> x2, waiting for transfers between devices: none -> 418 us  [the longest x1 238 us: shards(): lax.psum_scatter(part_num, 'pool', scatter_dimension=0, tiled=True)]
    gather x2 -> x5, local copies, waits for them, and re-layouts: 12 us -> 166 us  [the longest x4 154 us: shards(): jnp.take_along_axis(marks, row_ids.reshape(n_req, n_slots, -1), axis=2)]
    all_to_all x1 -> x0, waiting for transfers between devices: 143 us -> none  [shards(): lax.all_to_all(outgoing, 'pool', split_axis=0, concat_axis=0, tiled=True)]
    pmax x0 -> x1, waiting for transfers between devices: none -> 132 us  [shards(): cached_peak = lax.pmax(part_peak, 'pool')]
    unnamed x44 -> x19, local copies, waits for them, and re-layouts: 1.09 us -> 114 us
    reduce_or x1 -> x0, other arithmetic: 21 us -> none  [shards(): jnp.any(row_ids[..., None] == own_rows[:, :, None, None, None, :], axis=-1)]
    dot_general x2, matrix products: 48.9 us -> 29.8 us  [the longest x1 15.9 us: shards(): jnp.einsum('rqhd,rkd->rqhk', all_queries, local_keys, preferred_element_t...]
    reduce_sum x3, other arithmetic: 29.4 us -> 14.4 us  [summarize(): return (peak, jnp.sum(powers, axis=-1), powers.astype(jnp.bfloat16))]
  transfers between devices with their start and end apart: 3 -> 6, of which waited for: 2 -> 4; matrix products, arithmetic and copies ran while one was open for 18% -> 36% of each run, Pallas kernels for 0% -> 0%
where the time goes in v1:
time: 984 us; the launch traced here: 982 us
  waiting for transfers between devices  588 us (60%)
  local copies, waits for them, and re-layouts  289 us (29%)
  other arithmetic  47.1 us (5%)
  matrix products  41.7 us (4%)
  between operations  15 us (2%)
    reduce_scatter x1, waiting for transfers between devices, shards(): lax.psum_scatter(part_num, 'pool', scatter_dimension=0, tiled=True)  238 us
    reduce_scatter x1, waiting for transfers between devices, shards(): lax.psum_scatter(part_weight, 'pool', scatter_dimension=0, tiled=True)  180 us
    gather x4, local copies, waits for them, and re-layouts, shards(): jnp.take_along_axis(marks, row_ids.reshape(n_req, n_slots, -1), axis=2)  154 us
    pmax x1, waiting for transfers between devices, shards(): cached_peak = lax.pmax(part_peak, 'pool')  132 us
    unnamed x19, local copies, waits for them, and re-layouts  114 us
    reduce_scatter x1, waiting for transfers between devices, shards(): lax.psum_scatter(partial_out, 'tp', scatter_dimension=2, tiled=True)  37.5 us
  transfers between devices with their start and end apart: 6, of which 4 were waited for; matrix products, arithmetic and copies ran while one was open for 36% of the time, Pallas kernels for 0%

profile of v1, /device:TPU:1, one launch (start us, length us, event | category | flops | bytes accessed | tf_op | source)
XLA Modules:
  0.0 981.5 jit_solution(2416802428726064187)
XLA Ops:
  10.7 1.5 gather_fusion
  17.7 112.1 %scatter_custom_fusion = pred[524288]{0:T(1024)(128)(4,1)} fusion(s32[26624]{0:T(1024)S(1)} %reshape.505, pred[26624]{0:T(1024)(128)(4,1)S(1)} %broadcast.417, pred[]{:T(512)} %constant.49.clone.1), kind=kCustom, calls=%fused_computation.54 | custom fusion | bytes 524289
  129.8 1.3 reshape.478
  131.1 154.0 %gather_fusion.2 = pred[16384]{0:T(1024)(128)(4,1)S(1)} fusion(pred[64,4,2048]{2,1,0:T(4,128)(4,1)S(1)} %reshape.478, s32[16384]{0:T(1024)S(1)} %reshape.499), kind=kCustom, calls=%fused_computation.2 | custom fusion | bytes 229376 | tf_op jit(solution)/shard_map/jit(take_along_axis)/gather | solution.py:100
  285.7 11.5 %gather_fusion.1 = bf16[1024,2,16,128]{3,2,1,0:T(8,128)(2,1)} fusion(bf16[256,2,16,128]{3,2,1,0:T(8,128)(2,1)} %bitcast.166, s32[1024]{0:T(1024)S(1)} %broadcast_clamp_fusion), kind=kCustom, calls=%fused_computation.1 | custom fusion | bytes 16781312 | tf_op jit(solution)/shard_map/gather | solution.py:88
  298.3 6.1 fusion.87
  304.4 5.1 subtract_convert_fusion
  309.6 15.9 %fusion = (f32[64,64,5]{1,2,0:T(8,128)}, f32[64,64,5,256]{3,1,2,0:T(8,128)}) fusion(pred[64,256]{1,0:T(8,128)(4,1)S(1)} %select_not_fusion, bf16[64,64,5,128]{3,1,2,0:T(8,128)(2,1)} %all-gather.3.cloned.1.call-done, bf16[64,256,64]{2,1,0:T(8,128)(2,1)} %bitcast.168, bf16[64,256,64]{2,1,0:T(8,128)(2,1)} %bitcast.167), kind=kOutput, calls=%fused_computation.8 | convolution fusion | flops 1366274048 | bytes 30507008 | tf_op jit(solution)/shard_map/rqhd,rkd->rqhk/dot_general | solution.py:104
  326.1 12.7 %fusion.3 = f32[64,64,5]{1,2,0:T(8,128)S(1)} fusion(f32[64,64,5,256]{3,1,2,0:T(8,128)} %get-tuple-element.36, f32[64,64,5]{1,2,0:T(8,128)} %get-tuple-element.35, pred[64,256]{1,0:T(8,128)(4,1)S(1)} %select_not_fusion), kind=kLoop, calls=%fused_computation.11 | loop fusion | flops 26193920 | bytes 21151744 | tf_op jit(solution)/shard_map/reduce_sum | solution.py:31
  338.8 132.2 %all-reduce.2.cloned.1.call-done = f32[64,64,5]{1,2,0:T(8,128)} async-done(((f32[64,64,5]{1,2,0:T(8,128)}), f32[64,64,5]{1,2,0:T(8,128)}) %all-reduce.2.cloned.1.call-update) | async-done | bytes 81936 | tf_op jit(solution)/shard_map/pmax | solution.py:112
  470.9 1.7 broadcast_maximum_fusion
  472.7 13.9 %convert_multiply_fusion.2 = f32[64,64,5,128]{3,1,2,0:T(8,128)} fusion(f32[64,64,5]{1,2,0:T(8,128)} %get-tuple-element.22, f32[64,64,5]{1,2,0:T(8,128)S(1)} %get-tuple-element.21, bf16[64,256,128,1]{2,1,3,0:T(8,128)(2,1)} %bitcast.169, f32[64,64,5,256]{3,1,2,0:T(8,128)} %get-tuple-element.36, f32[64,64,5]{1,2,0:T(8,128)S(1)} %copy-done.3, ...), kind=kOutput, calls=%fused_computation.14 | convolution fusion | flops 1378877440 | bytes 35913728 | tf_op jit(solution)/shard_map/rqhk,rkd->rqhd/dot_general | solution.py:108
  489.6 5.3 fusion.1
  495.4 2.6 fusion.26
  498.1 1.8 fusion.59
  501.6 1.9 copy.117
  503.5 2.8 reshape.471
  506.3 1.7 exponential_reduce_fusion
  508.0 180.0 %reduce-scatter.6.cloned.1.call-done = f32[2,64,5]{1,2,0:T(8,128)} async-done(((f32[64,64,5]{1,2,0:T(8,128)}), f32[2,64,5]{1,2,0:T(8,128)}) %reduce-scatter.6.cloned.1.call-update) | async-done | bytes 2576 | tf_op jit(solution)/shard_map/reduce_scatter | solution.py:116
  689.9 237.6 %reduce-scatter.4.cloned.1.call-done = f32[2,64,5,128]{3,1,2,0:T(8,128)} async-done(((f32[64,64,5,128]{3,1,2,0:T(8,128)}), f32[2,64,5,128]{3,1,2,0:T(8,128)}) %reduce-scatter.4.cloned.1.call-update) | async-done | bytes 327696 | tf_op jit(solution)/shard_map/reduce_scatter | solution.py:115
  927.5 1.8 fusion.40
  929.6 5.6 fusion.16
  935.2 37.5 %reduce-scatter.8.cloned.1.call-done = f32[2,64,640]{2,1,0:T(8,128)} async-done(((f32[2,64,5120]{2,1,0:T(8,128)}), f32[2,64,640]{2,1,0:T(8,128)}) %reduce-scatter.8.cloned.1.call-update) | async-done | bytes 327696 | tf_op jit(solution)/shard_map/reduce_scatter | solution.py:179
  972.7 1.7 convert_element_type.131
  (91 shorter events, 18.3 us)
Async XLA Ops:
  7.4 487.5 %copy-start = (bf16[5120,2,1,128]{3,1,2,0:T(2,128)(2,1)S(1)}, bf16[5120,2,1,128]{3,1,2,0:T(2,128)(2,1)}, u32[]{:S(2)}) copy-start(bf16[5120,2,1,128]{3,1,2,0:T(2,128)(2,1)} %param.20) | copy-start | bytes 7864324
  7.4 302.2 %all-gather.3.cloned.1.call-start = ((), (), s32[]{:S(2)}) async-start(), calls=%async_computation.3 | async-start | bytes 5406720 | tf_op jit(solution)/shard_map/all_gather | solution.py:84
  9.7 461.2 %all-reduce.2.cloned.1.call-start = ((), (), s32[]{:S(2)}) async-start(), calls=%async_computation.4 | async-start | bytes 524288 | tf_op jit(solution)/shard_map/pmax | solution.py:112
  131.1 154.5 %copy-start.6 = (s32[64,4]{0,1:T(4,128)S(1)}, s32[64,4]{0,1:T(4,128)}, u32[]{:S(2)}) copy-start(s32[64,4]{0,1:T(4,128)} %param.14) | copy-start | bytes 3076
  325.5 164.1 %all-gather.5.cloned.1.call-start = ((), (), s32[]{:S(2)}) async-start(), calls=%async_computation.6 | async-start | bytes 9584640 | tf_op jit(solution)/shard_map/all_gather | solution.py:128
  326.0 362.0 %reduce-scatter.6.cloned.1.call-start = ((), (), s32[]{:S(2)}) async-start(), calls=%async_computation.7 | async-start | bytes 270336 | tf_op jit(solution)/shard_map/reduce_scatter | solution.py:116
  326.1 144.8 %copy-start.3 = (f32[64,64,5]{1,2,0:T(8,128)S(1)}, f32[64,64,5]{1,2,0:T(8,128)}, u32[]{:S(2)}) copy-start(f32[64,64,5]{1,2,0:T(8,128)} %get-tuple-element.35) | copy-start | bytes 245764
  472.7 454.8 %reduce-scatter.4.cloned.1.call-start = ((), (), s32[]{:S(2)}) async-start(), calls=%async_computation.5 | async-start | bytes 10813440 | tf_op jit(solution)/shard_map/reduce_scatter | solution.py:115
  486.7 0.7 copy-start.7
  486.7 0.9 copy-start.5
  486.7 1.7 copy-start.4
  486.7 486.0 %reduce-scatter.8.cloned.1.call-start = ((), (), s32[]{:S(2)}) async-start(), calls=%async_computation.8 | async-start | bytes 2949120 | tf_op jit(solution)/shard_map/reduce_scatter | solution.py:179
  489.6 5.9 copy-start.2
  500.5 1.1 copy-start.1
Sparse Core Ops, SparseCore 0:
  10.7 85.6 all-gather.2
  325.6 145.2 all-reduce.1
  474.7 213.2 reduce-scatter.5
  692.0 235.4 reduce-scatter.3
Sparse Core Ops, SparseCore 1:
  327.8 56.7 all-gather.4
  935.3 37.4 reduce-scatter.7

commit v2 on v0

--- a/solution.py
+++ b/solution.py
@@ -1,6 +1,10 @@
+import functools
+
 import jax
 import jax.numpy as jnp
 from jax import lax
+from jax.experimental import pallas as pl
+from jax.experimental.pallas import tpu as pltpu
 from jax.sharding import PartitionSpec as P
 
 THETA = 1000000.0
@@ -61,6 +65,102 @@
     slot_ids = jnp.sum(jnp.where(picks, (pages % pages_dev)[..., None, :], 0), axis=-1)
     page_index = jnp.sum(jnp.where(picks, jnp.arange(pages.shape[-1], dtype=jnp.int32), 0), axis=-1)
     return (slot_ids, page_index)
+
+
+def frequencies(head_dim):
+    halfway = head_dim // 2
+    return THETA ** (-(jnp.arange(halfway, dtype=jnp.float32) * 2.0) / head_dim)
+
+
+SET_BLOCK = 8
+
+
+def cached_kernel(scale, q_ref, kv_ref, valid_ref, table_ref, peak_ref, sum_ref, num_ref, m_acc, w_acc, n_acc):
+    block = pl.program_id(1)
+    n_blocks = pl.num_programs(1)
+    n_pages = kv_ref.shape[2]
+    page_rows = kv_ref.shape[4]
+    head_dim = kv_ref.shape[5]
+    n_slots = table_ref.shape[1] // 2
+    slot_rows = (n_pages // n_slots) * page_rows
+
+    @pl.when(block == 0)
+    def _():
+        m_acc[...] = jnp.full(m_acc.shape, NEGATIVE, jnp.float32)
+        w_acc[...] = jnp.zeros(w_acc.shape, jnp.float32)
+        n_acc[...] = jnp.zeros(n_acc.shape, jnp.float32)
+
+    query = q_ref[0]
+    table = table_ref[0]
+    cosine = jnp.concatenate(
+        [jnp.broadcast_to(table[2 * c : 2 * c + 1], (slot_rows, head_dim)) for c in range(n_slots)], axis=0
+    )
+    sine = jnp.concatenate(
+        [jnp.broadcast_to(table[2 * c + 1 : 2 * c + 2], (slot_rows, head_dim)) for c in range(n_slots)], axis=0
+    )
+
+    def one_set(i, carry):
+        keys = kv_ref[i, 0, :, 0].reshape(n_pages * page_rows, head_dim).astype(jnp.float32)
+        values = kv_ref[i, 0, :, 1].reshape(n_pages * page_rows, head_dim)
+        keys = (keys * cosine + pltpu.roll(keys, head_dim // 2, 1) * sine).astype(jnp.bfloat16)
+        scores = lax.dot_general(
+            query, keys, (((1,), (1,)), ((), ())), preferred_element_type=jnp.float32
+        ) * scale
+        valid = valid_ref[0, pl.ds(i, 1), :] > 0.5
+        masked = jnp.where(valid, scores, NEGATIVE)
+        peak = jnp.max(masked, axis=1, keepdims=True)
+        powers = jnp.where(valid, jnp.exp(masked - peak), 0.0)
+        total = jnp.sum(powers, axis=1, keepdims=True)
+        acc = jnp.dot(powers.astype(jnp.bfloat16), values, preferred_element_type=jnp.float32)
+        normalised = (acc / jnp.maximum(total, 1.0)).astype(jnp.bfloat16).astype(jnp.float32)
+        old = m_acc[...]
+        merged = jnp.maximum(old, peak)
+        rescale = jnp.exp(old - merged)
+        weight = total * jnp.exp(peak - merged)
+        m_acc[...] = merged
+        w_acc[...] = w_acc[...] * rescale + weight
+        n_acc[...] = n_acc[...] * rescale + normalised * weight
+        return carry
+
+    lax.fori_loop(0, kv_ref.shape[0], one_set, 0)
+
+    @pl.when(block == n_blocks - 1)
+    def _():
+        peak_ref[0] = m_acc[...]
+        sum_ref[0] = w_acc[...]
+        num_ref[0] = n_acc[...]
+
+
+def cached_attention(queries, arrived, valid, tables, scale):
+    req_dev, rows, head_dim = queries.shape
+    pool_count = arrived.shape[0]
+    kv_block = (SET_BLOCK,) + (1,) + arrived.shape[2:]
+    return pl.pallas_call(
+        functools.partial(cached_kernel, scale),
+        grid=(req_dev, pool_count // SET_BLOCK),
+        in_specs=[
+            pl.BlockSpec((1, rows, head_dim), lambda r, j: (r, 0, 0)),
+            pl.BlockSpec(kv_block, lambda r, j: (j, r, 0, 0, 0, 0)),
+            pl.BlockSpec((1, SET_BLOCK, valid.shape[2]), lambda r, j: (r, j, 0)),
+            pl.BlockSpec((1,) + tables.shape[1:], lambda r, j: (r, 0, 0)),
+        ],
+        out_specs=[
+            pl.BlockSpec((1, rows, 1), lambda r, j: (r, 0, 0)),
+            pl.BlockSpec((1, rows, 1), lambda r, j: (r, 0, 0)),
+            pl.BlockSpec((1, rows, head_dim), lambda r, j: (r, 0, 0)),
+        ],
+        out_shape=[
+            jax.ShapeDtypeStruct((req_dev, rows, 1), jnp.float32),
+            jax.ShapeDtypeStruct((req_dev, rows, 1), jnp.float32),
+            jax.ShapeDtypeStruct((req_dev, rows, head_dim), jnp.float32),
+        ],
+        scratch_shapes=[
+            pltpu.VMEM((rows, 1), jnp.float32),
+            pltpu.VMEM((rows, 1), jnp.float32),
+            pltpu.VMEM((rows, head_dim), jnp.float32),
+        ],
+        compiler_params=pltpu.CompilerParams(dimension_semantics=("parallel", "arbitrary")),
+    )(queries, arrived, valid, tables)
 
 
 def shards(
@@ -149,27 +249,27 @@
     )
     row_ids = page_index[..., None] * page_rows + jnp.arange(page_rows, dtype=jnp.int32)
     replaced = jnp.any(row_ids[..., None] == own_rows[:, :, None, None, None, :], axis=-1)
-    key_rows = rotate(
-        arrived[:, :, :, :, :, 0].astype(jnp.float32), own_offsets[None, :, :, None, None, None]
-    ).astype(jnp.bfloat16)
-    cached_scores = (
-        jnp.einsum("rqkgd,srcpktd->rqkgscpt", grouped, key_rows, preferred_element_type=jnp.float32)
-        * score_scale
-    )
-    flat_scores = cached_scores.reshape(req_dev, qlen, kv_heads, group_size, pool_count, -1)
-    flat_valid = (
-        jnp.logical_not(replaced).transpose(0, 2, 1, 3, 4).reshape(req_dev, 1, 1, 1, pool_count, -1)
-    )
-    part_peak, part_sum, part_weights = summarize(flat_scores, flat_valid)
-    part_weights = part_weights.reshape(cached_scores.shape)
-    part_acc = jnp.einsum(
-        "rqkgscpt,srcpktd->rqkgsd",
-        part_weights,
-        arrived[:, :, :, :, :, 1],
-        preferred_element_type=jnp.float32,
-    )
-    part_norm = (part_acc / jnp.maximum(part_sum, 1.0)[..., None]).astype(jnp.bfloat16)
-    cached = merge_normalised(part_peak, part_sum, part_norm, 4)
+    valid = jnp.logical_not(replaced).transpose(0, 2, 1, 3, 4).reshape(req_dev, pool_count, -1)
+    angles = own_offsets[..., None] * frequencies(head_dim)
+    tables = jnp.stack(
+        [
+            jnp.concatenate([jnp.cos(angles), jnp.cos(angles)], axis=-1),
+            jnp.concatenate([-jnp.sin(angles), jnp.sin(angles)], axis=-1),
+        ],
+        axis=2,
+    ).reshape(req_dev, 2 * n_slots, head_dim)
+    cached = cached_attention(
+        queries.reshape(req_dev, qlen * heads, head_dim),
+        arrived.reshape(pool_count, req_dev, n_slots * peer_pages, 2, page_rows, head_dim),
+        valid.astype(jnp.float32),
+        tables,
+        score_scale,
+    )
+    cached = (
+        cached[0].reshape(req_dev, qlen, kv_heads, group_size),
+        cached[1].reshape(req_dev, qlen, kv_heads, group_size),
+        cached[2].reshape(req_dev, qlen, kv_heads, group_size, head_dim),
+    )
     total = combine(
         combine(cached, (fresh_peak, fresh_sum, fresh_acc)), (own_peak, own_sum, own_acc)
     )

time: 392 us -> 353 us (0.901)
  Pallas kernels: 0 us -> 68.7 us
  matrix products: 60.9 us -> 11.3 us
  other arithmetic: 73.6 us -> 44.2 us
  waiting for transfers between devices: 189 us -> 174 us
  local copies, waits for them, and re-layouts: 36.6 us -> 26.6 us
    pallas_call x0 -> x1, Pallas kernels: none -> 68.7 us  [cached_attention(): pl.pallas_call(functools.partial(cached_kernel, scale), grid=(req_dev, po...]
    dot_general x2 -> x0, matrix products: 48.9 us -> none  [the longest x1 28.3 us: shards(): jnp.einsum('rqkgscpt,srcpktd->rqkgsd', part_weights, arrived[:, :, :, :,...]
    reduce_sum x3 -> x2, other arithmetic: 29.4 us -> 1.78 us  [summarize(): return (peak, jnp.sum(powers, axis=-1), powers.astype(jnp.bfloat16))]
    reshape x1 -> x4, local copies, waits for them, and re-layouts: 9.93 us -> 0.45 us  [the longest x2 0.23 us: shards(): cached[1].reshape(req_dev, qlen, kv_heads, group_size)]
    all_to_all x1, waiting for transfers between devices: 143 us -> 135 us  [shards(): lax.all_to_all(outgoing, 'pool', split_axis=0, concat_axis=0, tiled=True)]
    reduce_scatter x1, waiting for transfers between devices: 45 us -> 37.8 us  [shards(): lax.psum_scatter(partial_out, 'tp', scatter_dimension=2, tiled=True)]
    slice x1 -> x0, local copies, waits for them, and re-layouts: 6.27 us -> none  [shards(): arrived[:, :, :, :, :, 1]]
  transfers between devices with their start and end apart: 3 -> 3, of which waited for: 2 -> 2; matrix products, arithmetic and copies ran while one was open for 18% -> 19% of each run, Pallas kernels for 0% -> 0%
where the time goes in v2:
time: 353 us; the launch traced here: 351 us
  waiting for transfers between devices  174 us (49%)
  Pallas kernels  68.7 us (19%)
  other arithmetic  44.2 us (13%)
  local copies, waits for them, and re-layouts  26.6 us (8%)
  between operations  13.8 us (4%)
  starting transfers between devices  12.3 us (3%)
  matrix products  11.3 us (3%)
    all_to_all x1, waiting for transfers between devices, shards(): lax.all_to_all(outgoing, 'pool', split_axis=0, concat_axis=0, tiled=True)  135 us
    pallas_call x1, Pallas kernels, cached_attention(): pl.pallas_call(functools.partial(cached_kernel, scale), grid=(req_dev, po...  68.7 us
    reduce_scatter x1, waiting for transfers between devices, shards(): lax.psum_scatter(partial_out, 'tp', scatter_dimension=2, tiled=True)  37.8 us
    reduce_or x1, other arithmetic, shards(): jnp.any(row_ids[..., None] == own_rows[:, :, None, None, None, :], axis=-1)  20.4 us
    all_to_all x1, starting transfers between devices, shards(): lax.all_to_all(outgoing, 'pool', split_axis=0, concat_axis=0, tiled=True)  12.3 us
    gather x1, local copies, waits for them, and re-layouts, shards(): outgoing = pool_kv[slot_ids]  11.5 us
  transfers between devices with their start and end apart: 3, of which 2 were waited for; matrix products, arithmetic and copies ran while one was open for 19% of the time, Pallas kernels for 0%

profile of v2, /device:TPU:1, one launch (start us, length us, event | category | flops | bytes accessed | tf_op | source)
XLA Modules:
  0.0 350.9 jit_solution(18104712425886601498)
XLA Ops:
  8.2 1.5 gather_fusion
  9.8 1.2 reduce_window_sum.22
  11.8 11.5 %gather_fusion.1 = bf16[1024,2,16,128]{3,2,1,0:T(8,128)(2,1)} fusion(bf16[256,2,16,128]{3,2,1,0:T(8,128)(2,1)} %bitcast.146, s32[1024]{0:T(1024)S(1)} %broadcast_clamp_fusion), kind=kCustom, calls=%fused_computation.1 | custom fusion | bytes 16781312 | tf_op jit(solution)/shard_map/gather | solution.py:243
  23.2 12.3 %all-to-all-start = ((bf16[32,2,4,4,1,2,16,128]{7,6,5,3,2,1,4,0:T(8,128)(2,1)}), bf16[32,2,4,4,1,2,16,128]{7,6,5,3,2,1,4,0:T(8,128)(2,1)}, u32[]{:S(2)}, u32[]{:S(2)}) async-start(bf16[32,2,4,4,1,2,16,128]{7,6,5,3,2,1,4,0:T(8,128)(2,1)} %bitcast.145), calls=%async_computation | async-start | bytes 16777216 | tf_op jit(solution)/shard_map/all_to_all | solution.py:245
  36.7 2.3 reduce_window_sum.23
  42.4 20.4 %compare_reduce_fusion = pred[2,4,32,4,16]{4,3,2,1,0:T(4,128)(4,1)S(1)} fusion(s32[2,4,104]{2,1,0:T(4,128)S(1)} %get-tuple-element.17, s32[2,4,32,4,16]{4,3,2,1,0:T(4,128)S(1)} %iota_add_fusion), kind=kLoop, calls=%fused_computation.10 | loop fusion | flops 3391488 | bytes 85248 | tf_op jit(solution)/shard_map/reduce_or | solution.py:251
  63.8 1.2 copy.107
  66.7 1.7 pad_maximum_fusion.q_ref
  69.2 5.3 %fusion = f32[2,4,104]{2,1,0:T(4,128)S(1)} fusion(bf16[2,4,104,5120]{3,2,1,0:T(8,128)(2,1)} %all-gather.2.cloned.1.call-done), kind=kLoop, calls=%fused_computation.5 | loop fusion | flops 12778688 | bytes 8523008 | tf_op jit(solution)/shard_map/reduce_sum | solution.py:212
  75.1 2.6 fusion.10
  78.4 1.8 fusion.43
  80.8 1.1 copy-done.2
  81.9 1.9 copy.117
  83.8 2.8 reshape.557
  86.6 1.7 exponential_reduce_fusion
  88.3 135.5 %all-to-all-done = bf16[32,2,4,4,1,2,16,128]{7,6,5,3,2,1,4,0:T(8,128)(2,1)} async-done(((bf16[32,2,4,4,1,2,16,128]{7,6,5,3,2,1,4,0:T(8,128)(2,1)}), bf16[32,2,4,4,1,2,16,128]{7,6,5,3,2,1,4,0:T(8,128)(2,1)}, u32[]{:S(2)}, u32[]{:S(2)}) %all-to-all-start) | async-done | bytes 8388640 | tf_op jit(solution)/shard_map/all_to_all | solution.py:245
  223.7 68.7 %shard_map.109 = (f32[2,320,1]{2,1,0:T(8,128)}, f32[2,320,1]{2,1,0:T(8,128)}, f32[2,320,128]{2,1,0:T(8,128)}) custom-call(bf16[2,320,128]{2,1,0:T(8,128)(2,1)} %pad_maximum_fusion.q_ref, bf16[32,2,16,2,16,128]{5,4,3,2,1,0:T(8,128)(2,1)} %bitcast.6.kv_ref, f32[2,32,256]{2,1,0:T(8,128)} %copy.110.valid_ref, f32[2,8,128]{2,1,0:T(8,128)} %bitcast.154), custom_call_target="tpu_custom_call" | custom-call | tf_op jit(solution)/shard_map/pallas_call | solution.py:138
  292.4 1.2 copy.111
  293.6 1.1 reduce.6
  294.8 1.2 reduce.7
  296.7 2.0 fusion.25
  299.0 5.6 %fusion.6 = f32[2,64,5120]{2,1,0:T(8,128)} fusion(bf16[2,64,640]{2,1,0:T(8,128)(2,1)S(1)} %reshape.561, bf16[640,5120]{1,0:T(8,128)(2,1)} %param.21), kind=kOutput, calls=%fused_computation.11 | convolution fusion | flops 838860800 | bytes 9338880 | tf_op jit(solution)/shard_map/rqh,hm->rqm/dot_general | solution.py:283
  304.6 37.8 %reduce-scatter.2.cloned.1.call-done = f32[2,64,640]{2,1,0:T(8,128)} async-done(((f32[2,64,5120]{2,1,0:T(8,128)}), f32[2,64,640]{2,1,0:T(8,128)}) %reduce-scatter.2.cloned.1.call-update) | async-done | bytes 327696 | tf_op jit(solution)/shard_map/reduce_scatter | solution.py:284
  342.4 1.7 convert_element_type.124
  (83 shorter events, 13.2 us)
Async XLA Ops:
  6.5 68.0 %copy-start = (bf16[5120,2,1,128]{3,1,2,0:T(2,128)(2,1)S(1)}, bf16[5120,2,1,128]{3,1,2,0:T(2,128)(2,1)}, u32[]{:S(2)}) copy-start(bf16[5120,2,1,128]{3,1,2,0:T(2,128)(2,1)} %param.20) | copy-start | bytes 7864324
  6.5 62.7 %all-gather.2.cloned.1.call-start = ((), (), s32[]{:S(2)}) async-start(), calls=%async_computation.2 | async-start | bytes 9584640 | tf_op jit(solution)/shard_map/all_gather | solution.py:209
  23.2 12.4 %copy-start.8 = (s32[64]{0:T(128)S(1)}, s32[64]{0:T(128)}, u32[]{:S(2)}) copy-start(s32[64]{0:T(128)} %param.16) | copy-start | bytes 772
  23.2 12.5 %copy-start.6 = (s32[64,4]{0,1:T(4,128)S(1)}, s32[64,4]{0,1:T(4,128)}, u32[]{:S(2)}) copy-start(s32[64,4]{0,1:T(4,128)} %param.13) | copy-start | bytes 3076
  23.2 12.5 %copy-start.7 = (s32[64,4]{0,1:T(4,128)S(1)}, s32[64,4]{0,1:T(4,128)}, u32[]{:S(2)}) copy-start(s32[64,4]{0,1:T(4,128)} %param.14) | copy-start | bytes 3076
  23.2 12.8 %copy-start.1 = (s32[64,128]{1,0:T(8,128)S(1)}, s32[64,128]{1,0:T(8,128)}, u32[]{:S(2)}) copy-start(s32[64,128]{1,0:T(8,128)} %param.12) | copy-start | bytes 98308
  23.2 16.6 %copy-start.5 = (bf16[2,64,5,128]{3,1,2,0:T(8,128)(2,1)S(1)}, bf16[2,64,5,128]{3,1,2,0:T(8,128)(2,1)}, u32[]{:S(2)}) copy-start(bf16[2,64,5,128]{3,1,2,0:T(8,128)(2,1)} %param.17) | copy-start | bytes 491524
  23.2 200.5 %all-to-all-start = ((bf16[32,2,4,4,1,2,16,128]{7,6,5,3,2,1,4,0:T(8,128)(2,1)}), bf16[32,2,4,4,1,2,16,128]{7,6,5,3,2,1,4,0:T(8,128)(2,1)}, u32[]{:S(2)}, u32[]{:S(2)}) async-start(bf16[32,2,4,4,1,2,16,128]{7,6,5,3,2,1,4,0:T(8,128)(2,1)} %bitcast.145), calls=%async_computation | async-start | bytes 16777216 | tf_op jit(solution)/shard_map/all_to_all | solution.py:245
  35.6 306.8 %reduce-scatter.2.cloned.1.call-start = ((), (), s32[]{:S(2)}) async-start(), calls=%async_computation.3 | async-start | bytes 2949120 | tf_op jit(solution)/shard_map/reduce_scatter | solution.py:284
  40.2 28.3 %copy-start.4 = (bf16[2,64,2,1,128]{4,2,3,1,0:T(2,128)(2,1)S(1)}, bf16[2,64,2,1,128]{4,2,3,1,0:T(2,128)(2,1)}, u32[]{:S(2)}) copy-start(bf16[2,64,2,1,128]{4,2,3,1,0:T(2,128)(2,1)} %param.18) | copy-start | bytes 196612
  69.2 5.8 %copy-start.3 = (bf16[2,4,104,5120]{3,2,1,0:T(8,128)(2,1)S(1)}, bf16[2,4,104,5120]{3,2,1,0:T(8,128)(2,1)}, u32[]{:S(2)}) copy-start(bf16[2,4,104,5120]{3,2,1,0:T(8,128)(2,1)} %all-gather.2.cloned.1.call-done) | copy-start | bytes 25559044
  80.8 1.1 copy-start.2
Sparse Core Ops, SparseCore 0:
  9.2 56.8 all-gather.1
  304.7 37.5 reduce-scatter.1

commit v3 on v2

--- a/solution.py
+++ b/solution.py
@@ -240,9 +240,13 @@
     )
     all_pages = span_pages[req_spans]
     slot_ids, unused_index = local_pages(all_pages, device, pages_dev, peer_pages)
-    outgoing = pool_kv[slot_ids]
-    outgoing = outgoing.reshape((pool_count, req_dev) + outgoing.shape[1:])
-    arrived = lax.all_to_all(outgoing, "pool", split_axis=0, concat_axis=0, tiled=True)
+    slot_ids = slot_ids.reshape((pool_count, req_dev) + slot_ids.shape[1:])
+    arrivals = []
+    for r in range(req_dev):
+        outgoing = pool_kv[slot_ids[:, r]]
+        if arrivals:
+            arrivals[-1], outgoing = lax.optimization_barrier((arrivals[-1], outgoing))
+        arrivals.append(lax.all_to_all(outgoing, "pool", split_axis=0, concat_axis=0, tiled=True))
     mine = span_pages[own_spans]
     unused_slots, page_index = local_pages(
         mine[:, :, None, :], jnp.arange(pool_count, dtype=jnp.int32)[:, None], pages_dev, peer_pages
@@ -258,13 +262,18 @@
         ],
         axis=2,
     ).reshape(req_dev, 2 * n_slots, head_dim)
-    cached = cached_attention(
-        queries.reshape(req_dev, qlen * heads, head_dim),
-        arrived.reshape(pool_count, req_dev, n_slots * peer_pages, 2, page_rows, head_dim),
-        valid.astype(jnp.float32),
-        tables,
-        score_scale,
-    )
+    flat_queries = queries.reshape(req_dev, qlen * heads, head_dim)
+    parts = [
+        cached_attention(
+            flat_queries[r : r + 1],
+            arrivals[r].reshape(pool_count, 1, n_slots * peer_pages, 2, page_rows, head_dim),
+            valid[r : r + 1].astype(jnp.float32),
+            tables[r : r + 1],
+            score_scale,
+        )
+        for r in range(req_dev)
+    ]
+    cached = [jnp.concatenate([part[i] for part in parts], axis=0) for i in range(3)]
     cached = (
         cached[0].reshape(req_dev, qlen, kv_heads, group_size),
         cached[1].reshape(req_dev, qlen, kv_heads, group_size),

time: 353 us -> 318 us (0.901)
  waiting for transfers between devices: 174 us -> 130 us
  starting transfers between devices: 12.3 us -> 22 us
    all_to_all x1 -> x2, waiting for transfers between devices: 135 us -> 92.4 us  [shards(): lax.all_to_all(outgoing, 'pool', split_axis=0, concat_axis=0, tiled=True)]
    all_to_all x1 -> x2, starting transfers between devices: 12.3 us -> 21.7 us  [shards(): lax.all_to_all(outgoing, 'pool', split_axis=0, concat_axis=0, tiled=True)]
    gather x1 -> x2, local copies, waits for them, and re-layouts: 11.5 us -> 9.5 us  [shards(): outgoing = pool_kv[slot_ids[:, r]]]
    pallas_call x1 -> x2, Pallas kernels: 68.7 us -> 70.4 us  [cached_attention(): pl.pallas_call(functools.partial(cached_kernel, scale), grid=(req_dev, po...]
  transfers between devices with their start and end apart: 3 -> 4, of which waited for: 2 -> 3; matrix products, arithmetic and copies ran while one was open for 19% -> 21% of each run, Pallas kernels for 0% -> 11%
where the time goes in v3:
time: 318 us; the launch traced here: 316 us
  waiting for transfers between devices  130 us (41%)
  Pallas kernels  70.4 us (22%)
  other arithmetic  40.7 us (13%)
  local copies, waits for them, and re-layouts  28.1 us (9%)
  starting transfers between devices  22 us (7%)
  between operations  13.9 us (4%)
  matrix products  11.3 us (4%)
    all_to_all x2, waiting for transfers between devices, shards(): lax.all_to_all(outgoing, 'pool', split_axis=0, concat_axis=0, tiled=True)  92.4 us
    pallas_call x2, Pallas kernels, cached_attention(): pl.pallas_call(functools.partial(cached_kernel, scale), grid=(req_dev, po...  70.4 us
    reduce_scatter x1, waiting for transfers between devices, shards(): lax.psum_scatter(partial_out, 'tp', scatter_dimension=2, tiled=True)  36.5 us
    all_to_all x2, starting transfers between devices, shards(): lax.all_to_all(outgoing, 'pool', split_axis=0, concat_axis=0, tiled=True)  21.7 us
    reduce_or x1, other arithmetic, shards(): jnp.any(row_ids[..., None] == own_rows[:, :, None, None, None, :], axis=-1)  20.4 us
    gather x2, local copies, waits for them, and re-layouts, shards(): outgoing = pool_kv[slot_ids[:, r]]  9.5 us
  transfers between devices with their start and end apart: 4, of which 3 were waited for; matrix products, arithmetic and copies ran while one was open for 21% of the time, Pallas kernels for 11%

profile of v3, /device:TPU:1, one launch (start us, length us, event | category | flops | bytes accessed | tf_op | source)
XLA Modules:
  0.0 315.8 jit_solution(3161713307723802749)
XLA Ops:
  8.2 1.5 gather_fusion
  9.8 1.2 reduce_window_sum.22
  11.9 4.8 %gather_fusion.1 = bf16[512,2,16,128]{3,2,1,0:T(8,128)(2,1)} fusion(bf16[256,2,16,128]{3,2,1,0:T(8,128)(2,1)} %bitcast.156, s32[1024]{0:T(1024)S(1)} %pad_clamp_fusion.2), kind=kCustom, calls=%fused_computation.1 | custom fusion | bytes 8390656 | tf_op jit(solution)/shard_map/gather | solution.py:246
  16.7 12.2 %all-to-all-start = ((bf16[32,4,4,1,2,16,128]{6,5,4,2,1,3,0:T(8,128)(2,1)}), bf16[32,4,4,1,2,16,128]{6,5,4,2,1,3,0:T(8,128)(2,1)}, u32[]{:S(2)}, u32[]{:S(2)}) async-start(bf16[32,4,4,1,2,16,128]{6,5,4,2,1,3,0:T(8,128)(2,1)} %bitcast.159), calls=%async_computation | async-start | bytes 8388608 | tf_op jit(solution)/shard_map/all_to_all | solution.py:249
  29.0 4.7 %gather_fusion.2 = bf16[512,2,16,128]{3,2,1,0:T(8,128)(2,1)} fusion(bf16[256,2,16,128]{3,2,1,0:T(8,128)(2,1)} %bitcast.157, s32[1024]{0:T(1024)S(1)} %pad_clamp_fusion.1), kind=kCustom, calls=%fused_computation.2 | custom fusion | bytes 8390656 | tf_op jit(solution)/shard_map/gather | solution.py:246
  33.7 87.6 %all-to-all-done = bf16[32,4,4,1,2,16,128]{6,5,4,2,1,3,0:T(8,128)(2,1)} async-done(((bf16[32,4,4,1,2,16,128]{6,5,4,2,1,3,0:T(8,128)(2,1)}), bf16[32,4,4,1,2,16,128]{6,5,4,2,1,3,0:T(8,128)(2,1)}, u32[]{:S(2)}, u32[]{:S(2)}) %all-to-all-start) | async-done | bytes 4194336 | tf_op jit(solution)/shard_map/all_to_all | solution.py:249
  121.4 9.6 %all-to-all-start.1 = ((bf16[32,4,4,1,2,16,128]{6,5,4,2,1,3,0:T(8,128)(2,1)}), bf16[32,4,4,1,2,16,128]{6,5,4,2,1,3,0:T(8,128)(2,1)}, u32[]{:S(2)}, u32[]{:S(2)}) async-start(bf16[32,4,4,1,2,16,128]{6,5,4,2,1,3,0:T(8,128)(2,1)} %bitcast.158), calls=%async_computation.1 | async-start | bytes 8388608 | tf_op jit(solution)/shard_map/all_to_all | solution.py:249
  132.1 2.3 reduce_window_sum.23
  136.4 20.4 %compare_reduce_fusion = pred[2,4,32,4,16]{4,3,2,1,0:T(4,128)(4,1)S(1)} fusion(s32[2,4,104]{2,1,0:T(4,128)S(1)} %get-tuple-element.27, s32[2,4,32,4,16]{4,3,2,1,0:T(4,128)S(1)} %iota_add_fusion), kind=kLoop, calls=%fused_computation.11 | loop fusion | flops 3391488 | bytes 85248 | tf_op jit(solution)/shard_map/reduce_or | solution.py:255
  162.4 35.2 %shard_map.109 = (f32[1,320,1]{2,1,0:T(8,128)}, f32[1,320,1]{2,1,0:T(8,128)}, f32[1,320,128]{2,1,0:T(8,128)}) custom-call(bf16[1,320,128]{2,1,0:T(8,128)(2,1)} %slice.72.q_ref, bf16[32,1,16,2,16,128]{5,4,3,2,1,0:T(8,128)(2,1)} %bitcast.7.kv_ref, f32[1,32,256]{2,1,0:T(8,128)} %copy.186.valid_ref, f32[1,8,128]{2,1,0:T(8,128)} %bitcast.170), custom_call_target="tpu_custom_call" | custom-call | tf_op jit(solution)/shard_map/pallas_call | solution.py:138
  198.6 1.0 copy.201
  199.7 5.3 %fusion = f32[2,4,104]{2,1,0:T(4,128)S(1)} fusion(bf16[2,4,104,5120]{3,2,1,0:T(8,128)(2,1)} %all-gather.2.cloned.1.call-done), kind=kLoop, calls=%fused_computation.6 | loop fusion | flops 12778688 | bytes 8523008 | tf_op jit(solution)/shard_map/reduce_sum | solution.py:212
  205.5 2.6 fusion.10
  208.8 2.0 fusion.43
  211.4 1.1 copy-done.2
  212.5 1.9 copy.197
  214.4 2.8 reshape.629
  217.2 1.7 exponential_reduce_fusion
  218.9 4.8 %all-to-all-done.1 = bf16[32,4,4,1,2,16,128]{6,5,4,2,1,3,0:T(8,128)(2,1)} async-done(((bf16[32,4,4,1,2,16,128]{6,5,4,2,1,3,0:T(8,128)(2,1)}), bf16[32,4,4,1,2,16,128]{6,5,4,2,1,3,0:T(8,128)(2,1)}, u32[]{:S(2)}, u32[]{:S(2)}) %all-to-all-start.1) | async-done | bytes 4194336 | tf_op jit(solution)/shard_map/all_to_all | solution.py:249
  223.7 35.2 %shard_map.110 = (f32[1,320,1]{2,1,0:T(8,128)}, f32[1,320,1]{2,1,0:T(8,128)}, f32[1,320,128]{2,1,0:T(8,128)}) custom-call(bf16[1,320,128]{2,1,0:T(8,128)(2,1)} %slice.79.q_ref, bf16[32,1,16,2,16,128]{5,4,3,2,1,0:T(8,128)(2,1)} %bitcast.15.kv_ref, f32[1,32,256]{2,1,0:T(8,128)} %copy.188.valid_ref, f32[1,8,128]{2,1,0:T(8,128)} %bitcast.169), custom_call_target="tpu_custom_call" | custom-call | tf_op jit(solution)/shard_map/pallas_call | solution.py:138
  262.9 2.0 fusion.25
  265.3 5.6 %fusion.6 = f32[2,64,5120]{2,1,0:T(8,128)} fusion(bf16[2,64,640]{2,1,0:T(8,128)(2,1)S(1)} %reshape.633, bf16[640,5120]{1,0:T(8,128)(2,1)} %param.21), kind=kOutput, calls=%fused_computation.12 | convolution fusion | flops 838860800 | bytes 9338880 | tf_op jit(solution)/shard_map/rqh,hm->rqm/dot_general | solution.py:292
  270.8 36.5 %reduce-scatter.2.cloned.1.call-done = f32[2,64,640]{2,1,0:T(8,128)} async-done(((f32[2,64,5120]{2,1,0:T(8,128)}), f32[2,64,640]{2,1,0:T(8,128)}) %reduce-scatter.2.cloned.1.call-update) | async-done | bytes 327696 | tf_op jit(solution)/shard_map/reduce_scatter | solution.py:293
  307.3 1.7 convert_element_type.127
  (102 shorter events, 18.4 us)
Async XLA Ops:
  6.5 198.4 %copy-start = (bf16[5120,2,1,128]{3,1,2,0:T(2,128)(2,1)S(1)}, bf16[5120,2,1,128]{3,1,2,0:T(2,128)(2,1)}, u32[]{:S(2)}) copy-start(bf16[5120,2,1,128]{3,1,2,0:T(2,128)(2,1)} %param.20) | copy-start | bytes 7864324
  6.5 193.1 %all-gather.2.cloned.1.call-start = ((), (), s32[]{:S(2)}) async-start(), calls=%async_computation.3 | async-start | bytes 9584640 | tf_op jit(solution)/shard_map/all_gather | solution.py:209
  16.7 104.7 %all-to-all-start = ((bf16[32,4,4,1,2,16,128]{6,5,4,2,1,3,0:T(8,128)(2,1)}), bf16[32,4,4,1,2,16,128]{6,5,4,2,1,3,0:T(8,128)(2,1)}, u32[]{:S(2)}, u32[]{:S(2)}) async-start(bf16[32,4,4,1,2,16,128]{6,5,4,2,1,3,0:T(8,128)(2,1)} %bitcast.159), calls=%async_computation | async-start | bytes 8388608 | tf_op jit(solution)/shard_map/all_to_all | solution.py:249
  121.4 9.9 %copy-start.7 = (s32[64,4]{0,1:T(4,128)S(1)}, s32[64,4]{0,1:T(4,128)}, u32[]{:S(2)}) copy-start(s32[64,4]{0,1:T(4,128)} %param.13) | copy-start | bytes 3076
  121.4 9.9 %copy-start.8 = (s32[64,4]{0,1:T(4,128)S(1)}, s32[64,4]{0,1:T(4,128)}, u32[]{:S(2)}) copy-start(s32[64,4]{0,1:T(4,128)} %param.14) | copy-start | bytes 3076
  121.4 10.1 %copy-start.1 = (s32[64,128]{1,0:T(8,128)S(1)}, s32[64,128]{1,0:T(8,128)}, u32[]{:S(2)}) copy-start(s32[64,128]{1,0:T(8,128)} %param.12) | copy-start | bytes 98308
  121.4 36.5 %copy-start.6 = (bf16[2,64,5,128]{3,1,2,0:T(8,128)(2,1)S(1)}, bf16[2,64,5,128]{3,1,2,0:T(8,128)(2,1)}, u32[]{:S(2)}) copy-start(bf16[2,64,5,128]{3,1,2,0:T(8,128)(2,1)} %param.17) | copy-start | bytes 491524
  121.4 102.3 %all-to-all-start.1 = ((bf16[32,4,4,1,2,16,128]{6,5,4,2,1,3,0:T(8,128)(2,1)}), bf16[32,4,4,1,2,16,128]{6,5,4,2,1,3,0:T(8,128)(2,1)}, u32[]{:S(2)}, u32[]{:S(2)}) async-start(bf16[32,4,4,1,2,16,128]{6,5,4,2,1,3,0:T(8,128)(2,1)} %bitcast.158), calls=%async_computation.1 | async-start | bytes 8388608 | tf_op jit(solution)/shard_map/all_to_all | solution.py:249
  131.0 29.6 %copy-start.9 = (s32[64]{0:T(128)S(1)}, s32[64]{0:T(128)}, u32[]{:S(2)}) copy-start(s32[64]{0:T(128)} %param.16) | copy-start | bytes 772
  131.0 30.7 %copy-start.4 = (bf16[2,64,2,1,128]{4,2,3,1,0:T(2,128)(2,1)S(1)}, bf16[2,64,2,1,128]{4,2,3,1,0:T(2,128)(2,1)}, u32[]{:S(2)}) copy-start(bf16[2,64,2,1,128]{4,2,3,1,0:T(2,128)(2,1)} %param.18) | copy-start | bytes 196612
  131.0 176.3 %reduce-scatter.2.cloned.1.call-start = ((), (), s32[]{:S(2)}) async-start(), calls=%async_computation.4 | async-start | bytes 2949120 | tf_op jit(solution)/shard_map/reduce_scatter | solution.py:293
  199.6 5.9 %copy-start.3 = (bf16[2,4,104,5120]{3,2,1,0:T(8,128)(2,1)S(1)}, bf16[2,4,104,5120]{3,2,1,0:T(8,128)(2,1)}, u32[]{:S(2)}) copy-start(bf16[2,4,104,5120]{3,2,1,0:T(8,128)(2,1)} %all-gather.2.cloned.1.call-done) | copy-start | bytes 25559044
  211.4 1.1 copy-start.2
  214.4 44.5 %copy-start.5 = (f32[1,320,128]{2,1,0:T(8,128)S(1)}, f32[1,320,128]{2,1,0:T(8,128)}, u32[]{:S(2)}) copy-start(f32[1,320,128]{2,1,0:T(8,128)} %get-tuple-element.14) | copy-start | bytes 491524
Sparse Core Ops, SparseCore 0:
  9.2 56.8 all-gather.1
  271.0 36.3 reduce-scatter.1

commit v4 on v2

--- a/solution.py
+++ b/solution.py
@@ -238,11 +238,43 @@
     own_acc = jnp.einsum(
         "rqkgj,rjkd->rqkgd", own_weights, own_values, preferred_element_type=jnp.float32
     )
-    all_pages = span_pages[req_spans]
-    slot_ids, unused_index = local_pages(all_pages, device, pages_dev, peer_pages)
-    outgoing = pool_kv[slot_ids]
-    outgoing = outgoing.reshape((pool_count, req_dev) + outgoing.shape[1:])
-    arrived = lax.all_to_all(outgoing, "pool", split_axis=0, concat_axis=0, tiled=True)
+    own_keys = rotate(question_kv[:, :, 0].astype(jnp.float32), qpos[None, :, None]).astype(
+        jnp.bfloat16
+    )
+    own_values = question_kv[:, :, 1]
+    hidden = lax.all_gather(recompute_hidden, "tp", axis=3, tiled=True)
+    widened = hidden.astype(jnp.float32)
+    normed = (
+        widened * lax.rsqrt(jnp.mean(widened * widened, axis=-1, keepdims=True) + 1e-06)
+    ).astype(jnp.bfloat16)
+    fresh = jnp.einsum("rcnd,dskh->rcnskh", normed, w_kv, preferred_element_type=jnp.float32)
+    fresh_pos = own_offsets[:, :, None] + own_rows.astype(jnp.float32)
+    fresh_keys = rotate(fresh[:, :, :, 0], fresh_pos[..., None]).astype(jnp.bfloat16)
+    fresh_values = fresh[:, :, :, 1].astype(jnp.bfloat16)
+    fresh_scores = (
+        jnp.einsum("rqkgd,rcnkd->rqkgcn", grouped, fresh_keys, preferred_element_type=jnp.float32)
+        * score_scale
+    )
+    fresh_scores = fresh_scores.reshape(req_dev, qlen, kv_heads, group_size, -1)
+    fresh_peak, fresh_sum, fresh_weights = summarize(fresh_scores, True)
+    fresh_acc = jnp.einsum(
+        "rqkgn,rnkd->rqkgd",
+        fresh_weights,
+        fresh_values.reshape(req_dev, -1, kv_heads, head_dim),
+        preferred_element_type=jnp.float32,
+    )
+    visible = (steps_q[None, None, :] <= steps_q[None, :, None]) & (
+        steps_q[None, None, :] < own_lengths[:, None, None]
+    )
+    own_scores = (
+        jnp.einsum("rqkgd,rjkd->rqkgj", grouped, own_keys, preferred_element_type=jnp.float32)
+        * score_scale
+    )
+    own_peak, own_sum, own_weights = summarize(own_scores, visible[:, :, None, None, :])
+    own_acc = jnp.einsum(
+        "rqkgj,rjkd->rqkgd", own_weights, own_values, preferred_element_type=jnp.float32
+    )
+
     mine = span_pages[own_spans]
     unused_slots, page_index = local_pages(
         mine[:, :, None, :], jnp.arange(pool_count, dtype=jnp.int32)[:, None], pages_dev, peer_pages
@@ -250,6 +282,7 @@
     row_ids = page_index[..., None] * page_rows + jnp.arange(page_rows, dtype=jnp.int32)
     replaced = jnp.any(row_ids[..., None] == own_rows[:, :, None, None, None, :], axis=-1)
     valid = jnp.logical_not(replaced).transpose(0, 2, 1, 3, 4).reshape(req_dev, pool_count, -1)
+    valid = valid.astype(jnp.float32)
     angles = own_offsets[..., None] * frequencies(head_dim)
     tables = jnp.stack(
         [
@@ -258,30 +291,54 @@
         ],
         axis=2,
     ).reshape(req_dev, 2 * n_slots, head_dim)
-    cached = cached_attention(
-        queries.reshape(req_dev, qlen * heads, head_dim),
-        arrived.reshape(pool_count, req_dev, n_slots * peer_pages, 2, page_rows, head_dim),
-        valid.astype(jnp.float32),
-        tables,
-        score_scale,
-    )
-    cached = (
-        cached[0].reshape(req_dev, qlen, kv_heads, group_size),
-        cached[1].reshape(req_dev, qlen, kv_heads, group_size),
-        cached[2].reshape(req_dev, qlen, kv_heads, group_size, head_dim),
-    )
-    total = combine(
-        combine(cached, (fresh_peak, fresh_sum, fresh_acc)), (own_peak, own_sum, own_acc)
-    )
-    attn = total[2] / total[1][..., None]
-    live = steps_q[None, :] < own_lengths[:, None]
-    attn = (
-        jnp.where(live[:, :, None, None, None], attn, 0.0)
-        .astype(jnp.bfloat16)
-        .reshape(req_dev, qlen, heads * head_dim)
-    )
-    partial_out = jnp.einsum("rqh,hm->rqm", attn, w_out, preferred_element_type=jnp.float32)
-    return lax.psum_scatter(partial_out, "tp", scatter_dimension=2, tiled=True).astype(jnp.bfloat16)
+    local = (fresh_peak, fresh_sum, fresh_acc, own_peak, own_sum, own_acc, valid, tables)
+
+    all_pages = span_pages[req_spans]
+    slot_ids, unused_index = local_pages(all_pages, device, pages_dev, peer_pages)
+    slot_ids = slot_ids.reshape((pool_count, req_dev) + slot_ids.shape[1:])
+    arrivals = []
+    for r in range(req_dev):
+        outgoing = pool_kv[slot_ids[:, r]]
+        if arrivals:
+            arrivals[-1], outgoing, local = lax.optimization_barrier((arrivals[-1], outgoing, local))
+        arrivals.append(lax.all_to_all(outgoing, "pool", split_axis=0, concat_axis=0, tiled=True))
+    fresh_peak, fresh_sum, fresh_acc, own_peak, own_sum, own_acc, valid, tables = local
+
+    flat_queries = queries.reshape(req_dev, qlen * heads, head_dim)
+    outputs = []
+    for r in range(req_dev):
+        one = slice(r, r + 1)
+        arrived = arrivals[r]
+        if outputs:
+            arrived, outputs[-1] = lax.optimization_barrier((arrived, outputs[-1]))
+        cached = cached_attention(
+            flat_queries[one],
+            arrived.reshape(pool_count, 1, n_slots * peer_pages, 2, page_rows, head_dim),
+            valid[one],
+            tables[one],
+            score_scale,
+        )
+        cached = (
+            cached[0].reshape(1, qlen, kv_heads, group_size),
+            cached[1].reshape(1, qlen, kv_heads, group_size),
+            cached[2].reshape(1, qlen, kv_heads, group_size, head_dim),
+        )
+        total = combine(
+            combine(cached, (fresh_peak[one], fresh_sum[one], fresh_acc[one])),
+            (own_peak[one], own_sum[one], own_acc[one]),
+        )
+        attn = total[2] / total[1][..., None]
+        live = steps_q < own_lengths[r]
+        attn = (
+            jnp.where(live[None, :, None, None, None], attn, 0.0)
+            .astype(jnp.bfloat16)
+            .reshape(1, qlen, heads * head_dim)
+        )
+        partial_out = jnp.einsum("rqh,hm->rqm", attn, w_out, preferred_element_type=jnp.float32)
+        outputs.append(
+            lax.psum_scatter(partial_out, "tp", scatter_dimension=2, tiled=True).astype(jnp.bfloat16)
+        )
+    return jnp.concatenate(outputs, axis=0)
 
 
 def solution(mesh):

time: 353 us -> 314 us (0.89)
  waiting for transfers between devices: 174 us -> 113 us
  starting transfers between devices: 12.3 us -> 21.9 us
  other arithmetic: 44.2 us -> 50.1 us
  matrix products: 11.3 us -> 16.6 us
    all_to_all x1 -> x2, waiting for transfers between devices: 135 us -> 42.1 us  [shards(): lax.all_to_all(outgoing, 'pool', split_axis=0, concat_axis=0, tiled=True)]
    reduce_scatter x1 -> x2, waiting for transfers between devices: 37.8 us -> 68.6 us  [shards(): lax.psum_scatter(partial_out, 'tp', scatter_dimension=2, tiled=True)]
    all_to_all x1 -> x2, starting transfers between devices: 12.3 us -> 21.8 us  [shards(): lax.all_to_all(outgoing, 'pool', split_axis=0, concat_axis=0, tiled=True)]
    dot_general x1 -> x2, matrix products: 5.56 us -> 10.4 us  [shards(): jnp.einsum('rqh,hm->rqm', attn, w_out, preferred_element_type=jnp.float32)]
    slice x0 -> x8, local copies, waits for them, and re-layouts: none -> 4.12 us  [the longest x4 1.47 us: shards(): flat_queries[one]]
    gather x1 -> x2, local copies, waits for them, and re-layouts: 11.5 us -> 9.54 us  [shards(): outgoing = pool_kv[slot_ids[:, r]]]
    pallas_call x1 -> x2, Pallas kernels: 68.7 us -> 70.4 us  [cached_attention(): pl.pallas_call(functools.partial(cached_kernel, scale), grid=(req_dev, po...]
  transfers between devices with their start and end apart: 3 -> 5, of which waited for: 2 -> 5; matrix products, arithmetic and copies ran while one was open for 19% -> 26% of each run, Pallas kernels for 0% -> 11%
where the time goes in v4:
time: 314 us; the launch traced here: 311 us
  waiting for transfers between devices  113 us (36%)
  Pallas kernels  70.4 us (22%)
  other arithmetic  50.1 us (16%)
  local copies, waits for them, and re-layouts  26.3 us (8%)
  starting transfers between devices  21.9 us (7%)
  matrix products  16.6 us (5%)
  between operations  13.6 us (4%)
    pallas_call x2, Pallas kernels, cached_attention(): pl.pallas_call(functools.partial(cached_kernel, scale), grid=(req_dev, po...  70.4 us
    reduce_scatter x2, waiting for transfers between devices, shards(): lax.psum_scatter(partial_out, 'tp', scatter_dimension=2, tiled=True)  68.6 us
    all_to_all x2, waiting for transfers between devices, shards(): lax.all_to_all(outgoing, 'pool', split_axis=0, concat_axis=0, tiled=True)  42.1 us
    all_to_all x2, starting transfers between devices, shards(): lax.all_to_all(outgoing, 'pool', split_axis=0, concat_axis=0, tiled=True)  21.8 us
    reduce_or x1, other arithmetic, shards(): jnp.any(row_ids[..., None] == own_rows[:, :, None, None, None, :], axis=-1)  20.4 us
    dot_general x2, matrix products, shards(): jnp.einsum('rqh,hm->rqm', attn, w_out, preferred_element_type=jnp.float32)  10.4 us
    gather x2, local copies, waits for them, and re-layouts, shards(): outgoing = pool_kv[slot_ids[:, r]]  9.54 us
  transfers between devices with their start and end apart: 5, of which 5 were waited for; matrix products, arithmetic and copies ran while one was open for 26% of the time, Pallas kernels for 11%

profile of v4, /device:TPU:1, one launch (start us, length us, event | category | flops | bytes accessed | tf_op | source)
XLA Modules:
  0.0 311.4 jit_solution(17502286652811347590)
XLA Ops:
  8.2 1.5 gather_fusion
  9.8 1.2 reduce_window_sum.22
  12.5 4.7 %gather_fusion.1 = bf16[512,2,16,128]{3,2,1,0:T(8,128)(2,1)} fusion(bf16[256,2,16,128]{3,2,1,0:T(8,128)(2,1)} %bitcast.157, s32[1024]{0:T(1024)S(1)} %pad_clamp_fusion.2), kind=kCustom, calls=%fused_computation.1 | custom fusion | bytes 8390656 | tf_op jit(solution)/shard_map/gather | solution.py:301
  17.3 12.5 %all-to-all-start = ((bf16[32,4,4,1,2,16,128]{6,5,4,2,1,3,0:T(8,128)(2,1)}), bf16[32,4,4,1,2,16,128]{6,5,4,2,1,3,0:T(8,128)(2,1)}, u32[]{:S(2)}, u32[]{:S(2)}) async-start(bf16[32,4,4,1,2,16,128]{6,5,4,2,1,3,0:T(8,128)(2,1)} %bitcast.160), calls=%async_computation | async-start | bytes 8388608 | tf_op jit(solution)/shard_map/all_to_all | solution.py:304
  30.9 2.3 reduce_window_sum.23
  35.1 20.4 %compare_reduce_fusion = pred[2,4,32,4,16]{4,3,2,1,0:T(4,128)(4,1)S(1)} fusion(s32[2,4,104]{2,1,0:T(4,128)S(1)} %get-tuple-element.42, s32[2,4,32,4,16]{4,3,2,1,0:T(4,128)S(1)} %iota_add_fusion), kind=kLoop, calls=%fused_computation.11 | loop fusion | flops 3391488 | bytes 85248 | tf_op jit(solution)/shard_map/reduce_or | solution.py:283
  57.6 4.8 %gather_fusion.2 = bf16[512,2,16,128]{3,2,1,0:T(8,128)(2,1)} fusion(bf16[256,2,16,128]{3,2,1,0:T(8,128)(2,1)} %bitcast.158, s32[1024]{0:T(1024)S(1)} %pad_clamp_fusion.1), kind=kCustom, calls=%fused_computation.2 | custom fusion | bytes 8390656 | tf_op jit(solution)/shard_map/gather | solution.py:301
  66.1 5.3 %fusion = f32[2,4,104]{2,1,0:T(4,128)S(1)} fusion(bf16[2,4,104,5120]{3,2,1,0:T(8,128)(2,1)} %all-gather.2.cloned.1.call-done), kind=kLoop, calls=%fused_computation.6 | loop fusion | flops 12778688 | bytes 8523008 | tf_op jit(solution)/shard_map/reduce_sum | solution.py:248
  71.9 2.6 fusion.8
  74.6 2.0 fusion.31
  78.3 1.9 copy.165
  80.2 2.8 reshape.530
  83.0 2.3 exponential_reduce_fusion
  85.3 1.7 convolution_bitcast_fusion.2
  87.0 35.3 %all-to-all-done = bf16[32,4,4,1,2,16,128]{6,5,4,2,1,3,0:T(8,128)(2,1)} async-done(((bf16[32,4,4,1,2,16,128]{6,5,4,2,1,3,0:T(8,128)(2,1)}), bf16[32,4,4,1,2,16,128]{6,5,4,2,1,3,0:T(8,128)(2,1)}, u32[]{:S(2)}, u32[]{:S(2)}) %all-to-all-start) | async-done | bytes 4194336 | tf_op jit(solution)/shard_map/all_to_all | solution.py:304
  122.3 9.3 %all-to-all-start.1 = ((bf16[32,4,4,1,2,16,128]{6,5,4,2,1,3,0:T(8,128)(2,1)}), bf16[32,4,4,1,2,16,128]{6,5,4,2,1,3,0:T(8,128)(2,1)}, u32[]{:S(2)}, u32[]{:S(2)}) async-start(bf16[32,4,4,1,2,16,128]{6,5,4,2,1,3,0:T(8,128)(2,1)} %bitcast.159), calls=%async_computation.1 | async-start | bytes 8388608 | tf_op jit(solution)/shard_map/all_to_all | solution.py:304
  136.2 35.2 %shard_map.109 = (f32[1,320,1]{2,1,0:T(8,128)}, f32[1,320,1]{2,1,0:T(8,128)}, f32[1,320,128]{2,1,0:T(8,128)}) custom-call(bf16[1,320,128]{2,1,0:T(8,128)(2,1)} %slice.117.q_ref, bf16[32,1,16,2,16,128]{5,4,3,2,1,0:T(8,128)(2,1)} %bitcast.54.kv_ref, f32[1,32,256]{2,1,0:T(8,128)} %get-tuple-element.56.valid_ref, f32[1,8,128]{2,1,0:T(8,128)} %get-tuple-element.70.table_ref), custom_call_target="tpu_custom_call" | custom-call | tf_op jit(solution)/shard_map/pallas_call | solution.py:138
  174.7 1.2 fusion.47
  176.0 5.2 %convolution_bitcast_fusion.1 = f32[1,64,5120]{2,1,0:T(8,128)} fusion(bf16[640,5120]{1,0:T(8,128)(2,1)} %param.21, bf16[8,8,5,128]{3,2,1,0:T(8,128)(2,1)S(1)} %bitcast.165), kind=kOutput, calls=%fused_computation.13 | convolution fusion | flops 419430400 | bytes 7946240 | tf_op jit(solution)/shard_map/rqh,hm->rqm/dot_general | solution.py:337
  182.7 34.0 %reduce-scatter.3.cloned.1.call-done = f32[1,64,640]{2,1,0:T(8,128)} async-done(((f32[1,64,5120]{2,1,0:T(8,128)}), f32[1,64,640]{2,1,0:T(8,128)}) %reduce-scatter.3.cloned.1.call-update) | async-done | bytes 163856 | tf_op jit(solution)/shard_map/reduce_scatter | solution.py:339
  217.6 6.8 %all-to-all-done.1 = bf16[32,4,4,1,2,16,128]{6,5,4,2,1,3,0:T(8,128)(2,1)} async-done(((bf16[32,4,4,1,2,16,128]{6,5,4,2,1,3,0:T(8,128)(2,1)}), bf16[32,4,4,1,2,16,128]{6,5,4,2,1,3,0:T(8,128)(2,1)}, u32[]{:S(2)}, u32[]{:S(2)}) %all-to-all-start.1) | async-done | bytes 4194336 | tf_op jit(solution)/shard_map/all_to_all | solution.py:304
  224.4 35.2 %shard_map.110 = (f32[1,320,1]{2,1,0:T(8,128)}, f32[1,320,1]{2,1,0:T(8,128)}, f32[1,320,128]{2,1,0:T(8,128)}) custom-call(bf16[1,320,128]{2,1,0:T(8,128)(2,1)} %slice.128.q_ref, bf16[32,1,16,2,16,128]{5,4,3,2,1,0:T(8,128)(2,1)} %bitcast.63.kv_ref, f32[1,32,256]{2,1,0:T(8,128)} %get-tuple-element.55.valid_ref, f32[1,8,128]{2,1,0:T(8,128)} %get-tuple-element.69.table_ref), custom_call_target="tpu_custom_call" | custom-call | tf_op jit(solution)/shard_map/pallas_call | solution.py:138
  263.5 5.2 %convolution_bitcast_fusion = f32[1,64,5120]{2,1,0:T(8,128)} fusion(bf16[640,5120]{1,0:T(8,128)(2,1)} %param.21, bf16[8,8,5,128]{3,2,1,0:T(8,128)(2,1)S(1)} %bitcast.166), kind=kOutput, calls=%fused_computation.12 | convolution fusion | flops 419430400 | bytes 7946240 | tf_op jit(solution)/shard_map/rqh,hm->rqm/dot_general | solution.py:337
  268.7 34.5 %reduce-scatter.5.cloned.1.call-done = f32[1,64,640]{2,1,0:T(8,128)} async-done(((f32[1,64,5120]{2,1,0:T(8,128)}), f32[1,64,640]{2,1,0:T(8,128)}) %reduce-scatter.5.cloned.1.call-update) | async-done | bytes 163856 | tf_op jit(solution)/shard_map/reduce_scatter | solution.py:339
  (120 shorter events, 29.7 us)
Async XLA Ops:
  6.5 64.9 %copy-start = (bf16[5120,2,1,128]{3,1,2,0:T(2,128)(2,1)S(1)}, bf16[5120,2,1,128]{3,1,2,0:T(2,128)(2,1)}, u32[]{:S(2)}) copy-start(bf16[5120,2,1,128]{3,1,2,0:T(2,128)(2,1)} %param.20) | copy-start | bytes 7864324
  6.5 59.5 %all-gather.2.cloned.1.call-start = ((), (), s32[]{:S(2)}) async-start(), calls=%async_computation.4 | async-start | bytes 9584640 | tf_op jit(solution)/shard_map/all_gather | solution.py:245
  17.2 12.5 %copy-start.8 = (s32[64,4]{0,1:T(4,128)S(1)}, s32[64,4]{0,1:T(4,128)}, u32[]{:S(2)}) copy-start(s32[64,4]{0,1:T(4,128)} %param.13) | copy-start | bytes 3076
  17.3 12.5 %copy-start.9 = (s32[64,4]{0,1:T(4,128)S(1)}, s32[64,4]{0,1:T(4,128)}, u32[]{:S(2)}) copy-start(s32[64,4]{0,1:T(4,128)} %param.14) | copy-start | bytes 3076
  17.3 12.7 %copy-start.6 = (bf16[2,64,5,128]{3,1,2,0:T(8,128)(2,1)S(1)}, bf16[2,64,5,128]{3,1,2,0:T(8,128)(2,1)}, u32[]{:S(2)}) copy-start(bf16[2,64,5,128]{3,1,2,0:T(8,128)(2,1)} %param.17) | copy-start | bytes 491524
  17.3 12.7 %copy-start.12 = (s32[64]{0:T(128)S(1)}, s32[64]{0:T(128)}, u32[]{:S(2)}) copy-start(s32[64]{0:T(128)} %param.16) | copy-start | bytes 772
  17.3 13.0 %copy-start.1 = (s32[64,128]{1,0:T(8,128)S(1)}, s32[64,128]{1,0:T(8,128)}, u32[]{:S(2)}) copy-start(s32[64,128]{1,0:T(8,128)} %param.12) | copy-start | bytes 98308
  17.3 105.1 %all-to-all-start = ((bf16[32,4,4,1,2,16,128]{6,5,4,2,1,3,0:T(8,128)(2,1)}), bf16[32,4,4,1,2,16,128]{6,5,4,2,1,3,0:T(8,128)(2,1)}, u32[]{:S(2)}, u32[]{:S(2)}) async-start(bf16[32,4,4,1,2,16,128]{6,5,4,2,1,3,0:T(8,128)(2,1)} %bitcast.160), calls=%async_computation | async-start | bytes 8388608 | tf_op jit(solution)/shard_map/all_to_all | solution.py:304
  30.1 32.7 %copy-start.10 = (s32[2]{0:T(128)}, s32[2]{0:T(128)S(1)}, u32[]{:S(2)}) copy-start(s32[2]{0:T(128)S(1)} %dynamic_slice.14) | copy-start | bytes 28
  57.6 5.5 %copy-start.5 = (bf16[2,64,2,1,128]{4,2,3,1,0:T(2,128)(2,1)S(1)}, bf16[2,64,2,1,128]{4,2,3,1,0:T(2,128)(2,1)}, u32[]{:S(2)}) copy-start(bf16[2,64,2,1,128]{4,2,3,1,0:T(2,128)(2,1)} %param.18) | copy-start | bytes 196612
  66.1 5.8 %copy-start.3 = (bf16[2,4,104,5120]{3,2,1,0:T(8,128)(2,1)S(1)}, bf16[2,4,104,5120]{3,2,1,0:T(8,128)(2,1)}, u32[]{:S(2)}) copy-start(bf16[2,4,104,5120]{3,2,1,0:T(8,128)(2,1)} %all-gather.2.cloned.1.call-done) | copy-start | bytes 25559044
  77.2 1.1 copy-start.2
  122.3 10.3 %copy-start.11 = (s32[2]{0:T(128)S(1)}, s32[2]{0:T(128)}, u32[]{:S(2)}) copy-start(s32[2]{0:T(128)} %copy-done.10) | copy-start | bytes 28
  122.3 102.1 %all-to-all-start.1 = ((bf16[32,4,4,1,2,16,128]{6,5,4,2,1,3,0:T(8,128)(2,1)}), bf16[32,4,4,1,2,16,128]{6,5,4,2,1,3,0:T(8,128)(2,1)}, u32[]{:S(2)}, u32[]{:S(2)}) async-start(bf16[32,4,4,1,2,16,128]{6,5,4,2,1,3,0:T(8,128)(2,1)} %bitcast.159), calls=%async_computation.1 | async-start | bytes 8388608 | tf_op jit(solution)/shard_map/all_to_all | solution.py:304
  131.7 85.0 %reduce-scatter.3.cloned.1.call-start = ((), (), s32[]{:S(2)}) async-start(), calls=%async_computation.5 | async-start | bytes 1474560 | tf_op jit(solution)/shard_map/reduce_scatter | solution.py:339
  131.9 42.8 %copy-start.4 = (f32[2,64,1,5,128]{4,1,3,0,2:T(8,128)S(1)}, f32[2,64,1,5,128]{4,1,3,0,2:T(8,128)}, u32[]{:S(2)}) copy-start(f32[2,64,1,5,128]{4,1,3,0,2:T(8,128)} %convolution_bitcast_fusion.3) | copy-start | bytes 983044
  181.2 81.0 %copy-start.7 = (f32[2,64,5]{1,2,0:T(8,128)S(1)}, f32[2,64,5]{1,2,0:T(8,128)}, u32[]{:S(2)}) copy-start(f32[2,64,5]{1,2,0:T(8,128)} %exponential_reduce_fusion) | copy-start | bytes 7684
  181.2 122.0 %reduce-scatter.5.cloned.1.call-start = ((), (), s32[]{:S(2)}) async-start(), calls=%async_computation.6 | async-start | bytes 1474560 | tf_op jit(solution)/shard_map/reduce_scatter | solution.py:339
Sparse Core Ops, SparseCore 0:
  9.2 56.8 all-gather.1
  181.3 35.3 reduce-scatter.2
  268.8 34.3 reduce-scatter.4

commit v5 on v4

--- a/solution.py
+++ b/solution.py
@@ -304,6 +304,19 @@
         arrivals.append(lax.all_to_all(outgoing, "pool", split_axis=0, concat_axis=0, tiled=True))
     fresh_peak, fresh_sum, fresh_acc, own_peak, own_sum, own_acc, valid, tables = local
 
+    tp_count = lax.axis_size("tp")
+    out_cols = w_out.shape[1] // tp_count
+    rank = lax.axis_index("tp")
+    blocks = w_out.reshape(w_out.shape[0], tp_count, out_cols)
+    shifted = []
+    for k in range(tp_count):
+        piece = lax.dynamic_index_in_dim(blocks, (rank + k) % tp_count, axis=1, keepdims=False)
+        if k:
+            piece = lax.ppermute(
+                piece, "tp", [(i, (i + k) % tp_count) for i in range(tp_count)]
+            )
+        shifted.append(piece)
+    columns = jnp.stack(shifted)
     flat_queries = queries.reshape(req_dev, qlen * heads, head_dim)
     outputs = []
     for r in range(req_dev):
@@ -332,12 +345,17 @@
         attn = (
             jnp.where(live[None, :, None, None, None], attn, 0.0)
             .astype(jnp.bfloat16)
-            .reshape(1, qlen, heads * head_dim)
-        )
-        partial_out = jnp.einsum("rqh,hm->rqm", attn, w_out, preferred_element_type=jnp.float32)
-        outputs.append(
-            lax.psum_scatter(partial_out, "tp", scatter_dimension=2, tiled=True).astype(jnp.bfloat16)
-        )
+            .reshape(qlen, heads * head_dim)
+        )
+        gathered = jnp.stack(
+            [attn]
+            + [
+                lax.ppermute(attn, "tp", [(i, (i + k) % tp_count) for i in range(tp_count)])
+                for k in range(1, tp_count)
+            ]
+        )
+        out = jnp.einsum("tqh,thm->qm", gathered, columns, preferred_element_type=jnp.float32)
+        outputs.append(out.astype(jnp.bfloat16)[None])
     return jnp.concatenate(outputs, axis=0)
 
 

time: 314 us -> 376 us (1.20)
  local copies, waits for them, and re-layouts: 26.3 us -> 82.3 us
  starting transfers between devices: 21.9 us -> 47.6 us
  waiting for transfers between devices: 113 us -> 99.4 us
  other arithmetic: 50.1 us -> 45.2 us
    reduce_scatter x2 -> x0, waiting for transfers between devices: 68.6 us -> none  [shards(): lax.psum_scatter(partial_out, 'tp', scatter_dimension=2, tiled=True)]
    ppermute x0 -> x21, waiting for transfers between devices: none -> 57 us  [the longest x7 49.2 us: shards(): lax.ppermute(piece, 'tp', [(i, (i + k) % tp_count) for i in range(tp_coun...]
    dynamic_slice x0 -> x1, local copies, waits for them, and re-layouts: none -> 31.8 us  [shards(): lax.dynamic_index_in_dim(blocks, (rank + k) % tp_count, axis=1, keepdims=...]
    ppermute x0 -> x21, starting transfers between devices: none -> 25.6 us  [the longest x14 16.4 us: shards(): lax.ppermute(attn, 'tp', [(i, (i + k) % tp_count) for i in range(tp_count)])]
    unnamed x26 -> x59, local copies, waits for them, and re-layouts: 1.64 us -> 26.7 us
  transfers between devices with their start and end apart: 5 -> 24, of which waited for: 5 -> 12; matrix products, arithmetic and copies ran while one was open for 26% -> 35% of each run, Pallas kernels for 11% -> 9%
where the time goes in v5:
time: 376 us; the launch traced here: 372 us
  waiting for transfers between devices  99.4 us (26%)
  local copies, waits for them, and re-layouts  82.3 us (22%)
  Pallas kernels  70.4 us (19%)
  starting transfers between devices  47.6 us (13%)
  other arithmetic  45.2 us (12%)
  between operations  14.4 us (4%)
  matrix products  13.2 us (4%)
    pallas_call x2, Pallas kernels, cached_attention(): pl.pallas_call(functools.partial(cached_kernel, scale), grid=(req_dev, po...  70.4 us
    ppermute x7, waiting for transfers between devices, shards(): lax.ppermute(piece, 'tp', [(i, (i + k) % tp_count) for i in range(tp_coun...  49.2 us
    all_to_all x2, waiting for transfers between devices, shards(): lax.all_to_all(outgoing, 'pool', split_axis=0, concat_axis=0, tiled=True)  39.3 us
    dynamic_slice x1, local copies, waits for them, and re-layouts, shards(): lax.dynamic_index_in_dim(blocks, (rank + k) % tp_count, axis=1, keepdims=...  31.8 us
    unnamed x59, local copies, waits for them, and re-layouts  26.7 us
    all_to_all x2, starting transfers between devices, shards(): lax.all_to_all(outgoing, 'pool', split_axis=0, concat_axis=0, tiled=True)  22.1 us
    reduce_or x1, other arithmetic, shards(): jnp.any(row_ids[..., None] == own_rows[:, :, None, None, None, :], axis=-1)  20.4 us
    ppermute x14, starting transfers between devices, shards(): lax.ppermute(attn, 'tp', [(i, (i + k) % tp_count) for i in range(tp_count)])  16.4 us
  transfers between devices with their start and end apart: 24, of which 12 were waited for; matrix products, arithmetic and copies ran while one was open for 35% of the time, Pallas kernels for 9%

profile of v5, /device:TPU:1, one launch (start us, length us, event | category | flops | bytes accessed | tf_op | source)
XLA Modules:
  0.0 372.5 jit_solution(2856465107902619861)
XLA Ops:
  12.1 4.8 %gather_fusion.1 = bf16[512,2,16,128]{3,2,1,0:T(8,128)(2,1)} fusion(bf16[256,2,16,128]{3,2,1,0:T(8,128)(2,1)} %bitcast.245, s32[1024]{0:T(1024)S(1)} %get-tuple-element.95), kind=kCustom, calls=%fused_computation.1 | custom fusion | bytes 8390656 | tf_op jit(solution)/shard_map/gather | solution.py:301
  17.0 12.5 %all-to-all-start = ((bf16[32,4,4,1,2,16,128]{6,5,4,2,1,3,0:T(8,128)(2,1)}), bf16[32,4,4,1,2,16,128]{6,5,4,2,1,3,0:T(8,128)(2,1)}, u32[]{:S(2)}, u32[]{:S(2)}) async-start(bf16[32,4,4,1,2,16,128]{6,5,4,2,1,3,0:T(8,128)(2,1)} %bitcast.248), calls=%async_computation | async-start | bytes 8388608 | tf_op jit(solution)/shard_map/all_to_all | solution.py:304
  30.5 2.3 reduce_window_sum.23
  34.8 20.4 %compare_reduce_fusion = pred[2,4,32,4,16]{4,3,2,1,0:T(4,128)(4,1)S(1)} fusion(s32[2,4,104]{2,1,0:T(4,128)S(1)} %get-tuple-element.42, s32[2,4,32,4,16]{4,3,2,1,0:T(4,128)S(1)} %iota_add_fusion), kind=kLoop, calls=%fused_computation.11 | loop fusion | flops 3391488 | bytes 85248 | tf_op jit(solution)/shard_map/reduce_or | solution.py:283
  56.3 4.8 %gather_fusion.2 = bf16[512,2,16,128]{3,2,1,0:T(8,128)(2,1)} fusion(bf16[256,2,16,128]{3,2,1,0:T(8,128)(2,1)} %bitcast.246, s32[1024]{0:T(1024)S(1)} %get-tuple-element.94), kind=kCustom, calls=%fused_computation.2 | custom fusion | bytes 8390656 | tf_op jit(solution)/shard_map/gather | solution.py:301
  63.6 2.4 all-gather.2.cloned.1.call-done
  66.1 5.3 %fusion = f32[2,4,104]{2,1,0:T(4,128)S(1)} fusion(bf16[2,4,104,5120]{3,2,1,0:T(8,128)(2,1)} %all-gather.2.cloned.1.call-done), kind=kLoop, calls=%fused_computation.6 | loop fusion | flops 12778688 | bytes 8523008 | tf_op jit(solution)/shard_map/reduce_sum | solution.py:248
  71.9 2.6 fusion.8
  78.9 2.3 reshape.528
  82.5 39.3 %all-to-all-done = bf16[32,4,4,1,2,16,128]{6,5,4,2,1,3,0:T(8,128)(2,1)} async-done(((bf16[32,4,4,1,2,16,128]{6,5,4,2,1,3,0:T(8,128)(2,1)}), bf16[32,4,4,1,2,16,128]{6,5,4,2,1,3,0:T(8,128)(2,1)}, u32[]{:S(2)}, u32[]{:S(2)}) %all-to-all-start) | async-done | bytes 4194336 | tf_op jit(solution)/shard_map/all_to_all | solution.py:304
  121.8 9.6 %all-to-all-start.1 = ((bf16[32,4,4,1,2,16,128]{6,5,4,2,1,3,0:T(8,128)(2,1)}), bf16[32,4,4,1,2,16,128]{6,5,4,2,1,3,0:T(8,128)(2,1)}, u32[]{:S(2)}, u32[]{:S(2)}) async-start(bf16[32,4,4,1,2,16,128]{6,5,4,2,1,3,0:T(8,128)(2,1)} %bitcast.247), calls=%async_computation.1 | async-start | bytes 8388608 | tf_op jit(solution)/shard_map/all_to_all | solution.py:304
  131.5 7.1 %copy.258 = bf16[80,8,8,640]{3,2,1,0:T(8,128)(2,1)} copy(bf16[80,8,8,640]{3,1,2,0:T(8,128)(2,1)} %bitcast.249) | data formatting | bytes 13107200
  138.6 31.8 %constant_dynamic-slice_fusion.7 = (bf16[640,1,640]{2,1,0:T(2,128)(2,1)S(1)}, bf16[640,1,640]{2,1,0:T(2,128)(2,1)S(1)}, bf16[640,1,640]{2,1,0:T(2,128)(2,1)S(1)}...) fusion(bf16[640,8,640]{2,1,0:T(8,128)(2,1)} %bitcast.244, ...), kind=kLoop, calls=%fused_computation.194 | loop fusion | bytes 13107232 | tf_op jit(solution)/shard_map/jit(dynamic_index_in_dim)/dynamic_slice | solution.py:313
  171.3 2.2 collective-permute-start.7
  194.1 16.0 %collective-permute-done.8 = bf16[640,640]{1,0:T(8,128)(2,1)} collective-permute-done((bf16[640,640]{1,0:T(8,128)(2,1)}, bf16[640,640]{1,0:T(8,128)(2,1)}, u32[]{:S(2)}, u32[]{:S(2)}) %collective-permute-start.8) | collective-permute-done | bytes 819232 | tf_op jit(solution)/shard_map/ppermute | solution.py:315
  210.1 2.1 bitcast_dynamic-update-slice_fusion.5
  212.2 13.2 %collective-permute-done.9 = bf16[640,640]{1,0:T(8,128)(2,1)} collective-permute-done((bf16[640,640]{1,0:T(8,128)(2,1)}, bf16[640,640]{1,0:T(8,128)(2,1)}, u32[]{:S(2)}, u32[]{:S(2)}) %collective-permute-start.9) | collective-permute-done | bytes 819232 | tf_op jit(solution)/shard_map/ppermute | solution.py:315
  225.4 2.1 bitcast_dynamic-update-slice_fusion.4
  227.6 18.3 %collective-permute-done.10 = bf16[640,640]{1,0:T(8,128)(2,1)} collective-permute-done((bf16[640,640]{1,0:T(8,128)(2,1)}, bf16[640,640]{1,0:T(8,128)(2,1)}, u32[]{:S(2)}, u32[]{:S(2)}) %collective-permute-start.10) | collective-permute-done | bytes 819232 | tf_op jit(solution)/shard_map/ppermute | solution.py:315
  253.4 35.2 %shard_map.109 = (f32[1,320,1]{2,1,0:T(8,128)}, f32[1,320,1]{2,1,0:T(8,128)}, f32[1,320,128]{2,1,0:T(8,128)}) custom-call(bf16[1,320,128]{2,1,0:T(8,128)(2,1)} %slice.117.q_ref, bf16[32,1,16,2,16,128]{5,4,3,2,1,0:T(8,128)(2,1)} %bitcast.54.kv_ref, f32[1,32,256]{2,1,0:T(8,128)} %get-tuple-element.64.valid_ref, f32[1,8,128]{2,1,0:T(8,128)} %get-tuple-element.78.table_ref), custom_call_target="tpu_custom_call" | custom-call | tf_op jit(solution)/shard_map/pallas_call | solution.py:138
  304.6 4.1 %fusion.18 = bf16[1,64,640]{2,1,0:T(8,128)(2,1)S(1)} fusion(bf16[8,64,640]{2,1,0:T(8,128)(2,1)S(1)} %bitcast_dynamic-update-slice_fusion.14, bf16[8,640,640]{2,1,0:T(8,128)(2,1)} %bitcast_dynamic-update-slice_fusion), kind=kOutput, calls=%fused_computation.28 | convolution fusion | flops 419471360 | bytes 7290880 | tf_op jit(solution)/shard_map/tqh,thm->qm/dot_general | solution.py:357
  308.7 35.2 %shard_map.110 = (f32[1,320,1]{2,1,0:T(8,128)}, f32[1,320,1]{2,1,0:T(8,128)}, f32[1,320,128]{2,1,0:T(8,128)}) custom-call(bf16[1,320,128]{2,1,0:T(8,128)(2,1)} %slice.128.q_ref, bf16[32,1,16,2,16,128]{5,4,3,2,1,0:T(8,128)(2,1)} %bitcast.86.kv_ref, f32[1,32,256]{2,1,0:T(8,128)} %get-tuple-element.63.valid_ref, f32[1,8,128]{2,1,0:T(8,128)} %get-tuple-element.77.table_ref), custom_call_target="tpu_custom_call" | custom-call | tf_op jit(solution)/shard_map/pallas_call | solution.py:138
  349.5 2.7 collective-permute-start.16
  360.5 4.3 %fusion.17 = bf16[1,64,640]{2,1,0:T(8,128)(2,1)S(1)} fusion(bf16[8,64,640]{2,1,0:T(8,128)(2,1)S(1)} %bitcast_dynamic-update-slice_fusion.7, bf16[8,640,640]{2,1,0:T(8,128)(2,1)} %bitcast_dynamic-update-slice_fusion), kind=kOutput, calls=%fused_computation.27 | convolution fusion | flops 419471360 | bytes 7290880 | tf_op jit(solution)/shard_map/tqh,thm->qm/dot_general | solution.py:357
  (193 shorter events, 77.5 us)
Async XLA Ops:
  6.5 59.5 %all-gather.2.cloned.1.call-start = ((), (), s32[]{:S(2)}) async-start(), calls=%async_computation.2 | async-start | bytes 9584640 | tf_op jit(solution)/shard_map/all_gather | solution.py:245
  17.0 104.9 %all-to-all-start = ((bf16[32,4,4,1,2,16,128]{6,5,4,2,1,3,0:T(8,128)(2,1)}), bf16[32,4,4,1,2,16,128]{6,5,4,2,1,3,0:T(8,128)(2,1)}, u32[]{:S(2)}, u32[]{:S(2)}) async-start(bf16[32,4,4,1,2,16,128]{6,5,4,2,1,3,0:T(8,128)(2,1)} %bitcast.248), calls=%async_computation | async-start | bytes 8388608 | tf_op jit(solution)/shard_map/all_to_all | solution.py:304
  121.8 186.9 %all-to-all-start.1 = ((bf16[32,4,4,1,2,16,128]{6,5,4,2,1,3,0:T(8,128)(2,1)}), bf16[32,4,4,1,2,16,128]{6,5,4,2,1,3,0:T(8,128)(2,1)}, u32[]{:S(2)}, u32[]{:S(2)}) async-start(bf16[32,4,4,1,2,16,128]{6,5,4,2,1,3,0:T(8,128)(2,1)} %bitcast.247), calls=%async_computation.1 | async-start | bytes 8388608 | tf_op jit(solution)/shard_map/all_to_all | solution.py:304
  171.3 19.0 %collective-permute-start.7 = (bf16[640,640]{1,0:T(8,128)(2,1)}, bf16[640,640]{1,0:T(8,128)(2,1)}, u32[]{:S(2)}, u32[]{:S(2)}) collective-permute-start(bf16[640,640]{1,0:T(8,128)(2,1)} %bitcast.240), channel_id=1, source_target_pairs={{0,1},{1,2},{2,3},{3,4},{4,5},{5,6},{6,7},{7,0},{8,9},{9,10},{10,1... | collective-permute-start | bytes 2457608 | tf_op jit(solution)/shard_map/ppermute | solution.py:315
  174.6 35.5 %collective-permute-start.8 = (bf16[640,640]{1,0:T(8,128)(2,1)}, bf16[640,640]{1,0:T(8,128)(2,1)}, u32[]{:S(2)}, u32[]{:S(2)}) collective-permute-start(bf16[640,640]{1,0:T(8,128)(2,1)} %bitcast.239), channel_id=1, source_target_pairs={{0,2},{1,3},{2,4},{3,5},{4,6},{5,7},{6,0},{7,1},{8,10},{9,11},{10,... | collective-permute-start | bytes 2457608 | tf_op jit(solution)/shard_map/ppermute | solution.py:315
  176.9 48.6 %collective-permute-start.9 = (bf16[640,640]{1,0:T(8,128)(2,1)}, bf16[640,640]{1,0:T(8,128)(2,1)}, u32[]{:S(2)}, u32[]{:S(2)}) collective-permute-start(bf16[640,640]{1,0:T(8,128)(2,1)} %bitcast.238), channel_id=1, source_target_pairs={{0,3},{1,4},{2,5},{3,6},{4,7},{5,0},{6,1},{7,2},{8,11},{9,12},{10,... | collective-permute-start | bytes 2457608 | tf_op jit(solution)/shard_map/ppermute | solution.py:315
  179.4 66.5 %collective-permute-start.10 = (bf16[640,640]{1,0:T(8,128)(2,1)}, bf16[640,640]{1,0:T(8,128)(2,1)}, u32[]{:S(2)}, u32[]{:S(2)}) collective-permute-start(bf16[640,640]{1,0:T(8,128)(2,1)} %bitcast.237), channel_id=1, source_target_pairs={{0,4},{1,5},{2,6},{3,7},{4,0},{5,1},{6,2},{7,3},{8,12},{9,13},{10,... | collective-permute-start | bytes 2457608 | tf_op jit(solution)/shard_map/ppermute | solution.py:315
  180.0 68.0 %collective-permute-start.11 = (bf16[640,640]{1,0:T(8,128)(2,1)S(1)}, bf16[640,640]{1,0:T(8,128)(2,1)}, u32[]{:S(2)}, u32[]{:S(2)}) collective-permute-start(bf16[640,640]{1,0:T(8,128)(2,1)S(1)} %bitcast.256), channel_id=1, source_target_pairs={{0,5},{1,6},{2,7},{3,0},{4,1},{5,2},{6,3},{7,4},{8,13},{9,14},{10,... | collective-permute-start | bytes 2457608 | tf_op jit(solution)/shard_map/ppermute | solution.py:315
  190.3 59.8 %collective-permute-start.12 = (bf16[640,640]{1,0:T(8,128)(2,1)}, bf16[640,640]{1,0:T(8,128)(2,1)S(1)}, u32[]{:S(2)}, u32[]{:S(2)}) collective-permute-start(bf16[640,640]{1,0:T(8,128)(2,1)} %bitcast.258), channel_id=1, source_target_pairs={{0,6},{1,7},{2,0},{3,1},{4,2},{5,3},{6,4},{7,5},{8,14},{9,15},{10,... | collective-permute-start | bytes 2457608 | tf_op jit(solution)/shard_map/ppermute | solution.py:315
  210.1 41.0 %collective-permute-start.13 = (bf16[640,640]{1,0:T(8,128)(2,1)}, bf16[640,640]{1,0:T(8,128)(2,1)S(1)}, u32[]{:S(2)}, u32[]{:S(2)}) collective-permute-start(bf16[640,640]{1,0:T(8,128)(2,1)} %bitcast.257), channel_id=1, source_target_pairs={{0,7},{1,0},{2,1},{3,2},{4,3},{5,4},{6,5},{7,6},{8,15},{9,8},{10,9... | collective-permute-start | bytes 2457608 | tf_op jit(solution)/shard_map/ppermute | solution.py:315
  292.7 5.4 %collective-permute-start = (bf16[64,640]{1,0:T(8,128)(2,1)S(1)}, bf16[64,640]{1,0:T(8,128)(2,1)S(1)}, u32[]{:S(2)}, u32[]{:S(2)}) collective-permute-start(bf16[64,640]{1,0:T(8,128)(2,1)S(1)} %bitcast.268), channel_id=1, source_target_pairs={{0,1},{1,2},{2,3},{3,4},{4,5},{5,6},{6,7},{7,0},{8,9},{9,10},{10,1... | collective-permute-start | bytes 245768 | tf_op jit(solution)/shard_map/ppermute | solution.py:353
  292.7 6.4 %collective-permute-start.1 = (bf16[64,640]{1,0:T(8,128)(2,1)S(1)}, bf16[64,640]{1,0:T(8,128)(2,1)S(1)}, u32[]{:S(2)}, u32[]{:S(2)}) collective-permute-start(bf16[64,640]{1,0:T(8,128)(2,1)S(1)} %bitcast.269), channel_id=1, source_target_pairs={{0,2},{1,3},{2,4},{3,5},{4,6},{5,7},{6,0},{7,1},{8,10},{9,11},{10,... | collective-permute-start | bytes 245768 | tf_op jit(solution)/shard_map/ppermute | solution.py:353
  294.0 6.5 %collective-permute-start.2 = (bf16[64,640]{1,0:T(8,128)(2,1)S(1)}, bf16[64,640]{1,0:T(8,128)(2,1)S(1)}, u32[]{:S(2)}, u32[]{:S(2)}) collective-permute-start(bf16[64,640]{1,0:T(8,128)(2,1)S(1)} %bitcast.270), channel_id=1, source_target_pairs={{0,3},{1,4},{2,5},{3,6},{4,7},{5,0},{6,1},{7,2},{8,11},{9,12},{10,... | collective-permute-start | bytes 245768 | tf_op jit(solution)/shard_map/ppermute | solution.py:353
  296.1 5.7 %collective-permute-start.3 = (bf16[64,640]{1,0:T(8,128)(2,1)S(1)}, bf16[64,640]{1,0:T(8,128)(2,1)S(1)}, u32[]{:S(2)}, u32[]{:S(2)}) collective-permute-start(bf16[64,640]{1,0:T(8,128)(2,1)S(1)} %bitcast.271), channel_id=1, source_target_pairs={{0,4},{1,5},{2,6},{3,7},{4,0},{5,1},{6,2},{7,3},{8,12},{9,13},{10,... | collective-permute-start | bytes 245768 | tf_op jit(solution)/shard_map/ppermute | solution.py:353
  297.6 5.4 %collective-permute-start.4 = (bf16[64,640]{1,0:T(8,128)(2,1)S(1)}, bf16[64,640]{1,0:T(8,128)(2,1)S(1)}, u32[]{:S(2)}, u32[]{:S(2)}) collective-permute-start(bf16[64,640]{1,0:T(8,128)(2,1)S(1)} %bitcast.272), channel_id=1, source_target_pairs={{0,5},{1,6},{2,7},{3,0},{4,1},{5,2},{6,3},{7,4},{8,13},{9,14},{10,... | collective-permute-start | bytes 245768 | tf_op jit(solution)/shard_map/ppermute | solution.py:353
  298.1 4.9 %collective-permute-start.5 = (bf16[64,640]{1,0:T(8,128)(2,1)S(1)}, bf16[64,640]{1,0:T(8,128)(2,1)S(1)}, u32[]{:S(2)}, u32[]{:S(2)}) collective-permute-start(bf16[64,640]{1,0:T(8,128)(2,1)S(1)} %bitcast.273), channel_id=1, source_target_pairs={{0,6},{1,7},{2,0},{3,1},{4,2},{5,3},{6,4},{7,5},{8,14},{9,15},{10,... | collective-permute-start | bytes 245768 | tf_op jit(solution)/shard_map/ppermute | solution.py:353
  299.1 5.4 %collective-permute-start.6 = (bf16[64,640]{1,0:T(8,128)(2,1)S(1)}, bf16[64,640]{1,0:T(8,128)(2,1)S(1)}, u32[]{:S(2)}, u32[]{:S(2)}) collective-permute-start(bf16[64,640]{1,0:T(8,128)(2,1)S(1)} %bitcast.274), channel_id=1, source_target_pairs={{0,7},{1,0},{2,1},{3,2},{4,3},{5,4},{6,5},{7,6},{8,15},{9,8},{10,9... | collective-permute-start | bytes 245768 | tf_op jit(solution)/shard_map/ppermute | solution.py:353
  347.9 6.3 %collective-permute-start.14 = (bf16[64,640]{1,0:T(8,128)(2,1)S(1)}, bf16[64,640]{1,0:T(8,128)(2,1)S(1)}, u32[]{:S(2)}, u32[]{:S(2)}) collective-permute-start(bf16[64,640]{1,0:T(8,128)(2,1)S(1)} %bitcast.275), channel_id=1, source_target_pairs={{0,1},{1,2},{2,3},{3,4},{4,5},{5,6},{6,7},{7,0},{8,9},{9,10},{10,1... | collective-permute-start | bytes 245768 | tf_op jit(solution)/shard_map/ppermute | solution.py:353
  349.0 5.9 %collective-permute-start.15 = (bf16[64,640]{1,0:T(8,128)(2,1)S(1)}, bf16[64,640]{1,0:T(8,128)(2,1)S(1)}, u32[]{:S(2)}, u32[]{:S(2)}) collective-permute-start(bf16[64,640]{1,0:T(8,128)(2,1)S(1)} %bitcast.276), channel_id=1, source_target_pairs={{0,2},{1,3},{2,4},{3,5},{4,6},{5,7},{6,0},{7,1},{8,10},{9,11},{10,... | collective-permute-start | bytes 245768 | tf_op jit(solution)/shard_map/ppermute | solution.py:353
  349.5 7.1 %collective-permute-start.16 = (bf16[64,640]{1,0:T(8,128)(2,1)S(1)}, bf16[64,640]{1,0:T(8,128)(2,1)S(1)}, u32[]{:S(2)}, u32[]{:S(2)}) collective-permute-start(bf16[64,640]{1,0:T(8,128)(2,1)S(1)} %bitcast.277), channel_id=1, source_target_pairs={{0,3},{1,4},{2,5},{3,6},{4,7},{5,0},{6,1},{7,2},{8,11},{9,12},{10,... | collective-permute-start | bytes 245768 | tf_op jit(solution)/shard_map/ppermute | solution.py:353
  352.2 6.1 %collective-permute-start.17 = (bf16[64,640]{1,0:T(8,128)(2,1)S(1)}, bf16[64,640]{1,0:T(8,128)(2,1)S(1)}, u32[]{:S(2)}, u32[]{:S(2)}) collective-permute-start(bf16[64,640]{1,0:T(8,128)(2,1)S(1)} %bitcast.278), channel_id=1, source_target_pairs={{0,4},{1,5},{2,6},{3,7},{4,0},{5,1},{6,2},{7,3},{8,12},{9,13},{10,... | collective-permute-start | bytes 245768 | tf_op jit(solution)/shard_map/ppermute | solution.py:353
  353.1 6.1 %collective-permute-start.18 = (bf16[64,640]{1,0:T(8,128)(2,1)S(1)}, bf16[64,640]{1,0:T(8,128)(2,1)S(1)}, u32[]{:S(2)}, u32[]{:S(2)}) collective-permute-start(bf16[64,640]{1,0:T(8,128)(2,1)S(1)} %bitcast.279), channel_id=1, source_target_pairs={{0,5},{1,6},{2,7},{3,0},{4,1},{5,2},{6,3},{7,4},{8,13},{9,14},{10,... | collective-permute-start | bytes 245768 | tf_op jit(solution)/shard_map/ppermute | solution.py:353
  354.3 5.0 %collective-permute-start.19 = (bf16[64,640]{1,0:T(8,128)(2,1)S(1)}, bf16[64,640]{1,0:T(8,128)(2,1)S(1)}, u32[]{:S(2)}, u32[]{:S(2)}) collective-permute-start(bf16[64,640]{1,0:T(8,128)(2,1)S(1)} %bitcast.280), channel_id=1, source_target_pairs={{0,6},{1,7},{2,0},{3,1},{4,2},{5,3},{6,4},{7,5},{8,14},{9,15},{10,... | collective-permute-start | bytes 245768 | tf_op jit(solution)/shard_map/ppermute | solution.py:353
  354.9 5.6 %collective-permute-start.20 = (bf16[64,640]{1,0:T(8,128)(2,1)S(1)}, bf16[64,640]{1,0:T(8,128)(2,1)S(1)}, u32[]{:S(2)}, u32[]{:S(2)}) collective-permute-start(bf16[64,640]{1,0:T(8,128)(2,1)S(1)} %bitcast.281), channel_id=1, source_target_pairs={{0,7},{1,0},{2,1},{3,2},{4,3},{5,4},{6,5},{7,6},{8,15},{9,8},{10,9... | collective-permute-start | bytes 245768 | tf_op jit(solution)/shard_map/ppermute | solution.py:353
  (14 other events, 305.9 us)
Sparse Core Ops, SparseCore 0:
  9.2 56.8 all-gather.1

commit v6 on v4

--- a/solution.py
+++ b/solution.py
@@ -104,15 +104,19 @@
         values = kv_ref[i, 0, :, 1].reshape(n_pages * page_rows, head_dim)
         keys = (keys * cosine + pltpu.roll(keys, head_dim // 2, 1) * sine).astype(jnp.bfloat16)
         scores = lax.dot_general(
-            query, keys, (((1,), (1,)), ((), ())), preferred_element_type=jnp.float32
+            keys, query, (((1,), (1,)), ((), ())), preferred_element_type=jnp.float32
         ) * scale
-        valid = valid_ref[0, pl.ds(i, 1), :] > 0.5
+        valid = valid_ref[0, i] > 0.5
         masked = jnp.where(valid, scores, NEGATIVE)
-        peak = jnp.max(masked, axis=1, keepdims=True)
+        peak = jnp.max(masked, axis=0, keepdims=True)
         powers = jnp.where(valid, jnp.exp(masked - peak), 0.0)
-        total = jnp.sum(powers, axis=1, keepdims=True)
-        acc = jnp.dot(powers.astype(jnp.bfloat16), values, preferred_element_type=jnp.float32)
-        normalised = (acc / jnp.maximum(total, 1.0)).astype(jnp.bfloat16).astype(jnp.float32)
+        total = jnp.sum(powers, axis=0, keepdims=True)
+        acc = lax.dot_general(
+            values, powers.astype(jnp.bfloat16), (((0,), (0,)), ((), ())),
+            preferred_element_type=jnp.float32,
+        )
+        inverse = 1.0 / jnp.maximum(total, 1.0)
+        normalised = (acc * inverse).astype(jnp.bfloat16).astype(jnp.float32)
         old = m_acc[...]
         merged = jnp.maximum(old, peak)
         rescale = jnp.exp(old - merged)
@@ -135,33 +139,34 @@
     req_dev, rows, head_dim = queries.shape
     pool_count = arrived.shape[0]
     kv_block = (SET_BLOCK,) + (1,) + arrived.shape[2:]
-    return pl.pallas_call(
+    valid = valid[..., None]
+    peak, total, num = pl.pallas_call(
         functools.partial(cached_kernel, scale),
         grid=(req_dev, pool_count // SET_BLOCK),
         in_specs=[
             pl.BlockSpec((1, rows, head_dim), lambda r, j: (r, 0, 0)),
             pl.BlockSpec(kv_block, lambda r, j: (j, r, 0, 0, 0, 0)),
-            pl.BlockSpec((1, SET_BLOCK, valid.shape[2]), lambda r, j: (r, j, 0)),
+            pl.BlockSpec((1, SET_BLOCK, valid.shape[2], 1), lambda r, j: (r, j, 0, 0)),
             pl.BlockSpec((1,) + tables.shape[1:], lambda r, j: (r, 0, 0)),
         ],
         out_specs=[
-            pl.BlockSpec((1, rows, 1), lambda r, j: (r, 0, 0)),
-            pl.BlockSpec((1, rows, 1), lambda r, j: (r, 0, 0)),
-            pl.BlockSpec((1, rows, head_dim), lambda r, j: (r, 0, 0)),
+            pl.BlockSpec((1, 1, rows), lambda r, j: (r, 0, 0)),
+            pl.BlockSpec((1, 1, rows), lambda r, j: (r, 0, 0)),
+            pl.BlockSpec((1, head_dim, rows), lambda r, j: (r, 0, 0)),
         ],
         out_shape=[
-            jax.ShapeDtypeStruct((req_dev, rows, 1), jnp.float32),
-            jax.ShapeDtypeStruct((req_dev, rows, 1), jnp.float32),
-            jax.ShapeDtypeStruct((req_dev, rows, head_dim), jnp.float32),
+            jax.ShapeDtypeStruct((req_dev, 1, rows), jnp.float32),
+            jax.ShapeDtypeStruct((req_dev, 1, rows), jnp.float32),
+            jax.ShapeDtypeStruct((req_dev, head_dim, rows), jnp.float32),
         ],
         scratch_shapes=[
-            pltpu.VMEM((rows, 1), jnp.float32),
-            pltpu.VMEM((rows, 1), jnp.float32),
-            pltpu.VMEM((rows, head_dim), jnp.float32),
+            pltpu.VMEM((1, rows), jnp.float32),
+            pltpu.VMEM((1, rows), jnp.float32),
+            pltpu.VMEM((head_dim, rows), jnp.float32),
         ],
         compiler_params=pltpu.CompilerParams(dimension_semantics=("parallel", "arbitrary")),
     )(queries, arrived, valid, tables)
-
+    return (peak, total, jnp.swapaxes(num, 1, 2))
 
 def shards(
     pool_kv,

time: 314 us -> 301 us (0.959)
  Pallas kernels: 70.4 us -> 40.8 us
  local copies, waits for them, and re-layouts: 26.3 us -> 39.4 us
  waiting for transfers between devices: 113 us -> 118 us
    pallas_call x2, Pallas kernels: 70.4 us -> 40.8 us  [cached_attention(): pl.pallas_call(functools.partial(cached_kernel, scale), grid=(req_dev, po...]
    all_to_all x2, waiting for transfers between devices: 42.1 us -> 53 us  [shards(): lax.all_to_all(outgoing, 'pool', split_axis=0, concat_axis=0, tiled=True)]
    broadcast_in_dim x0 -> x3, local copies, waits for them, and re-layouts: none -> 10.8 us  [cached_attention(): valid = valid[..., None]]
    reduce_scatter x2, waiting for transfers between devices: 68.6 us -> 62.7 us  [shards(): lax.psum_scatter(partial_out, 'tp', scatter_dimension=2, tiled=True)]
  transfers between devices with their start and end apart: 5 -> 5, of which waited for: 5 -> 5; matrix products, arithmetic and copies ran while one was open for 26% -> 30% of each run, Pallas kernels for 11% -> 7%
where the time goes in v6:
time: 301 us; the launch traced here: 299 us
  waiting for transfers between devices  118 us (39%)
  other arithmetic  48.6 us (16%)
  Pallas kernels  40.8 us (14%)
  local copies, waits for them, and re-layouts  39.4 us (13%)
  starting transfers between devices  21.9 us (7%)
  matrix products  16.7 us (6%)
  between operations  13.6 us (5%)
    reduce_scatter x2, waiting for transfers between devices, shards(): lax.psum_scatter(partial_out, 'tp', scatter_dimension=2, tiled=True)  62.7 us
    all_to_all x2, waiting for transfers between devices, shards(): lax.all_to_all(outgoing, 'pool', split_axis=0, concat_axis=0, tiled=True)  53 us
    pallas_call x2, Pallas kernels, cached_attention(): pl.pallas_call(functools.partial(cached_kernel, scale), grid=(req_dev, po...  40.8 us
    all_to_all x2, starting transfers between devices, shards(): lax.all_to_all(outgoing, 'pool', split_axis=0, concat_axis=0, tiled=True)  21.8 us
    reduce_or x1, other arithmetic, shards(): jnp.any(row_ids[..., None] == own_rows[:, :, None, None, None, :], axis=-1)  20.4 us
    broadcast_in_dim x3, local copies, waits for them, and re-layouts, cached_attention(): valid = valid[..., None]  10.8 us
    dot_general x2, matrix products, shards(): jnp.einsum('rqh,hm->rqm', attn, w_out, preferred_element_type=jnp.float32)  10.5 us
    gather x2, local copies, waits for them, and re-layouts, shards(): outgoing = pool_kv[slot_ids[:, r]]  9.54 us
  transfers between devices with their start and end apart: 5, of which 5 were waited for; matrix products, arithmetic and copies ran while one was open for 30% of the time, Pallas kernels for 7%

profile of v6, /device:TPU:1, one launch (start us, length us, event | category | flops | bytes accessed | tf_op | source)
XLA Modules:
  0.0 298.6 jit_solution(1670803435679674758)
XLA Ops:
  12.5 4.8 %gather_fusion.1 = bf16[512,2,16,128]{3,2,1,0:T(8,128)(2,1)} fusion(bf16[256,2,16,128]{3,2,1,0:T(8,128)(2,1)} %bitcast.163, s32[1024]{0:T(1024)S(1)} %pad_clamp_fusion.2), kind=kCustom, calls=%fused_computation.1 | custom fusion | bytes 8390656 | tf_op jit(solution)/shard_map/gather | solution.py:306
  17.3 12.5 %all-to-all-start = ((bf16[32,4,4,1,2,16,128]{6,5,4,2,1,3,0:T(8,128)(2,1)}), bf16[32,4,4,1,2,16,128]{6,5,4,2,1,3,0:T(8,128)(2,1)}, u32[]{:S(2)}, u32[]{:S(2)}) async-start(bf16[32,4,4,1,2,16,128]{6,5,4,2,1,3,0:T(8,128)(2,1)} %bitcast.166), calls=%async_computation | async-start | bytes 8388608 | tf_op jit(solution)/shard_map/all_to_all | solution.py:309
  30.9 2.3 reduce_window_sum.23
  35.1 20.4 %compare_reduce_fusion = pred[2,4,32,4,16]{4,3,2,1,0:T(4,128)(4,1)S(1)} fusion(s32[2,4,104]{2,1,0:T(4,128)S(1)} %get-tuple-element.42, s32[2,4,32,4,16]{4,3,2,1,0:T(4,128)S(1)} %iota_add_fusion), kind=kLoop, calls=%fused_computation.11 | loop fusion | flops 3391488 | bytes 85248 | tf_op jit(solution)/shard_map/reduce_or | solution.py:288
  57.6 4.8 %gather_fusion.2 = bf16[512,2,16,128]{3,2,1,0:T(8,128)(2,1)} fusion(bf16[256,2,16,128]{3,2,1,0:T(8,128)(2,1)} %bitcast.164, s32[1024]{0:T(1024)S(1)} %pad_clamp_fusion.1), kind=kCustom, calls=%fused_computation.2 | custom fusion | bytes 8390656 | tf_op jit(solution)/shard_map/gather | solution.py:306
  66.1 5.3 %fusion = f32[2,4,104]{2,1,0:T(4,128)S(1)} fusion(bf16[2,4,104,5120]{3,2,1,0:T(8,128)(2,1)} %all-gather.2.cloned.1.call-done), kind=kLoop, calls=%fused_computation.6 | loop fusion | flops 12778688 | bytes 8523008 | tf_op jit(solution)/shard_map/reduce_sum | solution.py:253
  71.9 2.6 fusion.8
  74.6 2.0 fusion.31
  78.3 1.9 copy.177
  80.2 2.8 reshape.530
  82.9 2.3 exponential_reduce_fusion
  85.2 1.7 convolution_bitcast_fusion.2
  87.0 35.4 %all-to-all-done = bf16[32,4,4,1,2,16,128]{6,5,4,2,1,3,0:T(8,128)(2,1)} async-done(((bf16[32,4,4,1,2,16,128]{6,5,4,2,1,3,0:T(8,128)(2,1)}), bf16[32,4,4,1,2,16,128]{6,5,4,2,1,3,0:T(8,128)(2,1)}, u32[]{:S(2)}, u32[]{:S(2)}) %all-to-all-start) | async-done | bytes 4194336 | tf_op jit(solution)/shard_map/all_to_all | solution.py:309
  122.4 9.3 %all-to-all-start.1 = ((bf16[32,4,4,1,2,16,128]{6,5,4,2,1,3,0:T(8,128)(2,1)}), bf16[32,4,4,1,2,16,128]{6,5,4,2,1,3,0:T(8,128)(2,1)}, u32[]{:S(2)}, u32[]{:S(2)}) async-start(bf16[32,4,4,1,2,16,128]{6,5,4,2,1,3,0:T(8,128)(2,1)} %bitcast.165), calls=%async_computation.1 | async-start | bytes 8388608 | tf_op jit(solution)/shard_map/all_to_all | solution.py:309
  134.5 1.6 slice_bitcast_fusion.1
  136.2 4.6 %copy.188.valid_ref = f32[1,32,256,1]{3,2,1,0:T(8,128)} copy(f32[1,32,256,1]{1,2,3,0:T(8,128)S(1)} %get-tuple-element.52) | data formatting | bytes 65536 | tf_op jit(solution)/shard_map/broadcast_in_dim | solution.py:142
  141.3 20.4 %shard_map.109 = (f32[1,1,320]{2,1,0:T(1,128)}, f32[1,1,320]{2,1,0:T(1,128)}, f32[1,128,320]{2,1,0:T(8,128)}) custom-call(bf16[1,320,128]{2,1,0:T(8,128)(2,1)} %slice.117.q_ref, bf16[32,1,16,2,16,128]{5,4,3,2,1,0:T(8,128)(2,1)} %bitcast.54.kv_ref, f32[1,32,256,1]{3,2,1,0:T(8,128)} %copy.188.valid_ref, f32[1,8,128]{2,1,0:T(8,128)} %get-tuple-element.70.table_ref), custom_call_target="tpu_custom_call" | custom-call | tf_op jit(solution)/shard_map/pallas_call | solution.py:143
  165.1 5.3 %convolution_bitcast_fusion.1 = f32[1,64,5120]{2,1,0:T(8,128)} fusion(bf16[640,5120]{1,0:T(8,128)(2,1)} %param.21, bf16[8,8,5,128]{3,2,1,0:T(8,128)(2,1)S(1)} %bitcast.173), kind=kOutput, calls=%fused_computation.13 | convolution fusion | flops 419430400 | bytes 7946240 | tf_op jit(solution)/shard_map/rqh,hm->rqm/dot_general | solution.py:342
  173.2 4.6 %copy.197.valid_ref = f32[1,32,256,1]{3,2,1,0:T(8,128)} copy(f32[1,32,256,1]{1,2,3,0:T(8,128)S(1)} %copy-done.5) | data formatting | bytes 65536 | tf_op jit(solution)/shard_map/broadcast_in_dim | solution.py:142
  177.8 28.1 %reduce-scatter.3.cloned.1.call-done = f32[1,64,640]{2,1,0:T(8,128)} async-done(((f32[1,64,5120]{2,1,0:T(8,128)}), f32[1,64,640]{2,1,0:T(8,128)}) %reduce-scatter.3.cloned.1.call-update) | async-done | bytes 163856 | tf_op jit(solution)/shard_map/reduce_scatter | solution.py:344
  206.8 17.6 %all-to-all-done.1 = bf16[32,4,4,1,2,16,128]{6,5,4,2,1,3,0:T(8,128)(2,1)} async-done(((bf16[32,4,4,1,2,16,128]{6,5,4,2,1,3,0:T(8,128)(2,1)}), bf16[32,4,4,1,2,16,128]{6,5,4,2,1,3,0:T(8,128)(2,1)}, u32[]{:S(2)}, u32[]{:S(2)}) %all-to-all-start.1) | async-done | bytes 4194336 | tf_op jit(solution)/shard_map/all_to_all | solution.py:309
  224.4 20.4 %shard_map.110 = (f32[1,1,320]{2,1,0:T(1,128)}, f32[1,1,320]{2,1,0:T(1,128)}, f32[1,128,320]{2,1,0:T(8,128)}) custom-call(bf16[1,320,128]{2,1,0:T(8,128)(2,1)} %slice.128.q_ref, bf16[32,1,16,2,16,128]{5,4,3,2,1,0:T(8,128)(2,1)} %bitcast.65.kv_ref, f32[1,32,256,1]{3,2,1,0:T(8,128)} %copy.197.valid_ref, f32[1,8,128]{2,1,0:T(8,128)} %get-tuple-element.69.table_ref), custom_call_target="tpu_custom_call" | custom-call | tf_op jit(solution)/shard_map/pallas_call | solution.py:143
  250.6 5.2 %convolution_bitcast_fusion = f32[1,64,5120]{2,1,0:T(8,128)} fusion(bf16[640,5120]{1,0:T(8,128)(2,1)} %param.21, bf16[8,8,5,128]{3,2,1,0:T(8,128)(2,1)S(1)} %bitcast.174), kind=kOutput, calls=%fused_computation.12 | convolution fusion | flops 419430400 | bytes 7946240 | tf_op jit(solution)/shard_map/rqh,hm->rqm/dot_general | solution.py:342
  255.9 34.6 %reduce-scatter.5.cloned.1.call-done = f32[1,64,640]{2,1,0:T(8,128)} async-done(((f32[1,64,5120]{2,1,0:T(8,128)}), f32[1,64,640]{2,1,0:T(8,128)}) %reduce-scatter.5.cloned.1.call-update) | async-done | bytes 163856 | tf_op jit(solution)/shard_map/reduce_scatter | solution.py:344
  (131 shorter events, 34.5 us)
Async XLA Ops:
  6.5 64.9 %copy-start = (bf16[5120,2,1,128]{3,1,2,0:T(2,128)(2,1)S(1)}, bf16[5120,2,1,128]{3,1,2,0:T(2,128)(2,1)}, u32[]{:S(2)}) copy-start(bf16[5120,2,1,128]{3,1,2,0:T(2,128)(2,1)} %param.20) | copy-start | bytes 7864324
  6.5 59.5 %all-gather.2.cloned.1.call-start = ((), (), s32[]{:S(2)}) async-start(), calls=%async_computation.4 | async-start | bytes 9584640 | tf_op jit(solution)/shard_map/all_gather | solution.py:250
  17.3 12.5 %copy-start.12 = (s32[64,4]{0,1:T(4,128)S(1)}, s32[64,4]{0,1:T(4,128)}, u32[]{:S(2)}) copy-start(s32[64,4]{0,1:T(4,128)} %param.13) | copy-start | bytes 3076
  17.3 12.5 %copy-start.13 = (s32[64,4]{0,1:T(4,128)S(1)}, s32[64,4]{0,1:T(4,128)}, u32[]{:S(2)}) copy-start(s32[64,4]{0,1:T(4,128)} %param.14) | copy-start | bytes 3076
  17.3 12.7 %copy-start.7 = (bf16[2,64,5,128]{3,1,2,0:T(8,128)(2,1)S(1)}, bf16[2,64,5,128]{3,1,2,0:T(8,128)(2,1)}, u32[]{:S(2)}) copy-start(bf16[2,64,5,128]{3,1,2,0:T(8,128)(2,1)} %param.17) | copy-start | bytes 491524
  17.3 12.7 %copy-start.16 = (s32[64]{0:T(128)S(1)}, s32[64]{0:T(128)}, u32[]{:S(2)}) copy-start(s32[64]{0:T(128)} %param.16) | copy-start | bytes 772
  17.3 13.0 %copy-start.1 = (s32[64,128]{1,0:T(8,128)S(1)}, s32[64,128]{1,0:T(8,128)}, u32[]{:S(2)}) copy-start(s32[64,128]{1,0:T(8,128)} %param.12) | copy-start | bytes 98308
  17.3 105.1 %all-to-all-start = ((bf16[32,4,4,1,2,16,128]{6,5,4,2,1,3,0:T(8,128)(2,1)}), bf16[32,4,4,1,2,16,128]{6,5,4,2,1,3,0:T(8,128)(2,1)}, u32[]{:S(2)}, u32[]{:S(2)}) async-start(bf16[32,4,4,1,2,16,128]{6,5,4,2,1,3,0:T(8,128)(2,1)} %bitcast.166), calls=%async_computation | async-start | bytes 8388608 | tf_op jit(solution)/shard_map/all_to_all | solution.py:309
  30.1 32.7 %copy-start.14 = (s32[2]{0:T(128)}, s32[2]{0:T(128)S(1)}, u32[]{:S(2)}) copy-start(s32[2]{0:T(128)S(1)} %dynamic_slice.14) | copy-start | bytes 28
  57.6 5.5 %copy-start.6 = (bf16[2,64,2,1,128]{4,2,3,1,0:T(2,128)(2,1)S(1)}, bf16[2,64,2,1,128]{4,2,3,1,0:T(2,128)(2,1)}, u32[]{:S(2)}) copy-start(bf16[2,64,2,1,128]{4,2,3,1,0:T(2,128)(2,1)} %param.18) | copy-start | bytes 196612
  64.0 100.7 %copy-start.8 = (f32[2,64,5]{1,2,0:T(8,128)}, f32[2,64,5]{1,2,0:T(8,128)S(1)}, u32[]{:S(2)}) copy-start(f32[2,64,5]{1,2,0:T(8,128)S(1)} %fusion.27) | copy-start | bytes 7684
  66.1 5.8 %copy-start.3 = (bf16[2,4,104,5120]{3,2,1,0:T(8,128)(2,1)S(1)}, bf16[2,4,104,5120]{3,2,1,0:T(8,128)(2,1)}, u32[]{:S(2)}) copy-start(bf16[2,4,104,5120]{3,2,1,0:T(8,128)(2,1)} %all-gather.2.cloned.1.call-done) | copy-start | bytes 25559044
  77.2 1.1 copy-start.2
  122.3 10.9 %copy-start.15 = (s32[2]{0:T(128)S(1)}, s32[2]{0:T(128)}, u32[]{:S(2)}) copy-start(s32[2]{0:T(128)} %copy-done.14) | copy-start | bytes 28
  122.4 102.1 %all-to-all-start.1 = ((bf16[32,4,4,1,2,16,128]{6,5,4,2,1,3,0:T(8,128)(2,1)}), bf16[32,4,4,1,2,16,128]{6,5,4,2,1,3,0:T(8,128)(2,1)}, u32[]{:S(2)}, u32[]{:S(2)}) async-start(bf16[32,4,4,1,2,16,128]{6,5,4,2,1,3,0:T(8,128)(2,1)} %bitcast.165), calls=%async_computation.1 | async-start | bytes 8388608 | tf_op jit(solution)/shard_map/all_to_all | solution.py:309
  131.7 74.2 %reduce-scatter.3.cloned.1.call-start = ((), (), s32[]{:S(2)}) async-start(), calls=%async_computation.5 | async-start | bytes 1474560 | tf_op jit(solution)/shard_map/reduce_scatter | solution.py:344
  141.3 23.3 %copy-start.10 = (f32[2,64,5]{1,2,0:T(8,128)S(1)}, f32[2,64,5]{1,2,0:T(8,128)}, u32[]{:S(2)}) copy-start(f32[2,64,5]{1,2,0:T(8,128)} %exponential_reduce_fusion) | copy-start | bytes 7684
  141.3 23.4 %copy-start.4 = (f32[2,64,1,5,128]{4,1,3,0,2:T(8,128)S(1)}, f32[2,64,1,5,128]{4,1,3,0,2:T(8,128)}, u32[]{:S(2)}) copy-start(f32[2,64,1,5,128]{4,1,3,0,2:T(8,128)} %convolution_bitcast_fusion.3) | copy-start | bytes 983044
  165.0 8.2 %copy-start.5 = (f32[1,32,256,1]{1,2,3,0:T(8,128)S(1)}, f32[1,32,256,1]{1,2,3,0:T(8,128)}, u32[]{:S(2)}) copy-start(f32[1,32,256,1]{1,2,3,0:T(8,128)} %get-tuple-element.51) | copy-start | bytes 98308
  170.4 120.1 %reduce-scatter.5.cloned.1.call-start = ((), (), s32[]{:S(2)}) async-start(), calls=%async_computation.6 | async-start | bytes 1474560 | tf_op jit(solution)/shard_map/reduce_scatter | solution.py:344
  224.4 24.5 %copy-start.9 = (f32[2,64,5]{1,2,0:T(8,128)S(1)}, f32[2,64,5]{1,2,0:T(8,128)}, u32[]{:S(2)}) copy-start(f32[2,64,5]{1,2,0:T(8,128)} %copy-done.8) | copy-start | bytes 7684
  224.4 24.5 %copy-start.11 = (f32[2,64,5]{1,2,0:T(8,128)S(1)}, f32[2,64,5]{1,2,0:T(8,128)}, u32[]{:S(2)}) copy-start(f32[2,64,5]{1,2,0:T(8,128)} %exponential_reduce_fusion) | copy-start | bytes 7684
Sparse Core Ops, SparseCore 0:
  9.2 56.8 all-gather.1
  170.5 35.3 reduce-scatter.2
  256.0 34.4 reduce-scatter.4

commit v7 on v6

--- a/solution.py
+++ b/solution.py
@@ -340,9 +340,14 @@
             .reshape(1, qlen, heads * head_dim)
         )
         partial_out = jnp.einsum("rqh,hm->rqm", attn, w_out, preferred_element_type=jnp.float32)
-        outputs.append(
-            lax.psum_scatter(partial_out, "tp", scatter_dimension=2, tiled=True).astype(jnp.bfloat16)
-        )
+        if r < req_dev - 1:
+            reduced = lax.psum_scatter(partial_out, "tp", scatter_dimension=2, tiled=True)
+        else:
+            tp_count = lax.axis_size("tp")
+            pieces = partial_out.reshape(1, qlen, tp_count, -1).transpose(2, 0, 1, 3)
+            pieces = lax.all_to_all(pieces, "tp", split_axis=0, concat_axis=0, tiled=True)
+            reduced = jnp.sum(pieces, axis=0)
+        outputs.append(reduced.astype(jnp.bfloat16))
     return jnp.concatenate(outputs, axis=0)
 
 

time: 301 us -> 290 us (0.963)
  waiting for transfers between devices: 118 us -> 82.4 us
  blocking collectives: 0 us -> 27.1 us
  other arithmetic: 48.6 us -> 44.6 us
  local copies, waits for them, and re-layouts: 39.4 us -> 43.4 us
    reduce_scatter x2 -> x1, waiting for transfers between devices: 62.7 us -> 20 us  [shards(): lax.psum_scatter(partial_out, 'tp', scatter_dimension=2, tiled=True)]
    all_to_all x0 -> x1, blocking collectives: none -> 27.1 us  [shards(): lax.all_to_all(pieces, 'tp', split_axis=0, concat_axis=0, tiled=True)]
    dot_general x0 -> x1, local copies, waits for them, and re-layouts: none -> 9.49 us  [shards(): jnp.einsum('rqh,hm->rqm', attn, w_out, preferred_element_type=jnp.float32)]
    all_to_all x2, waiting for transfers between devices: 53 us -> 60.5 us  [shards(): lax.all_to_all(outgoing, 'pool', split_axis=0, concat_axis=0, tiled=True)]
  transfers between devices with their start and end apart: 5 -> 4, of which waited for: 5 -> 4; matrix products, arithmetic and copies ran while one was open for 30% -> 32% of each run, Pallas kernels for 7% -> 7%
where the time goes in v7:
time: 290 us; the launch traced here: 289 us
  waiting for transfers between devices  82.4 us (28%)
  other arithmetic  44.6 us (15%)
  local copies, waits for them, and re-layouts  43.4 us (15%)
  Pallas kernels  40.8 us (14%)
  blocking collectives  27.1 us (9%)
  starting transfers between devices  21.9 us (8%)
  matrix products  15.2 us (5%)
  between operations  14 us (5%)
    all_to_all x2, waiting for transfers between devices, shards(): lax.all_to_all(outgoing, 'pool', split_axis=0, concat_axis=0, tiled=True)  60.5 us
    pallas_call x2, Pallas kernels, cached_attention(): pl.pallas_call(functools.partial(cached_kernel, scale), grid=(req_dev, po...  40.8 us
    all_to_all x1, blocking collectives, shards(): lax.all_to_all(pieces, 'tp', split_axis=0, concat_axis=0, tiled=True)  27.1 us
    all_to_all x2, starting transfers between devices, shards(): lax.all_to_all(outgoing, 'pool', split_axis=0, concat_axis=0, tiled=True)  21.8 us
    reduce_or x1, other arithmetic, shards(): jnp.any(row_ids[..., None] == own_rows[:, :, None, None, None, :], axis=-1)  20.4 us
    reduce_scatter x1, waiting for transfers between devices, shards(): lax.psum_scatter(partial_out, 'tp', scatter_dimension=2, tiled=True)  20 us
    dot_general x2, matrix products, shards(): jnp.einsum('rqh,hm->rqm', attn, w_out, preferred_element_type=jnp.float32)  10.3 us
    gather x2, local copies, waits for them, and re-layouts, shards(): outgoing = pool_kv[slot_ids[:, r]]  9.54 us
  transfers between devices with their start and end apart: 4, of which 4 were waited for; matrix products, arithmetic and copies ran while one was open for 32% of the time, Pallas kernels for 7%

profile of v7, /device:TPU:1, one launch (start us, length us, event | category | flops | bytes accessed | tf_op | source)
XLA Modules:
  0.0 289.3 jit_solution(13023914357171107576)
XLA Ops:
  8.2 1.5 gather_fusion
  12.5 4.7 %gather_fusion.1 = bf16[512,2,16,128]{3,2,1,0:T(8,128)(2,1)} fusion(bf16[256,2,16,128]{3,2,1,0:T(8,128)(2,1)} %bitcast.170, s32[1024]{0:T(1024)S(1)} %pad_clamp_fusion.2), kind=kCustom, calls=%fused_computation.1 | custom fusion | bytes 8390656 | tf_op jit(solution)/shard_map/gather | solution.py:306
  17.3 12.5 %all-to-all-start = ((bf16[32,4,4,1,2,16,128]{6,5,4,2,1,3,0:T(8,128)(2,1)}), bf16[32,4,4,1,2,16,128]{6,5,4,2,1,3,0:T(8,128)(2,1)}, u32[]{:S(2)}, u32[]{:S(2)}) async-start(bf16[32,4,4,1,2,16,128]{6,5,4,2,1,3,0:T(8,128)(2,1)} %bitcast.174), calls=%async_computation | async-start | bytes 8388608 | tf_op jit(solution)/shard_map/all_to_all | solution.py:309
  30.9 2.3 reduce_window_sum.23
  35.1 20.4 %compare_reduce_fusion = pred[2,4,32,4,16]{4,3,2,1,0:T(4,128)(4,1)S(1)} fusion(s32[2,4,104]{2,1,0:T(4,128)S(1)} %get-tuple-element.42, s32[2,4,32,4,16]{4,3,2,1,0:T(4,128)S(1)} %iota_add_fusion), kind=kLoop, calls=%fused_computation.11 | loop fusion | flops 3391488 | bytes 85248 | tf_op jit(solution)/shard_map/reduce_or | solution.py:288
  57.6 4.8 %gather_fusion.2 = bf16[512,2,16,128]{3,2,1,0:T(8,128)(2,1)} fusion(bf16[256,2,16,128]{3,2,1,0:T(8,128)(2,1)} %bitcast.171, s32[1024]{0:T(1024)S(1)} %pad_clamp_fusion.1), kind=kCustom, calls=%fused_computation.2 | custom fusion | bytes 8390656 | tf_op jit(solution)/shard_map/gather | solution.py:306
  66.1 5.3 %fusion = f32[2,4,104]{2,1,0:T(4,128)S(1)} fusion(bf16[2,4,104,5120]{3,2,1,0:T(8,128)(2,1)} %all-gather.2.cloned.1.call-done), kind=kLoop, calls=%fused_computation.6 | loop fusion | flops 12778688 | bytes 8523008 | tf_op jit(solution)/shard_map/reduce_sum | solution.py:253
  71.9 2.6 fusion.8
  74.6 2.0 fusion.31
  77.2 1.9 copy.182
  79.1 1.9 reshape.548
  81.8 40.5 %all-to-all-done = bf16[32,4,4,1,2,16,128]{6,5,4,2,1,3,0:T(8,128)(2,1)} async-done(((bf16[32,4,4,1,2,16,128]{6,5,4,2,1,3,0:T(8,128)(2,1)}), bf16[32,4,4,1,2,16,128]{6,5,4,2,1,3,0:T(8,128)(2,1)}, u32[]{:S(2)}, u32[]{:S(2)}) %all-to-all-start) | async-done | bytes 4194336 | tf_op jit(solution)/shard_map/all_to_all | solution.py:309
  122.3 9.3 %all-to-all-start.1 = ((bf16[32,4,4,1,2,16,128]{6,5,4,2,1,3,0:T(8,128)(2,1)}), bf16[32,4,4,1,2,16,128]{6,5,4,2,1,3,0:T(8,128)(2,1)}, u32[]{:S(2)}, u32[]{:S(2)}) async-start(bf16[32,4,4,1,2,16,128]{6,5,4,2,1,3,0:T(8,128)(2,1)} %bitcast.173), calls=%async_computation.1 | async-start | bytes 8388608 | tf_op jit(solution)/shard_map/all_to_all | solution.py:309
  133.9 4.6 %copy.193.valid_ref = f32[1,32,256,1]{3,2,1,0:T(8,128)} copy(f32[1,32,256,1]{1,2,3,0:T(8,128)S(1)} %get-tuple-element.52) | data formatting | bytes 65536 | tf_op jit(solution)/shard_map/broadcast_in_dim | solution.py:142
  139.1 20.4 %shard_map.109 = (f32[1,1,320]{2,1,0:T(1,128)}, f32[1,1,320]{2,1,0:T(1,128)}, f32[1,128,320]{2,1,0:T(8,128)}) custom-call(bf16[1,320,128]{2,1,0:T(8,128)(2,1)} %slice.117.q_ref, bf16[32,1,16,2,16,128]{5,4,3,2,1,0:T(8,128)(2,1)} %bitcast.54.kv_ref, f32[1,32,256,1]{3,2,1,0:T(8,128)} %copy.193.valid_ref, f32[1,8,128]{2,1,0:T(8,128)} %get-tuple-element.70.table_ref), custom_call_target="tpu_custom_call" | custom-call | tf_op jit(solution)/shard_map/pallas_call | solution.py:143
  162.8 5.2 %convolution_bitcast_fusion = f32[1,64,5120]{2,1,0:T(8,128)} fusion(bf16[640,5120]{1,0:T(8,128)(2,1)} %param.21, bf16[8,8,5,128]{3,2,1,0:T(8,128)(2,1)S(1)} %bitcast.181), kind=kOutput, calls=%fused_computation.12 | convolution fusion | flops 419430400 | bytes 7946240 | tf_op jit(solution)/shard_map/rqh,hm->rqm/dot_general | solution.py:342
  168.8 9.5 %copy.225 = bf16[5120,640]{1,0:T(8,128)(2,1)} copy(bf16[5120,640]{0,1:T(8,128)(2,1)} %bitcast.169) | data formatting | bytes 13107200 | tf_op jit(solution)/shard_map/rqh,hm->rqm/dot_general | solution.py:342
  178.9 4.6 %copy.202.valid_ref = f32[1,32,256,1]{3,2,1,0:T(8,128)} copy(f32[1,32,256,1]{1,2,3,0:T(8,128)S(1)} %get-tuple-element.51) | data formatting | bytes 65536 | tf_op jit(solution)/shard_map/broadcast_in_dim | solution.py:142
  183.5 20.0 %reduce-scatter.2.cloned.1.call-done = f32[1,64,640]{2,1,0:T(8,128)} async-done(((f32[1,64,5120]{2,1,0:T(8,128)}), f32[1,64,640]{2,1,0:T(8,128)}) %reduce-scatter.2.cloned.1.call-update) | async-done | bytes 163856 | tf_op jit(solution)/shard_map/reduce_scatter | solution.py:344
  204.4 20.0 %all-to-all-done.1 = bf16[32,4,4,1,2,16,128]{6,5,4,2,1,3,0:T(8,128)(2,1)} async-done(((bf16[32,4,4,1,2,16,128]{6,5,4,2,1,3,0:T(8,128)(2,1)}), bf16[32,4,4,1,2,16,128]{6,5,4,2,1,3,0:T(8,128)(2,1)}, u32[]{:S(2)}, u32[]{:S(2)}) %all-to-all-start.1) | async-done | bytes 4194336 | tf_op jit(solution)/shard_map/all_to_all | solution.py:309
  224.4 20.4 %shard_map.110 = (f32[1,1,320]{2,1,0:T(1,128)}, f32[1,1,320]{2,1,0:T(1,128)}, f32[1,128,320]{2,1,0:T(8,128)}) custom-call(bf16[1,320,128]{2,1,0:T(8,128)(2,1)} %slice.128.q_ref, bf16[32,1,16,2,16,128]{5,4,3,2,1,0:T(8,128)(2,1)} %bitcast.65.kv_ref, f32[1,32,256,1]{3,2,1,0:T(8,128)} %copy.202.valid_ref, f32[1,8,128]{2,1,0:T(8,128)} %get-tuple-element.69.table_ref), custom_call_target="tpu_custom_call" | custom-call | tf_op jit(solution)/shard_map/pallas_call | solution.py:143
  248.2 5.1 %convolution_bitcast_fusion.1 = f32[8,1,64,640]{3,2,1,0:T(8,128)S(1)} fusion(bf16[64,640,1]{1,0,2:T(8,128)(2,1)S(1)} %reshape.615, bf16[8,640,640]{2,1,0:T(8,128)(2,1)} %bitcast.172), kind=kOutput, calls=%fused_computation.16 | convolution fusion | flops 419430400 | bytes 7946240 | tf_op jit(solution)/shard_map/rqh,hm->rqm/dot_general | solution.py:342
  253.3 27.1 %all_to_all.15 = f32[8,1,64,640]{3,2,1,0:T(8,128)} all-to-all(f32[8,1,64,640]{3,2,1,0:T(8,128)S(1)} %convolution_bitcast_fusion.1), channel_id=1, replica_groups=mesh['pool'=32,'tp'=8] {'tp'}, dimensions={0} | all-to-all | bytes 2621440 | tf_op jit(solution)/shard_map/all_to_all | solution.py:348
  280.4 1.4 reduce_sum.65
  (127 shorter events, 27.3 us)
Async XLA Ops:
  6.5 64.9 %copy-start = (bf16[5120,2,1,128]{3,1,2,0:T(2,128)(2,1)S(1)}, bf16[5120,2,1,128]{3,1,2,0:T(2,128)(2,1)}, u32[]{:S(2)}) copy-start(bf16[5120,2,1,128]{3,1,2,0:T(2,128)(2,1)} %param.20) | copy-start | bytes 7864324
  6.5 59.5 %all-gather.2.cloned.1.call-start = ((), (), s32[]{:S(2)}) async-start(), calls=%async_computation.4 | async-start | bytes 9584640 | tf_op jit(solution)/shard_map/all_gather | solution.py:250
  17.3 12.5 %copy-start.10 = (s32[64,4]{0,1:T(4,128)S(1)}, s32[64,4]{0,1:T(4,128)}, u32[]{:S(2)}) copy-start(s32[64,4]{0,1:T(4,128)} %param.13) | copy-start | bytes 3076
  17.3 12.5 %copy-start.11 = (s32[64,4]{0,1:T(4,128)S(1)}, s32[64,4]{0,1:T(4,128)}, u32[]{:S(2)}) copy-start(s32[64,4]{0,1:T(4,128)} %param.14) | copy-start | bytes 3076
  17.3 12.7 %copy-start.7 = (bf16[2,64,5,128]{3,1,2,0:T(8,128)(2,1)S(1)}, bf16[2,64,5,128]{3,1,2,0:T(8,128)(2,1)}, u32[]{:S(2)}) copy-start(bf16[2,64,5,128]{3,1,2,0:T(8,128)(2,1)} %param.17) | copy-start | bytes 491524
  17.3 12.7 %copy-start.14 = (s32[64]{0:T(128)S(1)}, s32[64]{0:T(128)}, u32[]{:S(2)}) copy-start(s32[64]{0:T(128)} %param.16) | copy-start | bytes 772
  17.3 13.0 %copy-start.2 = (s32[64,128]{1,0:T(8,128)S(1)}, s32[64,128]{1,0:T(8,128)}, u32[]{:S(2)}) copy-start(s32[64,128]{1,0:T(8,128)} %param.12) | copy-start | bytes 98308
  17.3 105.1 %all-to-all-start = ((bf16[32,4,4,1,2,16,128]{6,5,4,2,1,3,0:T(8,128)(2,1)}), bf16[32,4,4,1,2,16,128]{6,5,4,2,1,3,0:T(8,128)(2,1)}, u32[]{:S(2)}, u32[]{:S(2)}) async-start(bf16[32,4,4,1,2,16,128]{6,5,4,2,1,3,0:T(8,128)(2,1)} %bitcast.174), calls=%async_computation | async-start | bytes 8388608 | tf_op jit(solution)/shard_map/all_to_all | solution.py:309
  30.1 32.7 %copy-start.12 = (s32[2]{0:T(128)}, s32[2]{0:T(128)S(1)}, u32[]{:S(2)}) copy-start(s32[2]{0:T(128)S(1)} %dynamic_slice.14) | copy-start | bytes 28
  57.6 5.5 %copy-start.6 = (bf16[2,64,2,1,128]{4,2,3,1,0:T(2,128)(2,1)S(1)}, bf16[2,64,2,1,128]{4,2,3,1,0:T(2,128)(2,1)}, u32[]{:S(2)}) copy-start(bf16[2,64,2,1,128]{4,2,3,1,0:T(2,128)(2,1)} %param.18) | copy-start | bytes 196612
  66.1 5.8 %copy-start.3 = (bf16[2,4,104,5120]{3,2,1,0:T(8,128)(2,1)S(1)}, bf16[2,4,104,5120]{3,2,1,0:T(8,128)(2,1)}, u32[]{:S(2)}) copy-start(bf16[2,4,104,5120]{3,2,1,0:T(8,128)(2,1)} %all-gather.2.cloned.1.call-done) | copy-start | bytes 25559044
  81.4 81.0 %copy-start.8 = (f32[2,64,5]{1,2,0:T(8,128)}, f32[2,64,5]{1,2,0:T(8,128)S(1)}, u32[]{:S(2)}) copy-start(f32[2,64,5]{1,2,0:T(8,128)S(1)} %exponential_reduce_fusion) | copy-start | bytes 7684
  122.3 10.3 %copy-start.13 = (s32[2]{0:T(128)S(1)}, s32[2]{0:T(128)}, u32[]{:S(2)}) copy-start(s32[2]{0:T(128)} %copy-done.12) | copy-start | bytes 28
  122.3 11.5 %copy-start.5 = (f32[2,32,4,4,16]{1,4,3,2,0:T(8,128)S(1)}, f32[2,32,4,4,16]{1,4,3,2,0:T(8,128)}, u32[]{:S(2)}) copy-start(f32[2,32,4,4,16]{1,4,3,2,0:T(8,128)} %copy.188) | copy-start | bytes 196612
  122.3 102.1 %all-to-all-start.1 = ((bf16[32,4,4,1,2,16,128]{6,5,4,2,1,3,0:T(8,128)(2,1)}), bf16[32,4,4,1,2,16,128]{6,5,4,2,1,3,0:T(8,128)(2,1)}, u32[]{:S(2)}, u32[]{:S(2)}) async-start(bf16[32,4,4,1,2,16,128]{6,5,4,2,1,3,0:T(8,128)(2,1)} %bitcast.173), calls=%async_computation.1 | async-start | bytes 8388608 | tf_op jit(solution)/shard_map/all_to_all | solution.py:309
  131.7 71.8 %reduce-scatter.2.cloned.1.call-start = ((), (), s32[]{:S(2)}) async-start(), calls=%async_computation.5 | async-start | bytes 1474560 | tf_op jit(solution)/shard_map/reduce_scatter | solution.py:344
  139.1 23.3 %copy-start.4 = (f32[2,64,1,5,128]{4,1,3,0,2:T(8,128)S(1)}, f32[2,64,1,5,128]{4,1,3,0,2:T(8,128)}, u32[]{:S(2)}) copy-start(f32[2,64,1,5,128]{4,1,3,0,2:T(8,128)} %convolution_bitcast_fusion.3) | copy-start | bytes 983044
  224.4 23.2 %copy-start.9 = (f32[2,64,5]{1,2,0:T(8,128)S(1)}, f32[2,64,5]{1,2,0:T(8,128)}, u32[]{:S(2)}) copy-start(f32[2,64,5]{1,2,0:T(8,128)} %copy-done.8) | copy-start | bytes 7684
  248.2 34.3 %copy-start.1 = (bf16[5120,2,1,128]{3,1,2,0:T(2,128)(2,1)S(1)}, bf16[5120,2,1,128]{3,1,2,0:T(2,128)(2,1)}, u32[]{:S(2)}) copy-start(bf16[5120,2,1,128]{3,1,2,0:T(2,128)(2,1)} %param.20) | copy-start | bytes 7864324
Sparse Core Ops, SparseCore 0:
  9.2 56.8 all-gather.1
  168.1 35.3 reduce-scatter.1

commit v8 on v7

--- a/solution.py
+++ b/solution.py
@@ -345,8 +345,10 @@
         else:
             tp_count = lax.axis_size("tp")
             pieces = partial_out.reshape(1, qlen, tp_count, -1).transpose(2, 0, 1, 3)
-            pieces = lax.all_to_all(pieces, "tp", split_axis=0, concat_axis=0, tiled=True)
-            reduced = jnp.sum(pieces, axis=0)
+            pieces = lax.all_to_all(
+                pieces.astype(jnp.bfloat16), "tp", split_axis=0, concat_axis=0, tiled=True
+            )
+            reduced = jnp.sum(pieces.astype(jnp.float32), axis=0)
         outputs.append(reduced.astype(jnp.bfloat16))
     return jnp.concatenate(outputs, axis=0)
 

time: 290 us -> 282 us (0.972)
  blocking collectives: 27.1 us -> 20.2 us
    all_to_all x1, blocking collectives: 27.1 us -> 20.2 us  [shards(): lax.all_to_all(pieces.astype(jnp.bfloat16), 'tp', split_axis=0, concat_ax...]
  transfers between devices with their start and end apart: 4 -> 4, of which waited for: 4 -> 4; matrix products, arithmetic and copies ran while one was open for 32% -> 33% of each run, Pallas kernels for 7% -> 7%
where the time goes in v8:
time: 282 us; the launch traced here: 281 us
  waiting for transfers between devices  82.5 us (29%)
  local copies, waits for them, and re-layouts  43.4 us (15%)
  other arithmetic  43.3 us (15%)
  Pallas kernels  40.8 us (14%)
  starting transfers between devices  21.9 us (8%)
  blocking collectives  20.2 us (7%)
  matrix products  15.2 us (5%)
  between operations  13.9 us (5%)
    all_to_all x2, waiting for transfers between devices, shards(): lax.all_to_all(outgoing, 'pool', split_axis=0, concat_axis=0, tiled=True)  60.5 us
    pallas_call x2, Pallas kernels, cached_attention(): pl.pallas_call(functools.partial(cached_kernel, scale), grid=(req_dev, po...  40.8 us
    all_to_all x2, starting transfers between devices, shards(): lax.all_to_all(outgoing, 'pool', split_axis=0, concat_axis=0, tiled=True)  21.8 us
    reduce_or x1, other arithmetic, shards(): jnp.any(row_ids[..., None] == own_rows[:, :, None, None, None, :], axis=-1)  20.4 us
    all_to_all x1, blocking collectives, shards(): lax.all_to_all(pieces.astype(jnp.bfloat16), 'tp', split_axis=0, concat_ax...  20.2 us
    reduce_scatter x1, waiting for transfers between devices, shards(): lax.psum_scatter(partial_out, 'tp', scatter_dimension=2, tiled=True)  20.1 us
    dot_general x2, matrix products, shards(): jnp.einsum('rqh,hm->rqm', attn, w_out, preferred_element_type=jnp.float32)  10.3 us
    gather x2, local copies, waits for them, and re-layouts, shards(): outgoing = pool_kv[slot_ids[:, r]]  9.54 us
  transfers between devices with their start and end apart: 4, of which 4 were waited for; matrix products, arithmetic and copies ran while one was open for 33% of the time, Pallas kernels for 7%

profile of v8, /device:TPU:1, one launch (start us, length us, event | category | flops | bytes accessed | tf_op | source)
XLA Modules:
  0.0 281.1 jit_solution(13091247990704507577)
XLA Ops:
  8.2 1.5 gather_fusion
  9.8 1.2 reduce_window_sum.22
  12.5 4.7 %gather_fusion.1 = bf16[512,2,16,128]{3,2,1,0:T(8,128)(2,1)} fusion(bf16[256,2,16,128]{3,2,1,0:T(8,128)(2,1)} %bitcast.168, s32[1024]{0:T(1024)S(1)} %pad_clamp_fusion.2), kind=kCustom, calls=%fused_computation.1 | custom fusion | bytes 8390656 | tf_op jit(solution)/shard_map/gather | solution.py:306
  17.3 12.5 %all-to-all-start = ((bf16[32,4,4,1,2,16,128]{6,5,4,2,1,3,0:T(8,128)(2,1)}), bf16[32,4,4,1,2,16,128]{6,5,4,2,1,3,0:T(8,128)(2,1)}, u32[]{:S(2)}, u32[]{:S(2)}) async-start(bf16[32,4,4,1,2,16,128]{6,5,4,2,1,3,0:T(8,128)(2,1)} %bitcast.172), calls=%async_computation | async-start | bytes 8388608 | tf_op jit(solution)/shard_map/all_to_all | solution.py:309
  30.9 2.3 reduce_window_sum.23
  35.1 20.4 %compare_reduce_fusion = pred[2,4,32,4,16]{4,3,2,1,0:T(4,128)(4,1)S(1)} fusion(s32[2,4,104]{2,1,0:T(4,128)S(1)} %get-tuple-element.42, s32[2,4,32,4,16]{4,3,2,1,0:T(4,128)S(1)} %iota_add_fusion), kind=kLoop, calls=%fused_computation.11 | loop fusion | flops 3391488 | bytes 85248 | tf_op jit(solution)/shard_map/reduce_or | solution.py:288
  57.6 4.8 %gather_fusion.2 = bf16[512,2,16,128]{3,2,1,0:T(8,128)(2,1)} fusion(bf16[256,2,16,128]{3,2,1,0:T(8,128)(2,1)} %bitcast.169, s32[1024]{0:T(1024)S(1)} %pad_clamp_fusion.1), kind=kCustom, calls=%fused_computation.2 | custom fusion | bytes 8390656 | tf_op jit(solution)/shard_map/gather | solution.py:306
  66.1 5.3 %fusion = f32[2,4,104]{2,1,0:T(4,128)S(1)} fusion(bf16[2,4,104,5120]{3,2,1,0:T(8,128)(2,1)} %all-gather.2.cloned.1.call-done), kind=kLoop, calls=%fused_computation.6 | loop fusion | flops 12778688 | bytes 8523008 | tf_op jit(solution)/shard_map/reduce_sum | solution.py:253
  71.9 2.6 fusion.8
  74.6 2.0 fusion.32
  77.2 1.9 copy.182
  79.1 1.9 reshape.540
  81.8 40.5 %all-to-all-done = bf16[32,4,4,1,2,16,128]{6,5,4,2,1,3,0:T(8,128)(2,1)} async-done(((bf16[32,4,4,1,2,16,128]{6,5,4,2,1,3,0:T(8,128)(2,1)}), bf16[32,4,4,1,2,16,128]{6,5,4,2,1,3,0:T(8,128)(2,1)}, u32[]{:S(2)}, u32[]{:S(2)}) %all-to-all-start) | async-done | bytes 4194336 | tf_op jit(solution)/shard_map/all_to_all | solution.py:309
  122.3 9.3 %all-to-all-start.1 = ((bf16[32,4,4,1,2,16,128]{6,5,4,2,1,3,0:T(8,128)(2,1)}), bf16[32,4,4,1,2,16,128]{6,5,4,2,1,3,0:T(8,128)(2,1)}, u32[]{:S(2)}, u32[]{:S(2)}) async-start(bf16[32,4,4,1,2,16,128]{6,5,4,2,1,3,0:T(8,128)(2,1)} %bitcast.171), calls=%async_computation.1 | async-start | bytes 8388608 | tf_op jit(solution)/shard_map/all_to_all | solution.py:309
  133.9 4.6 %copy.193.valid_ref = f32[1,32,256,1]{3,2,1,0:T(8,128)} copy(f32[1,32,256,1]{1,2,3,0:T(8,128)S(1)} %get-tuple-element.52) | data formatting | bytes 65536 | tf_op jit(solution)/shard_map/broadcast_in_dim | solution.py:142
  139.1 20.4 %shard_map.109 = (f32[1,1,320]{2,1,0:T(1,128)}, f32[1,1,320]{2,1,0:T(1,128)}, f32[1,128,320]{2,1,0:T(8,128)}) custom-call(bf16[1,320,128]{2,1,0:T(8,128)(2,1)} %slice.117.q_ref, bf16[32,1,16,2,16,128]{5,4,3,2,1,0:T(8,128)(2,1)} %bitcast.54.kv_ref, f32[1,32,256,1]{3,2,1,0:T(8,128)} %copy.193.valid_ref, f32[1,8,128]{2,1,0:T(8,128)} %get-tuple-element.70.table_ref), custom_call_target="tpu_custom_call" | custom-call | tf_op jit(solution)/shard_map/pallas_call | solution.py:143
  162.8 5.2 %convolution_bitcast_fusion = f32[1,64,5120]{2,1,0:T(8,128)} fusion(bf16[640,5120]{1,0:T(8,128)(2,1)} %param.21, bf16[8,8,5,128]{3,2,1,0:T(8,128)(2,1)S(1)} %bitcast.179), kind=kOutput, calls=%fused_computation.12 | convolution fusion | flops 419430400 | bytes 7946240 | tf_op jit(solution)/shard_map/rqh,hm->rqm/dot_general | solution.py:342
  168.8 9.5 %copy.225 = bf16[5120,640]{1,0:T(8,128)(2,1)} copy(bf16[5120,640]{0,1:T(8,128)(2,1)} %bitcast.167) | data formatting | bytes 13107200 | tf_op jit(solution)/shard_map/rqh,hm->rqm/dot_general | solution.py:342
  178.8 4.6 %copy.202.valid_ref = f32[1,32,256,1]{3,2,1,0:T(8,128)} copy(f32[1,32,256,1]{1,2,3,0:T(8,128)S(1)} %get-tuple-element.51) | data formatting | bytes 65536 | tf_op jit(solution)/shard_map/broadcast_in_dim | solution.py:142
  183.4 20.1 %reduce-scatter.2.cloned.1.call-done = f32[1,64,640]{2,1,0:T(8,128)} async-done(((f32[1,64,5120]{2,1,0:T(8,128)}), f32[1,64,640]{2,1,0:T(8,128)}) %reduce-scatter.2.cloned.1.call-update) | async-done | bytes 163856 | tf_op jit(solution)/shard_map/reduce_scatter | solution.py:344
  204.4 20.0 %all-to-all-done.1 = bf16[32,4,4,1,2,16,128]{6,5,4,2,1,3,0:T(8,128)(2,1)} async-done(((bf16[32,4,4,1,2,16,128]{6,5,4,2,1,3,0:T(8,128)(2,1)}), bf16[32,4,4,1,2,16,128]{6,5,4,2,1,3,0:T(8,128)(2,1)}, u32[]{:S(2)}, u32[]{:S(2)}) %all-to-all-start.1) | async-done | bytes 4194336 | tf_op jit(solution)/shard_map/all_to_all | solution.py:309
  224.4 20.4 %shard_map.110 = (f32[1,1,320]{2,1,0:T(1,128)}, f32[1,1,320]{2,1,0:T(1,128)}, f32[1,128,320]{2,1,0:T(8,128)}) custom-call(bf16[1,320,128]{2,1,0:T(8,128)(2,1)} %slice.128.q_ref, bf16[32,1,16,2,16,128]{5,4,3,2,1,0:T(8,128)(2,1)} %bitcast.65.kv_ref, f32[1,32,256,1]{3,2,1,0:T(8,128)} %copy.202.valid_ref, f32[1,8,128]{2,1,0:T(8,128)} %get-tuple-element.69.table_ref), custom_call_target="tpu_custom_call" | custom-call | tf_op jit(solution)/shard_map/pallas_call | solution.py:143
  248.2 5.1 %fusion.13 = bf16[8,1,64,640]{3,2,1,0:T(8,128)(2,1)S(1)} fusion(bf16[64,640,1]{1,0,2:T(8,128)(2,1)S(1)} %reshape.607, bf16[8,640,640]{2,1,0:T(8,128)(2,1)} %bitcast.170), kind=kOutput, calls=%fused_computation.20 | convolution fusion | flops 419758080 | bytes 7290880 | tf_op jit(solution)/shard_map/rqh,hm->rqm/dot_general | solution.py:342
  253.3 20.2 %all_to_all.15 = bf16[8,1,64,640]{3,2,1,0:T(8,128)(2,1)S(1)} all-to-all(bf16[8,1,64,640]{3,2,1,0:T(8,128)(2,1)S(1)} %fusion.13), channel_id=1, replica_groups=mesh['pool'=32,'tp'=8] {'tp'}, dimensions={0} | all-to-all | bytes 1310720 | tf_op jit(solution)/shard_map/all_to_all | solution.py:348
  (123 shorter events, 26.1 us)
Async XLA Ops:
  6.5 64.9 %copy-start = (bf16[5120,2,1,128]{3,1,2,0:T(2,128)(2,1)S(1)}, bf16[5120,2,1,128]{3,1,2,0:T(2,128)(2,1)}, u32[]{:S(2)}) copy-start(bf16[5120,2,1,128]{3,1,2,0:T(2,128)(2,1)} %param.20) | copy-start | bytes 7864324
  6.5 59.5 %all-gather.2.cloned.1.call-start = ((), (), s32[]{:S(2)}) async-start(), calls=%async_computation.4 | async-start | bytes 9584640 | tf_op jit(solution)/shard_map/all_gather | solution.py:250
  17.3 12.5 %copy-start.8 = (s32[64,4]{0,1:T(4,128)S(1)}, s32[64,4]{0,1:T(4,128)}, u32[]{:S(2)}) copy-start(s32[64,4]{0,1:T(4,128)} %param.13) | copy-start | bytes 3076
  17.3 12.5 %copy-start.9 = (s32[64,4]{0,1:T(4,128)S(1)}, s32[64,4]{0,1:T(4,128)}, u32[]{:S(2)}) copy-start(s32[64,4]{0,1:T(4,128)} %param.14) | copy-start | bytes 3076
  17.3 12.7 %copy-start.7 = (bf16[2,64,5,128]{3,1,2,0:T(8,128)(2,1)S(1)}, bf16[2,64,5,128]{3,1,2,0:T(8,128)(2,1)}, u32[]{:S(2)}) copy-start(bf16[2,64,5,128]{3,1,2,0:T(8,128)(2,1)} %param.17) | copy-start | bytes 491524
  17.3 12.7 %copy-start.12 = (s32[64]{0:T(128)S(1)}, s32[64]{0:T(128)}, u32[]{:S(2)}) copy-start(s32[64]{0:T(128)} %param.16) | copy-start | bytes 772
  17.3 13.0 %copy-start.2 = (s32[64,128]{1,0:T(8,128)S(1)}, s32[64,128]{1,0:T(8,128)}, u32[]{:S(2)}) copy-start(s32[64,128]{1,0:T(8,128)} %param.12) | copy-start | bytes 98308
  17.3 105.1 %all-to-all-start = ((bf16[32,4,4,1,2,16,128]{6,5,4,2,1,3,0:T(8,128)(2,1)}), bf16[32,4,4,1,2,16,128]{6,5,4,2,1,3,0:T(8,128)(2,1)}, u32[]{:S(2)}, u32[]{:S(2)}) async-start(bf16[32,4,4,1,2,16,128]{6,5,4,2,1,3,0:T(8,128)(2,1)} %bitcast.172), calls=%async_computation | async-start | bytes 8388608 | tf_op jit(solution)/shard_map/all_to_all | solution.py:309
  30.1 32.7 %copy-start.10 = (s32[2]{0:T(128)}, s32[2]{0:T(128)S(1)}, u32[]{:S(2)}) copy-start(s32[2]{0:T(128)S(1)} %dynamic_slice.14) | copy-start | bytes 28
  57.6 5.5 %copy-start.6 = (bf16[2,64,2,1,128]{4,2,3,1,0:T(2,128)(2,1)S(1)}, bf16[2,64,2,1,128]{4,2,3,1,0:T(2,128)(2,1)}, u32[]{:S(2)}) copy-start(bf16[2,64,2,1,128]{4,2,3,1,0:T(2,128)(2,1)} %param.18) | copy-start | bytes 196612
  66.1 5.8 %copy-start.3 = (bf16[2,4,104,5120]{3,2,1,0:T(8,128)(2,1)S(1)}, bf16[2,4,104,5120]{3,2,1,0:T(8,128)(2,1)}, u32[]{:S(2)}) copy-start(bf16[2,4,104,5120]{3,2,1,0:T(8,128)(2,1)} %all-gather.2.cloned.1.call-done) | copy-start | bytes 25559044
  122.3 10.3 %copy-start.11 = (s32[2]{0:T(128)S(1)}, s32[2]{0:T(128)}, u32[]{:S(2)}) copy-start(s32[2]{0:T(128)} %copy-done.10) | copy-start | bytes 28
  122.3 11.5 %copy-start.5 = (f32[2,32,4,4,16]{1,4,3,2,0:T(8,128)S(1)}, f32[2,32,4,4,16]{1,4,3,2,0:T(8,128)}, u32[]{:S(2)}) copy-start(f32[2,32,4,4,16]{1,4,3,2,0:T(8,128)} %copy.188) | copy-start | bytes 196612
  122.3 102.1 %all-to-all-start.1 = ((bf16[32,4,4,1,2,16,128]{6,5,4,2,1,3,0:T(8,128)(2,1)}), bf16[32,4,4,1,2,16,128]{6,5,4,2,1,3,0:T(8,128)(2,1)}, u32[]{:S(2)}, u32[]{:S(2)}) async-start(bf16[32,4,4,1,2,16,128]{6,5,4,2,1,3,0:T(8,128)(2,1)} %bitcast.171), calls=%async_computation.1 | async-start | bytes 8388608 | tf_op jit(solution)/shard_map/all_to_all | solution.py:309
  131.7 71.8 %reduce-scatter.2.cloned.1.call-start = ((), (), s32[]{:S(2)}) async-start(), calls=%async_computation.5 | async-start | bytes 1474560 | tf_op jit(solution)/shard_map/reduce_scatter | solution.py:344
  139.1 23.3 %copy-start.4 = (f32[2,64,1,5,128]{4,1,3,0,2:T(8,128)S(1)}, f32[2,64,1,5,128]{4,1,3,0,2:T(8,128)}, u32[]{:S(2)}) copy-start(f32[2,64,1,5,128]{4,1,3,0,2:T(8,128)} %convolution_bitcast_fusion.2) | copy-start | bytes 983044
  248.1 26.1 %copy-start.1 = (bf16[5120,2,1,128]{3,1,2,0:T(2,128)(2,1)S(1)}, bf16[5120,2,1,128]{3,1,2,0:T(2,128)(2,1)}, u32[]{:S(2)}) copy-start(bf16[5120,2,1,128]{3,1,2,0:T(2,128)(2,1)} %param.20) | copy-start | bytes 7864324
Sparse Core Ops, SparseCore 0:
  9.2 56.8 all-gather.1
  168.1 35.3 reduce-scatter.1

commit v9 on v6

--- a/solution.py
+++ b/solution.py
@@ -211,12 +211,26 @@
         jnp.bfloat16
     )
     own_values = question_kv[:, :, 1]
-    hidden = lax.all_gather(recompute_hidden, "tp", axis=3, tiled=True)
+    tp_count = lax.axis_size("tp")
+    rank = lax.axis_index("tp")
+    width = recompute_hidden.shape[3]
+    hidden = jnp.stack(
+        [recompute_hidden]
+        + [
+            lax.ppermute(recompute_hidden, "tp", [(i, (i + k) % tp_count) for i in range(tp_count)])
+            for k in range(1, tp_count)
+        ]
+    )
+    weights = jnp.stack(
+        [
+            lax.dynamic_slice_in_dim(w_kv, ((rank - k) % tp_count) * width, width, axis=0)
+            for k in range(tp_count)
+        ]
+    )
     widened = hidden.astype(jnp.float32)
-    normed = (
-        widened * lax.rsqrt(jnp.mean(widened * widened, axis=-1, keepdims=True) + 1e-06)
-    ).astype(jnp.bfloat16)
-    fresh = jnp.einsum("rcnd,dskh->rcnskh", normed, w_kv, preferred_element_type=jnp.float32)
+    square_mean = jnp.sum(widened * widened, axis=(0, 4)) / (tp_count * width)
+    normed = (widened * lax.rsqrt(square_mean + 1e-06)[None, ..., None]).astype(jnp.bfloat16)
+    fresh = jnp.einsum("trcnd,tdskh->rcnskh", normed, weights, preferred_element_type=jnp.float32)
     fresh_pos = own_offsets[:, :, None] + own_rows.astype(jnp.float32)
     fresh_keys = rotate(fresh[:, :, :, 0], fresh_pos[..., None]).astype(jnp.bfloat16)
     fresh_values = fresh[:, :, :, 1].astype(jnp.bfloat16)
@@ -247,12 +261,26 @@
         jnp.bfloat16
     )
     own_values = question_kv[:, :, 1]
-    hidden = lax.all_gather(recompute_hidden, "tp", axis=3, tiled=True)
+    tp_count = lax.axis_size("tp")
+    rank = lax.axis_index("tp")
+    width = recompute_hidden.shape[3]
+    hidden = jnp.stack(
+        [recompute_hidden]
+        + [
+            lax.ppermute(recompute_hidden, "tp", [(i, (i + k) % tp_count) for i in range(tp_count)])
+            for k in range(1, tp_count)
+        ]
+    )
+    weights = jnp.stack(
+        [
+            lax.dynamic_slice_in_dim(w_kv, ((rank - k) % tp_count) * width, width, axis=0)
+            for k in range(tp_count)
+        ]
+    )
     widened = hidden.astype(jnp.float32)
-    normed = (
-        widened * lax.rsqrt(jnp.mean(widened * widened, axis=-1, keepdims=True) + 1e-06)
-    ).astype(jnp.bfloat16)
-    fresh = jnp.einsum("rcnd,dskh->rcnskh", normed, w_kv, preferred_element_type=jnp.float32)
+    square_mean = jnp.sum(widened * widened, axis=(0, 4)) / (tp_count * width)
+    normed = (widened * lax.rsqrt(square_mean + 1e-06)[None, ..., None]).astype(jnp.bfloat16)
+    fresh = jnp.einsum("trcnd,tdskh->rcnskh", normed, weights, preferred_element_type=jnp.float32)
     fresh_pos = own_offsets[:, :, None] + own_rows.astype(jnp.float32)
     fresh_keys = rotate(fresh[:, :, :, 0], fresh_pos[..., None]).astype(jnp.bfloat16)
     fresh_values = fresh[:, :, :, 1].astype(jnp.bfloat16)
@@ -340,10 +368,10 @@
             .reshape(1, qlen, heads * head_dim)
         )
         partial_out = jnp.einsum("rqh,hm->rqm", attn, w_out, preferred_element_type=jnp.float32)
-        outputs.append(
-            lax.psum_scatter(partial_out, "tp", scatter_dimension=2, tiled=True).astype(jnp.bfloat16)
-        )
-    return jnp.concatenate(outputs, axis=0)
+        outputs.append(partial_out.astype(jnp.bfloat16))
+    pieces = jnp.concatenate(outputs, axis=0).reshape(req_dev, qlen, tp_count, -1).transpose(2, 0, 1, 3)
+    pieces = lax.all_to_all(pieces, "tp", split_axis=0, concat_axis=0, tiled=True)
+    return jnp.sum(pieces.astype(jnp.float32), axis=0).astype(jnp.bfloat16)
 
 
 def solution(mesh):

time: 301 us -> 279 us (0.927)
  waiting for transfers between devices: 118 us -> 86.6 us
  blocking collectives: 0 us -> 25.6 us
  between operations: 13.6 us -> 0.91 us
  other arithmetic: 48.6 us -> 37.9 us
  local copies, waits for them, and re-layouts: 39.4 us -> 46.7 us
  starting transfers between devices: 21.9 us -> 26.1 us
  matrix products: 16.7 us -> 13.3 us
    reduce_scatter x2 -> x0, waiting for transfers between devices: 62.7 us -> none  [shards(): lax.psum_scatter(partial_out, 'tp', scatter_dimension=2, tiled=True)]
    ppermute x0 -> x7, waiting for transfers between devices: none -> 35 us  [shards(): lax.ppermute(recompute_hidden, 'tp', [(i, (i + k) % tp_count) for i in ra...]
    all_to_all x0 -> x1, blocking collectives: none -> 25.6 us  [shards(): lax.all_to_all(pieces, 'tp', split_axis=0, concat_axis=0, tiled=True)]
    ppermute x0 -> x7, starting transfers between devices: none -> 10.2 us  [shards(): lax.ppermute(recompute_hidden, 'tp', [(i, (i + k) % tp_count) for i in ra...]
    unnamed x34 -> x51, local copies, waits for them, and re-layouts: 1.66 us -> 11.4 us
    all_to_all x2, starting transfers between devices: 21.8 us -> 15.9 us  [shards(): lax.all_to_all(outgoing, 'pool', split_axis=0, concat_axis=0, tiled=True)]
    dynamic_slice x0 -> x1, local copies, waits for them, and re-layouts: none -> 4.2 us  [shards(): lax.dynamic_slice_in_dim(w_kv, (rank - k) % tp_count * width, width, axis=0)]
  transfers between devices with their start and end apart: 5 -> 9, of which waited for: 5 -> 3; matrix products, arithmetic and copies ran while one was open for 30% -> 32% of each run, Pallas kernels for 7% -> 7%
where the time goes in v9:
time: 279 us; the launch traced here: 278 us
  waiting for transfers between devices  86.6 us (31%)
  local copies, waits for them, and re-layouts  46.7 us (17%)
  Pallas kernels  40.8 us (15%)
  other arithmetic  37.9 us (14%)
  starting transfers between devices  26.1 us (9%)
  blocking collectives  25.6 us (9%)
  matrix products  13.3 us (5%)
    all_to_all x2, waiting for transfers between devices, shards(): lax.all_to_all(outgoing, 'pool', split_axis=0, concat_axis=0, tiled=True)  51.6 us
    pallas_call x2, Pallas kernels, cached_attention(): pl.pallas_call(functools.partial(cached_kernel, scale), grid=(req_dev, po...  40.8 us
    ppermute x7, waiting for transfers between devices, shards(): lax.ppermute(recompute_hidden, 'tp', [(i, (i + k) % tp_count) for i in ra...  35 us
    all_to_all x1, blocking collectives, shards(): lax.all_to_all(pieces, 'tp', split_axis=0, concat_axis=0, tiled=True)  25.6 us
    reduce_or x1, other arithmetic, shards(): jnp.any(row_ids[..., None] == own_rows[:, :, None, None, None, :], axis=-1)  20.4 us
    all_to_all x2, starting transfers between devices, shards(): lax.all_to_all(outgoing, 'pool', split_axis=0, concat_axis=0, tiled=True)  15.9 us
    unnamed x51, local copies, waits for them, and re-layouts  11.4 us
    ppermute x7, starting transfers between devices, shards(): lax.ppermute(recompute_hidden, 'tp', [(i, (i + k) % tp_count) for i in ra...  10.2 us
  transfers between devices with their start and end apart: 9, of which 3 were waited for; matrix products, arithmetic and copies ran while one was open for 32% of the time, Pallas kernels for 7%

profile of v9, /device:TPU:1, one launch (start us, length us, event | category | flops | bytes accessed | tf_op | source)
XLA Modules:
  0.0 277.9 jit_solution(17577713559733066655)
XLA Ops:
  0.0 2.6 collective-permute-start
  7.0 2.6 collective-permute-start.4
  14.4 3.5 %gather_fusion.1 = bf16[512,2,16,128]{3,2,1,0:T(8,128)(2,1)} fusion(bf16[256,2,16,128]{3,2,1,0:T(8,128)(2,1)S(1)} %bitcast.206, s32[1024]{0:T(1024)S(1)} %get-tuple-element.95), kind=kCustom, calls=%fused_computation.1 | custom fusion | bytes 8390656 | tf_op jit(solution)/shard_map/gather | solution.py:334
  17.9 9.9 %all-to-all-start = ((bf16[32,4,4,1,2,16,128]{6,5,4,2,1,3,0:T(8,128)(2,1)}), bf16[32,4,4,1,2,16,128]{6,5,4,2,1,3,0:T(8,128)(2,1)}, u32[]{:S(2)}, u32[]{:S(2)}) async-start(bf16[32,4,4,1,2,16,128]{6,5,4,2,1,3,0:T(8,128)(2,1)} %bitcast.208), calls=%async_computation | async-start | bytes 8388608 | tf_op jit(solution)/shard_map/all_to_all | solution.py:337
  32.3 2.3 reduce_window_sum.23
  35.5 4.2 %constant_dynamic-slice_fusion.3 = (bf16[640,2,1,128]{3,1,2,0:T(2,128)(2,1)S(1)}, bf16[640,2,1,128]{3,1,2,0:T(2,128)(2,1)S(1)}, bf16[640,2,1,128]{3,1,2,0:T(2,12...) fusion(bf16[5120,2,1,128]{3,1,2,0:T(2,128)(2,1)} %param.20, ...), kind=kLoop, calls=%fused_computation.176 | loop fusion | bytes 5242912 | tf_op jit(solution)/shard_map/dynamic_slice | solution.py:276
  40.1 20.4 %compare_reduce_fusion = pred[2,4,32,4,16]{4,3,2,1,0:T(4,128)(4,1)S(1)} fusion(s32[2,4,104]{2,1,0:T(4,128)S(1)} %get-tuple-element.42, s32[2,4,32,4,16]{4,3,2,1,0:T(4,128)S(1)} %iota_add_fusion), kind=kLoop, calls=%fused_computation.11 | loop fusion | flops 3391488 | bytes 85248 | tf_op jit(solution)/shard_map/reduce_or | solution.py:316
  63.6 3.4 %gather_fusion.2 = bf16[512,2,16,128]{3,2,1,0:T(8,128)(2,1)} fusion(bf16[256,2,16,128]{3,2,1,0:T(8,128)(2,1)S(1)} %bitcast.207, s32[1024]{0:T(1024)S(1)} %get-tuple-element.94), kind=kCustom, calls=%fused_computation.2 | custom fusion | bytes 8390656 | tf_op jit(solution)/shard_map/gather | solution.py:334
  71.9 26.1 %collective-permute-done.1 = bf16[2,4,104,640]{3,2,1,0:T(8,128)(2,1)} collective-permute-done((bf16[2,4,104,640]{3,2,1,0:T(8,128)(2,1)}, bf16[2,4,104,640]{3,2,1,0:T(8,128)(2,1)}, u32[]{:S(2)}, u32[]{:S(2)}) %collective-permute-start.1) | collective-permute-done | bytes 1064992 | tf_op jit(solution)/shard_map/ppermute | solution.py:270
  103.9 8.9 %collective-permute-done.6 = bf16[2,4,104,640]{3,2,1,0:T(8,128)(2,1)S(1)} collective-permute-done((bf16[2,4,104,640]{3,2,1,0:T(8,128)(2,1)S(1)}, bf16[2,4,104,640]{3,2,1,0:T(8,128)(2,1)S(1)}, u32[]{:S(2)}, u32[]{:S(2)}) %collective-permute-start.6) | collective-permute-done | bytes 1064992 | tf_op jit(solution)/shard_map/ppermute | solution.py:270
  113.0 1.7 fusion
  114.8 2.8 %fusion.8 = f32[2,4,104,2,1,128]{5,2,3,1,0,4:T(8,128)S(1)} fusion(bf16[8,640,2,1,128]{4,1,0,2,3:T(8,128)(2,1)S(1)} %copy-done.14, bf16[8,2,4,104,640]{4,3,2,1,0:T(8,128)(2,1)S(1)} %bitcast_dynamic-update-slice_fusion, f32[2,4,104]{2,1,0:T(4,128)S(1)} %add_rsqrt_fusion), kind=kOutput, calls=%fused_computation.18 | convolution fusion | flops 2193817600 | bytes 11996416 | tf_op jit(solution)/shard_map/trcnd,tdskh->rcnskh/dot_general | solution.py:283
  117.6 1.8 fusion.31
  120.0 2.0 copy.219
  122.0 1.9 reshape.533
  124.8 5.9 %all-to-all-start.1 = ((bf16[32,4,4,1,2,16,128]{6,5,4,2,1,3,0:T(8,128)(2,1)}), bf16[32,4,4,1,2,16,128]{6,5,4,2,1,3,0:T(8,128)(2,1)}, u32[]{:S(2)}, u32[]{:S(2)}) async-start(bf16[32,4,4,1,2,16,128]{6,5,4,2,1,3,0:T(8,128)(2,1)} %bitcast.209), calls=%async_computation.1 | async-start | bytes 8388608 | tf_op jit(solution)/shard_map/all_to_all | solution.py:337
  134.2 4.5 %copy.230.valid_ref = f32[1,32,256,1]{3,2,1,0:T(8,128)} copy(f32[1,32,256,1]{1,2,3,0:T(8,128)S(1)} %get-tuple-element.60) | data formatting | bytes 65536 | tf_op jit(solution)/shard_map/broadcast_in_dim | solution.py:142
  139.3 20.4 %shard_map.109 = (f32[1,1,320]{2,1,0:T(1,128)}, f32[1,1,320]{2,1,0:T(1,128)}, f32[1,128,320]{2,1,0:T(8,128)}) custom-call(bf16[1,320,128]{2,1,0:T(8,128)(2,1)} %slice.117.q_ref, bf16[32,1,16,2,16,128]{5,4,3,2,1,0:T(8,128)(2,1)} %bitcast.72.kv_ref, f32[1,32,256,1]{3,2,1,0:T(8,128)} %copy.230.valid_ref, f32[1,8,128]{2,1,0:T(8,128)} %get-tuple-element.78.table_ref), custom_call_target="tpu_custom_call" | custom-call | tf_op jit(solution)/shard_map/pallas_call | solution.py:143
  163.0 4.6 %copy.239.valid_ref = f32[1,32,256,1]{3,2,1,0:T(8,128)} copy(f32[1,32,256,1]{1,2,3,0:T(8,128)S(1)} %get-tuple-element.59) | data formatting | bytes 65536 | tf_op jit(solution)/shard_map/broadcast_in_dim | solution.py:142
  167.6 4.1 %fusion.5 = bf16[1,64,5120]{2,1,0:T(8,128)(2,1)S(1)} fusion(bf16[640,5120]{1,0:T(8,128)(2,1)} %param.21, bf16[8,8,5,128]{3,2,1,0:T(8,128)(2,1)S(1)} %bitcast.220), kind=kOutput, calls=%fused_computation.14 | convolution fusion | flops 419758080 | bytes 7290880 | tf_op jit(solution)/shard_map/rqh,hm->rqm/dot_general | solution.py:370
  171.7 51.6 %all-to-all-done.1 = bf16[32,4,4,1,2,16,128]{6,5,4,2,1,3,0:T(8,128)(2,1)} async-done(((bf16[32,4,4,1,2,16,128]{6,5,4,2,1,3,0:T(8,128)(2,1)}), bf16[32,4,4,1,2,16,128]{6,5,4,2,1,3,0:T(8,128)(2,1)}, u32[]{:S(2)}, u32[]{:S(2)}) %all-to-all-start.1) | async-done | bytes 4194336 | tf_op jit(solution)/shard_map/all_to_all | solution.py:337
  223.3 20.4 %shard_map.110 = (f32[1,1,320]{2,1,0:T(1,128)}, f32[1,1,320]{2,1,0:T(1,128)}, f32[1,128,320]{2,1,0:T(8,128)}) custom-call(bf16[1,320,128]{2,1,0:T(8,128)(2,1)} %slice.128.q_ref, bf16[32,1,16,2,16,128]{5,4,3,2,1,0:T(8,128)(2,1)} %bitcast.83.kv_ref, f32[1,32,256,1]{3,2,1,0:T(8,128)} %copy.239.valid_ref, f32[1,8,128]{2,1,0:T(8,128)} %get-tuple-element.77.table_ref), custom_call_target="tpu_custom_call" | custom-call | tf_op jit(solution)/shard_map/pallas_call | solution.py:143
  247.0 4.1 %convolution_convert_fusion = bf16[64,5120]{1,0:T(8,128)(2,1)S(1)} fusion(bf16[640,5120]{1,0:T(8,128)(2,1)} %param.21, bf16[8,8,5,128]{3,2,1,0:T(8,128)(2,1)S(1)} %bitcast.221), kind=kOutput, calls=%fused_computation.12 | convolution fusion | flops 419758080 | bytes 7290880 | tf_op jit(solution)/shard_map/rqh,hm->rqm/dot_general | solution.py:370
  251.5 25.6 %all_to_all.15 = bf16[8,2,64,640]{3,2,1,0:T(8,128)(2,1)S(1)} all-to-all(bf16[8,2,64,640]{3,2,1,0:T(8,128)(2,1)S(1)} %maximum_bitcast_fusion), channel_id=1, replica_groups=mesh['pool'=32,'tp'=8] {'tp'}, dimensions={0} | all-to-all | bytes 2621440 | tf_op jit(solution)/shard_map/all_to_all | solution.py:373
  (158 shorter events, 41.5 us)
Async XLA Ops:
  0.0 14.3 %copy-start = (bf16[256,1,2,16,128]{4,3,2,1,0:T(8,128)(2,1)S(1)}, bf16[256,1,2,16,128]{4,3,2,1,0:T(8,128)(2,1)}, u32[]{:S(2)}) copy-start(bf16[256,1,2,16,128]{4,3,2,1,0:T(8,128)(2,1)} %param.11) | copy-start | bytes 6291460
  0.0 69.9 %collective-permute-start = (bf16[2,4,104,640]{3,2,1,0:T(8,128)(2,1)}, bf16[2,4,104,640]{3,2,1,0:T(8,128)(2,1)}, u32[]{:S(2)}, u32[]{:S(2)}) collective-permute-start(bf16[2,4,104,640]{3,2,1,0:T(8,128)(2,1)} %param.19), channel_id=1, source_target_pairs={{0,1},{1,2},{2,3},{3,4},{4,5},{5,6},{6,7},{7,0},{8,9},{9,10},{10,1... | collective-permute-start | bytes 3194888 | tf_op jit(solution)/shard_map/ppermute | solution.py:270
  2.6 95.4 %collective-permute-start.1 = (bf16[2,4,104,640]{3,2,1,0:T(8,128)(2,1)}, bf16[2,4,104,640]{3,2,1,0:T(8,128)(2,1)}, u32[]{:S(2)}, u32[]{:S(2)}) collective-permute-start(bf16[2,4,104,640]{3,2,1,0:T(8,128)(2,1)} %param.19), channel_id=1, source_target_pairs={{0,2},{1,3},{2,4},{3,5},{4,6},{5,7},{6,0},{7,1},{8,10},{9,11},{10,... | collective-permute-start | bytes 3194888 | tf_op jit(solution)/shard_map/ppermute | solution.py:270
  3.8 95.6 %collective-permute-start.2 = (bf16[2,4,104,640]{3,2,1,0:T(8,128)(2,1)}, bf16[2,4,104,640]{3,2,1,0:T(8,128)(2,1)}, u32[]{:S(2)}, u32[]{:S(2)}) collective-permute-start(bf16[2,4,104,640]{3,2,1,0:T(8,128)(2,1)} %param.19), channel_id=1, source_target_pairs={{0,3},{1,4},{2,5},{3,6},{4,7},{5,0},{6,1},{7,2},{8,11},{9,12},{10,... | collective-permute-start | bytes 3194888 | tf_op jit(solution)/shard_map/ppermute | solution.py:270
  5.4 95.5 %collective-permute-start.3 = (bf16[2,4,104,640]{3,2,1,0:T(8,128)(2,1)}, bf16[2,4,104,640]{3,2,1,0:T(8,128)(2,1)}, u32[]{:S(2)}, u32[]{:S(2)}) collective-permute-start(bf16[2,4,104,640]{3,2,1,0:T(8,128)(2,1)} %param.19), channel_id=1, source_target_pairs={{0,4},{1,5},{2,6},{3,7},{4,0},{5,1},{6,2},{7,3},{8,12},{9,13},{10,... | collective-permute-start | bytes 3194888 | tf_op jit(solution)/shard_map/ppermute | solution.py:270
  7.0 95.3 %collective-permute-start.4 = (bf16[2,4,104,640]{3,2,1,0:T(8,128)(2,1)}, bf16[2,4,104,640]{3,2,1,0:T(8,128)(2,1)}, u32[]{:S(2)}, u32[]{:S(2)}) collective-permute-start(bf16[2,4,104,640]{3,2,1,0:T(8,128)(2,1)} %param.19), channel_id=1, source_target_pairs={{0,5},{1,6},{2,7},{3,0},{4,1},{5,2},{6,3},{7,4},{8,13},{9,14},{10,... | collective-permute-start | bytes 3194888 | tf_op jit(solution)/shard_map/ppermute | solution.py:270
  17.8 10.2 %copy-start.15 = (s32[64,4]{0,1:T(4,128)S(1)}, s32[64,4]{0,1:T(4,128)}, u32[]{:S(2)}) copy-start(s32[64,4]{0,1:T(4,128)} %param.13) | copy-start | bytes 3076
  17.8 10.2 %copy-start.16 = (s32[64,4]{0,1:T(4,128)S(1)}, s32[64,4]{0,1:T(4,128)}, u32[]{:S(2)}) copy-start(s32[64,4]{0,1:T(4,128)} %param.14) | copy-start | bytes 3076
  17.8 11.5 %copy-start.12 = (bf16[2,64,5,128]{3,1,2,0:T(8,128)(2,1)S(1)}, bf16[2,64,5,128]{3,1,2,0:T(8,128)(2,1)}, u32[]{:S(2)}) copy-start(bf16[2,64,5,128]{3,1,2,0:T(8,128)(2,1)} %param.17) | copy-start | bytes 491524
  17.8 11.5 %copy-start.17 = (s32[64]{0:T(128)S(1)}, s32[64]{0:T(128)}, u32[]{:S(2)}) copy-start(s32[64]{0:T(128)} %param.16) | copy-start | bytes 772
  17.8 11.7 %copy-start.11 = (bf16[2,64,2,1,128]{4,2,3,1,0:T(2,128)(2,1)S(1)}, bf16[2,64,2,1,128]{4,2,3,1,0:T(2,128)(2,1)}, u32[]{:S(2)}) copy-start(bf16[2,64,2,1,128]{4,2,3,1,0:T(2,128)(2,1)} %param.18) | copy-start | bytes 196612
  17.9 106.9 %all-to-all-start = ((bf16[32,4,4,1,2,16,128]{6,5,4,2,1,3,0:T(8,128)(2,1)}), bf16[32,4,4,1,2,16,128]{6,5,4,2,1,3,0:T(8,128)(2,1)}, u32[]{:S(2)}, u32[]{:S(2)}) async-start(bf16[32,4,4,1,2,16,128]{6,5,4,2,1,3,0:T(8,128)(2,1)} %bitcast.208), calls=%async_computation | async-start | bytes 8388608 | tf_op jit(solution)/shard_map/all_to_all | solution.py:337
  27.8 3.8 %copy-start.2 = (s32[64,128]{1,0:T(8,128)S(1)}, s32[64,128]{1,0:T(8,128)}, u32[]{:S(2)}) copy-start(s32[64,128]{1,0:T(8,128)} %param.12) | copy-start | bytes 98308
  29.8 89.7 %copy-start.3 = (bf16[2,64,5,64]{3,1,2,0:T(8,128)(2,1)}, bf16[2,64,5,64]{3,1,2,0:T(8,128)(2,1)S(1)}, u32[]{:S(2)}) copy-start(bf16[2,64,5,64]{3,1,2,0:T(8,128)(2,1)S(1)} %get-tuple-element.55) | copy-start | bytes 245764
  29.8 89.7 %copy-start.5 = (bf16[2,64,5,64]{3,1,2,0:T(8,128)(2,1)}, bf16[2,64,5,64]{3,1,2,0:T(8,128)(2,1)S(1)}, u32[]{:S(2)}) copy-start(bf16[2,64,5,64]{3,1,2,0:T(8,128)(2,1)S(1)} %get-tuple-element.56) | copy-start | bytes 245764
  63.6 3.5 %copy-start.7 = (bf16[640,2,1,128]{3,1,2,0:T(2,128)(2,1)S(1)}, bf16[640,2,1,128]{3,1,2,0:T(2,128)(2,1)}, u32[]{:S(2)}) copy-start(bf16[640,2,1,128]{3,1,2,0:T(2,128)(2,1)} %get-tuple-element.52) | copy-start | bytes 983044
  69.9 33.8 %collective-permute-start.5 = (bf16[2,4,104,640]{3,2,1,0:T(8,128)(2,1)S(1)}, bf16[2,4,104,640]{3,2,1,0:T(8,128)(2,1)S(1)}, u32[]{:S(2)}, u32[]{:S(2)}) collective-permute-start(bf16[2,4,104,640]{3,2,1,0:T(8,128)(2,1)S(1)} %copy-done.9), channel_id=1, source_target_pairs={{0,6},{1,7},{2,0},{3,1},{4,2},{5,3},{6,4},{7,5},{8,14},{9,15},{10,... | collective-permute-start | bytes 3194888 | tf_op jit(solution)/shard_map/ppermute | solution.py:270
  98.0 14.8 %collective-permute-start.6 = (bf16[2,4,104,640]{3,2,1,0:T(8,128)(2,1)S(1)}, bf16[2,4,104,640]{3,2,1,0:T(8,128)(2,1)S(1)}, u32[]{:S(2)}, u32[]{:S(2)}) collective-permute-start(bf16[2,4,104,640]{3,2,1,0:T(8,128)(2,1)S(1)} %copy-done.9), channel_id=1, source_target_pairs={{0,7},{1,0},{2,1},{3,2},{4,3},{5,4},{6,5},{7,6},{8,15},{9,8},{10,9... | collective-permute-start | bytes 3194888 | tf_op jit(solution)/shard_map/ppermute | solution.py:270
  124.7 6.0 %copy-start.4 = (bf16[2,64,5,64]{3,1,2,0:T(8,128)(2,1)S(1)}, bf16[2,64,5,64]{3,1,2,0:T(8,128)(2,1)}, u32[]{:S(2)}) copy-start(bf16[2,64,5,64]{3,1,2,0:T(8,128)(2,1)} %copy-done.3) | copy-start | bytes 245764
  124.7 6.0 %copy-start.6 = (bf16[2,64,5,64]{3,1,2,0:T(8,128)(2,1)S(1)}, bf16[2,64,5,64]{3,1,2,0:T(8,128)(2,1)}, u32[]{:S(2)}) copy-start(bf16[2,64,5,64]{3,1,2,0:T(8,128)(2,1)} %copy-done.5) | copy-start | bytes 245764
  124.7 9.4 %copy-start.10 = (f32[2,32,4,4,16]{1,4,3,2,0:T(8,128)S(1)}, f32[2,32,4,4,16]{1,4,3,2,0:T(8,128)}, u32[]{:S(2)}) copy-start(f32[2,32,4,4,16]{1,4,3,2,0:T(8,128)} %copy.225) | copy-start | bytes 196612
  124.8 98.6 %all-to-all-start.1 = ((bf16[32,4,4,1,2,16,128]{6,5,4,2,1,3,0:T(8,128)(2,1)}), bf16[32,4,4,1,2,16,128]{6,5,4,2,1,3,0:T(8,128)(2,1)}, u32[]{:S(2)}, u32[]{:S(2)}) async-start(bf16[32,4,4,1,2,16,128]{6,5,4,2,1,3,0:T(8,128)(2,1)} %bitcast.209), calls=%async_computation.1 | async-start | bytes 8388608 | tf_op jit(solution)/shard_map/all_to_all | solution.py:337
  139.3 23.3 %copy-start.8 = (f32[2,64,1,5,128]{4,1,3,0,2:T(8,128)S(1)}, f32[2,64,1,5,128]{4,1,3,0,2:T(8,128)}, u32[]{:S(2)}) copy-start(f32[2,64,1,5,128]{4,1,3,0,2:T(8,128)} %convolution_bitcast_fusion.1) | copy-start | bytes 983044
  251.3 26.6 %copy-start.1 = (bf16[256,1,2,16,128]{4,3,2,1,0:T(8,128)(2,1)S(1)}, bf16[256,1,2,16,128]{4,3,2,1,0:T(8,128)(2,1)}, u32[]{:S(2)}) copy-start(bf16[256,1,2,16,128]{4,3,2,1,0:T(8,128)(2,1)} %param.11) | copy-start | bytes 6291460
  (3 other events, 6.1 us)

commit v10 on v9

--- a/solution.py
+++ b/solution.py
@@ -109,7 +109,7 @@
         valid = valid_ref[0, i] > 0.5
         masked = jnp.where(valid, scores, NEGATIVE)
         peak = jnp.max(masked, axis=0, keepdims=True)
-        powers = jnp.where(valid, jnp.exp(masked - peak), 0.0)
+        powers = jnp.exp(masked - jnp.maximum(peak, 0.1 * NEGATIVE))
         total = jnp.sum(powers, axis=0, keepdims=True)
         acc = lax.dot_general(
             values, powers.astype(jnp.bfloat16), (((0,), (0,)), ((), ())),
@@ -368,10 +368,25 @@
             .reshape(1, qlen, heads * head_dim)
         )
         partial_out = jnp.einsum("rqh,hm->rqm", attn, w_out, preferred_element_type=jnp.float32)
-        outputs.append(partial_out.astype(jnp.bfloat16))
-    pieces = jnp.concatenate(outputs, axis=0).reshape(req_dev, qlen, tp_count, -1).transpose(2, 0, 1, 3)
-    pieces = lax.all_to_all(pieces, "tp", split_axis=0, concat_axis=0, tiled=True)
-    return jnp.sum(pieces.astype(jnp.float32), axis=0).astype(jnp.bfloat16)
+        pieces = partial_out.astype(jnp.bfloat16).reshape(1, qlen, tp_count, -1)
+        if r < req_dev - 1:
+            own = lax.dynamic_index_in_dim(pieces, rank, axis=2, keepdims=False)
+            received = [own] + [
+                lax.ppermute(
+                    lax.dynamic_index_in_dim(pieces, (rank + k) % tp_count, axis=2, keepdims=False),
+                    "tp",
+                    [(i, (i + k) % tp_count) for i in range(tp_count)],
+                )
+                for k in range(1, tp_count)
+            ]
+            reduced = jnp.sum(jnp.stack(received).astype(jnp.float32), axis=0)
+        else:
+            pieces = lax.all_to_all(
+                pieces.transpose(2, 0, 1, 3), "tp", split_axis=0, concat_axis=0, tiled=True
+            )
+            reduced = jnp.sum(pieces.astype(jnp.float32), axis=0)
+        outputs.append(reduced.astype(jnp.bfloat16))
+    return jnp.concatenate(outputs, axis=0)
 
 
 def solution(mesh):

time: 279 us -> 276 us (0.989); the launches traced: 278 us -> 271 us
  waiting for transfers between devices: 86.6 us -> 76.4 us
  starting transfers between devices: 26.1 us -> 35.4 us
  blocking collectives: 25.6 us -> 18.3 us
    all_to_all x2, waiting for transfers between devices: 51.6 us -> 41.4 us  [shards(): lax.all_to_all(outgoing, 'pool', split_axis=0, concat_axis=0, tiled=True)]
    ppermute x0 -> x7, starting transfers between devices: none -> 8.66 us  [shards(): lax.ppermute(lax.dynamic_index_in_dim(pieces, (rank + k) % tp_count, axis...]
    all_to_all x1, blocking collectives: 25.6 us -> 18.3 us  [shards(): lax.all_to_all(pieces.transpose(2, 0, 1, 3), 'tp', split_axis=0, concat_a...]
    unnamed x51 -> x59, local copies, waits for them, and re-layouts: 11.4 us -> 11.6 us
  transfers between devices with their start and end apart: 9 -> 16, of which waited for: 3 -> 4; matrix products, arithmetic and copies ran while one was open for 32% -> 33% of each run, Pallas kernels for 7% -> 7%
where the time goes in v10:
time: 276 us; the launch traced here: 271 us
  waiting for transfers between devices  76.4 us (28%)
  local copies, waits for them, and re-layouts  48.2 us (17%)
  Pallas kernels  39.9 us (14%)
  other arithmetic  37.8 us (14%)
  starting transfers between devices  35.4 us (13%)
  blocking collectives  18.3 us (7%)
  matrix products  13.4 us (5%)
    all_to_all x2, waiting for transfers between devices, shards(): lax.all_to_all(outgoing, 'pool', split_axis=0, concat_axis=0, tiled=True)  41.4 us
    pallas_call x2, Pallas kernels, cached_attention(): pl.pallas_call(functools.partial(cached_kernel, scale), grid=(req_dev, po...  39.9 us
    ppermute x7, waiting for transfers between devices, shards(): lax.ppermute(recompute_hidden, 'tp', [(i, (i + k) % tp_count) for i in ra...  34.6 us
    reduce_or x1, other arithmetic, shards(): jnp.any(row_ids[..., None] == own_rows[:, :, None, None, None, :], axis=-1)  20.4 us
    all_to_all x1, blocking collectives, shards(): lax.all_to_all(pieces.transpose(2, 0, 1, 3), 'tp', split_axis=0, concat_a...  18.3 us
    all_to_all x2, starting transfers between devices, shards(): lax.all_to_all(outgoing, 'pool', split_axis=0, concat_axis=0, tiled=True)  16.3 us
    unnamed x59, local copies, waits for them, and re-layouts  11.6 us
    ppermute x7, starting transfers between devices, shards(): lax.ppermute(recompute_hidden, 'tp', [(i, (i + k) % tp_count) for i in ra...  10.4 us
  transfers between devices with their start and end apart: 16, of which 4 were waited for; matrix products, arithmetic and copies ran while one was open for 33% of the time, Pallas kernels for 7%

profile of v10, /device:TPU:1, one launch (start us, length us, event | category | flops | bytes accessed | tf_op | source)
XLA Modules:
  0.0 270.8 jit_solution(9890298213803076560)
XLA Ops:
  0.0 2.6 collective-permute-start
  7.0 2.6 collective-permute-start.4
  14.4 3.5 %gather_fusion.1 = bf16[512,2,16,128]{3,2,1,0:T(8,128)(2,1)} fusion(bf16[256,2,16,128]{3,2,1,0:T(8,128)(2,1)S(1)} %bitcast.242, s32[1024]{0:T(1024)S(1)} %get-tuple-element.103), kind=kCustom, calls=%fused_computation.1 | custom fusion | bytes 8390656 | tf_op jit(solution)/shard_map/gather | solution.py:334
  17.9 10.3 %all-to-all-start = ((bf16[32,4,4,1,2,16,128]{6,5,4,2,1,3,0:T(8,128)(2,1)}), bf16[32,4,4,1,2,16,128]{6,5,4,2,1,3,0:T(8,128)(2,1)}, u32[]{:S(2)}, u32[]{:S(2)}) async-start(bf16[32,4,4,1,2,16,128]{6,5,4,2,1,3,0:T(8,128)(2,1)} %bitcast.244), calls=%async_computation | async-start | bytes 8388608 | tf_op jit(solution)/shard_map/all_to_all | solution.py:337
  32.6 2.3 reduce_window_sum.23
  35.9 4.2 %constant_dynamic-slice_fusion.11 = (bf16[640,2,1,128]{3,1,2,0:T(2,128)(2,1)S(1)}, bf16[640,2,1,128]{3,1,2,0:T(2,128)(2,1)S(1)}, bf16[640,2,1,128]{3,1,2,0:T(2,1...) fusion(bf16[5120,2,1,128]{3,1,2,0:T(2,128)(2,1)} %param.20, ...), kind=kLoop, calls=%fused_computation.175 | loop fusion | bytes 5242912 | tf_op jit(solution)/shard_map/dynamic_slice | solution.py:276
  40.4 20.4 %compare_reduce_fusion = pred[2,4,32,4,16]{4,3,2,1,0:T(4,128)(4,1)S(1)} fusion(s32[2,4,104]{2,1,0:T(4,128)S(1)} %get-tuple-element.42, s32[2,4,32,4,16]{4,3,2,1,0:T(4,128)S(1)} %iota_add_fusion), kind=kLoop, calls=%fused_computation.11 | loop fusion | flops 3391488 | bytes 85248 | tf_op jit(solution)/shard_map/reduce_or | solution.py:316
  63.8 3.5 %gather_fusion.2 = bf16[512,2,16,128]{3,2,1,0:T(8,128)(2,1)} fusion(bf16[256,2,16,128]{3,2,1,0:T(8,128)(2,1)S(1)} %bitcast.243, s32[1024]{0:T(1024)S(1)} %get-tuple-element.102), kind=kCustom, calls=%fused_computation.2 | custom fusion | bytes 8390656 | tf_op jit(solution)/shard_map/gather | solution.py:334
  72.4 25.6 %collective-permute-done.1 = bf16[2,4,104,640]{3,2,1,0:T(8,128)(2,1)} collective-permute-done((bf16[2,4,104,640]{3,2,1,0:T(8,128)(2,1)}, bf16[2,4,104,640]{3,2,1,0:T(8,128)(2,1)}, u32[]{:S(2)}, u32[]{:S(2)}) %collective-permute-start.1) | collective-permute-done | bytes 1064992 | tf_op jit(solution)/shard_map/ppermute | solution.py:270
  103.9 8.9 %collective-permute-done.6 = bf16[2,4,104,640]{3,2,1,0:T(8,128)(2,1)S(1)} collective-permute-done((bf16[2,4,104,640]{3,2,1,0:T(8,128)(2,1)S(1)}, bf16[2,4,104,640]{3,2,1,0:T(8,128)(2,1)S(1)}, u32[]{:S(2)}, u32[]{:S(2)}) %collective-permute-start.6) | collective-permute-done | bytes 1064992 | tf_op jit(solution)/shard_map/ppermute | solution.py:270
  114.8 2.8 %fusion.7 = f32[2,4,104,2,1,128]{5,2,3,1,0,4:T(8,128)S(1)} fusion(bf16[8,640,2,1,128]{4,1,0,2,3:T(8,128)(2,1)S(1)} %copy-done.14, bf16[8,2,4,104,640]{4,3,2,1,0:T(8,128)(2,1)S(1)} %bitcast_dynamic-update-slice_fusion, f32[2,4,104]{2,1,0:T(4,128)S(1)} %add_rsqrt_fusion), kind=kOutput, calls=%fused_computation.17 | convolution fusion | flops 2193817600 | bytes 11996416 | tf_op jit(solution)/shard_map/trcnd,tdskh->rcnskh/dot_general | solution.py:283
  117.6 1.8 fusion.30
  120.0 2.0 copy.242
  122.0 1.9 reshape.557
  124.7 6.0 %all-to-all-start.1 = ((bf16[32,4,4,1,2,16,128]{6,5,4,2,1,3,0:T(8,128)(2,1)}), bf16[32,4,4,1,2,16,128]{6,5,4,2,1,3,0:T(8,128)(2,1)}, u32[]{:S(2)}, u32[]{:S(2)}) async-start(bf16[32,4,4,1,2,16,128]{6,5,4,2,1,3,0:T(8,128)(2,1)} %bitcast.245), calls=%async_computation.1 | async-start | bytes 8388608 | tf_op jit(solution)/shard_map/all_to_all | solution.py:337
  133.1 4.5 %copy.253.valid_ref = f32[1,32,256,1]{3,2,1,0:T(8,128)} copy(f32[1,32,256,1]{1,2,3,0:T(8,128)S(1)} %get-tuple-element.68) | data formatting | bytes 65536 | tf_op jit(solution)/shard_map/broadcast_in_dim | solution.py:142
  138.2 20.0 %shard_map.109 = (f32[1,1,320]{2,1,0:T(1,128)}, f32[1,1,320]{2,1,0:T(1,128)}, f32[1,128,320]{2,1,0:T(8,128)}) custom-call(bf16[1,320,128]{2,1,0:T(8,128)(2,1)} %slice.117.q_ref, bf16[32,1,16,2,16,128]{5,4,3,2,1,0:T(8,128)(2,1)} %bitcast.72.kv_ref, f32[1,32,256,1]{3,2,1,0:T(8,128)} %copy.253.valid_ref, f32[1,8,128]{2,1,0:T(8,128)} %get-tuple-element.86.table_ref), custom_call_target="tpu_custom_call" | custom-call | tf_op jit(solution)/shard_map/pallas_call | solution.py:143
  161.5 4.1 %convolution_convert_fusion.1 = bf16[64,5120]{1,0:T(8,128)(2,1)S(1)} fusion(bf16[640,5120]{1,0:T(8,128)(2,1)} %param.21, bf16[8,8,5,128]{3,2,1,0:T(8,128)(2,1)S(1)} %bitcast.257), kind=kOutput, calls=%fused_computation.13 | convolution fusion | flops 419758080 | bytes 7290880 | tf_op jit(solution)/shard_map/rqh,hm->rqm/dot_general | solution.py:370
  168.9 2.4 collective-permute-start.11
  177.3 4.6 %copy.270.valid_ref = f32[1,32,256,1]{3,2,1,0:T(8,128)} copy(f32[1,32,256,1]{1,2,3,0:T(8,128)S(1)} %get-tuple-element.67) | data formatting | bytes 65536 | tf_op jit(solution)/shard_map/broadcast_in_dim | solution.py:142
  182.3 41.4 %all-to-all-done.1 = bf16[32,4,4,1,2,16,128]{6,5,4,2,1,3,0:T(8,128)(2,1)} async-done(((bf16[32,4,4,1,2,16,128]{6,5,4,2,1,3,0:T(8,128)(2,1)}), bf16[32,4,4,1,2,16,128]{6,5,4,2,1,3,0:T(8,128)(2,1)}, u32[]{:S(2)}, u32[]{:S(2)}) %all-to-all-start.1) | async-done | bytes 4194336 | tf_op jit(solution)/shard_map/all_to_all | solution.py:337
  223.7 19.9 %shard_map.110 = (f32[1,1,320]{2,1,0:T(1,128)}, f32[1,1,320]{2,1,0:T(1,128)}, f32[1,128,320]{2,1,0:T(8,128)}) custom-call(bf16[1,320,128]{2,1,0:T(8,128)(2,1)} %slice.128.q_ref, bf16[32,1,16,2,16,128]{5,4,3,2,1,0:T(8,128)(2,1)} %bitcast.90.kv_ref, f32[1,32,256,1]{3,2,1,0:T(8,128)} %copy.270.valid_ref, f32[1,8,128]{2,1,0:T(8,128)} %get-tuple-element.85.table_ref), custom_call_target="tpu_custom_call" | custom-call | tf_op jit(solution)/shard_map/pallas_call | solution.py:143
  246.9 4.3 %convolution_convert_fusion = bf16[64,5120]{1,0:T(8,128)(2,1)S(1)} fusion(bf16[640,5120]{1,0:T(8,128)(2,1)} %param.21, bf16[8,8,5,128]{3,2,1,0:T(8,128)(2,1)S(1)} %bitcast.258), kind=kOutput, calls=%fused_computation.12 | convolution fusion | flops 419758080 | bytes 7290880 | tf_op jit(solution)/shard_map/rqh,hm->rqm/dot_general | solution.py:370
  251.4 18.3 %all_to_all.15 = bf16[8,1,64,640]{3,2,1,0:T(8,128)(2,1)S(1)} all-to-all(bf16[8,1,64,640]{3,2,1,0:T(8,128)(2,1)S(1)} %bitcast.250), channel_id=1, replica_groups=mesh['pool'=32,'tp'=8] {'tp'}, dimensions={0} | all-to-all | bytes 1310720 | tf_op jit(solution)/shard_map/all_to_all | solution.py:384
  (181 shorter events, 51.3 us)
Async XLA Ops:
  0.0 14.4 %copy-start = (bf16[256,1,2,16,128]{4,3,2,1,0:T(8,128)(2,1)S(1)}, bf16[256,1,2,16,128]{4,3,2,1,0:T(8,128)(2,1)}, u32[]{:S(2)}) copy-start(bf16[256,1,2,16,128]{4,3,2,1,0:T(8,128)(2,1)} %param.11) | copy-start | bytes 6291460
  0.0 70.2 %collective-permute-start = (bf16[2,4,104,640]{3,2,1,0:T(8,128)(2,1)}, bf16[2,4,104,640]{3,2,1,0:T(8,128)(2,1)}, u32[]{:S(2)}, u32[]{:S(2)}) collective-permute-start(bf16[2,4,104,640]{3,2,1,0:T(8,128)(2,1)} %param.19), channel_id=1, source_target_pairs={{0,1},{1,2},{2,3},{3,4},{4,5},{5,6},{6,7},{7,0},{8,9},{9,10},{10,1... | collective-permute-start | bytes 3194888 | tf_op jit(solution)/shard_map/ppermute | solution.py:270
  2.6 95.4 %collective-permute-start.1 = (bf16[2,4,104,640]{3,2,1,0:T(8,128)(2,1)}, bf16[2,4,104,640]{3,2,1,0:T(8,128)(2,1)}, u32[]{:S(2)}, u32[]{:S(2)}) collective-permute-start(bf16[2,4,104,640]{3,2,1,0:T(8,128)(2,1)} %param.19), channel_id=1, source_target_pairs={{0,2},{1,3},{2,4},{3,5},{4,6},{5,7},{6,0},{7,1},{8,10},{9,11},{10,... | collective-permute-start | bytes 3194888 | tf_op jit(solution)/shard_map/ppermute | solution.py:270
  3.8 95.6 %collective-permute-start.2 = (bf16[2,4,104,640]{3,2,1,0:T(8,128)(2,1)}, bf16[2,4,104,640]{3,2,1,0:T(8,128)(2,1)}, u32[]{:S(2)}, u32[]{:S(2)}) collective-permute-start(bf16[2,4,104,640]{3,2,1,0:T(8,128)(2,1)} %param.19), channel_id=1, source_target_pairs={{0,3},{1,4},{2,5},{3,6},{4,7},{5,0},{6,1},{7,2},{8,11},{9,12},{10,... | collective-permute-start | bytes 3194888 | tf_op jit(solution)/shard_map/ppermute | solution.py:270
  5.4 95.5 %collective-permute-start.3 = (bf16[2,4,104,640]{3,2,1,0:T(8,128)(2,1)}, bf16[2,4,104,640]{3,2,1,0:T(8,128)(2,1)}, u32[]{:S(2)}, u32[]{:S(2)}) collective-permute-start(bf16[2,4,104,640]{3,2,1,0:T(8,128)(2,1)} %param.19), channel_id=1, source_target_pairs={{0,4},{1,5},{2,6},{3,7},{4,0},{5,1},{6,2},{7,3},{8,12},{9,13},{10,... | collective-permute-start | bytes 3194888 | tf_op jit(solution)/shard_map/ppermute | solution.py:270
  7.0 95.3 %collective-permute-start.4 = (bf16[2,4,104,640]{3,2,1,0:T(8,128)(2,1)}, bf16[2,4,104,640]{3,2,1,0:T(8,128)(2,1)}, u32[]{:S(2)}, u32[]{:S(2)}) collective-permute-start(bf16[2,4,104,640]{3,2,1,0:T(8,128)(2,1)} %param.19), channel_id=1, source_target_pairs={{0,5},{1,6},{2,7},{3,0},{4,1},{5,2},{6,3},{7,4},{8,13},{9,14},{10,... | collective-permute-start | bytes 3194888 | tf_op jit(solution)/shard_map/ppermute | solution.py:270
  17.8 11.8 %copy-start.12 = (bf16[2,64,5,128]{3,1,2,0:T(8,128)(2,1)S(1)}, bf16[2,64,5,128]{3,1,2,0:T(8,128)(2,1)}, u32[]{:S(2)}) copy-start(bf16[2,64,5,128]{3,1,2,0:T(8,128)(2,1)} %param.17) | copy-start | bytes 491524
  17.8 11.9 %copy-start.17 = (s32[64]{0:T(128)S(1)}, s32[64]{0:T(128)}, u32[]{:S(2)}) copy-start(s32[64]{0:T(128)} %param.16) | copy-start | bytes 772
  17.8 12.0 %copy-start.11 = (bf16[2,64,2,1,128]{4,2,3,1,0:T(2,128)(2,1)S(1)}, bf16[2,64,2,1,128]{4,2,3,1,0:T(2,128)(2,1)}, u32[]{:S(2)}) copy-start(bf16[2,64,2,1,128]{4,2,3,1,0:T(2,128)(2,1)} %param.18) | copy-start | bytes 196612
  17.9 106.8 %all-to-all-start = ((bf16[32,4,4,1,2,16,128]{6,5,4,2,1,3,0:T(8,128)(2,1)}), bf16[32,4,4,1,2,16,128]{6,5,4,2,1,3,0:T(8,128)(2,1)}, u32[]{:S(2)}, u32[]{:S(2)}) async-start(bf16[32,4,4,1,2,16,128]{6,5,4,2,1,3,0:T(8,128)(2,1)} %bitcast.244), calls=%async_computation | async-start | bytes 8388608 | tf_op jit(solution)/shard_map/all_to_all | solution.py:337
  30.2 89.3 %copy-start.3 = (bf16[2,64,5,64]{3,1,2,0:T(8,128)(2,1)}, bf16[2,64,5,64]{3,1,2,0:T(8,128)(2,1)S(1)}, u32[]{:S(2)}) copy-start(bf16[2,64,5,64]{3,1,2,0:T(8,128)(2,1)S(1)} %get-tuple-element.63) | copy-start | bytes 245764
  30.2 89.3 %copy-start.5 = (bf16[2,64,5,64]{3,1,2,0:T(8,128)(2,1)}, bf16[2,64,5,64]{3,1,2,0:T(8,128)(2,1)S(1)}, u32[]{:S(2)}) copy-start(bf16[2,64,5,64]{3,1,2,0:T(8,128)(2,1)S(1)} %get-tuple-element.64) | copy-start | bytes 245764
  70.2 33.5 %collective-permute-start.5 = (bf16[2,4,104,640]{3,2,1,0:T(8,128)(2,1)S(1)}, bf16[2,4,104,640]{3,2,1,0:T(8,128)(2,1)S(1)}, u32[]{:S(2)}, u32[]{:S(2)}) collective-permute-start(bf16[2,4,104,640]{3,2,1,0:T(8,128)(2,1)S(1)} %copy-done.9), channel_id=1, source_target_pairs={{0,6},{1,7},{2,0},{3,1},{4,2},{5,3},{6,4},{7,5},{8,14},{9,15},{10,... | collective-permute-start | bytes 3194888 | tf_op jit(solution)/shard_map/ppermute | solution.py:270
  98.0 14.8 %collective-permute-start.6 = (bf16[2,4,104,640]{3,2,1,0:T(8,128)(2,1)S(1)}, bf16[2,4,104,640]{3,2,1,0:T(8,128)(2,1)S(1)}, u32[]{:S(2)}, u32[]{:S(2)}) collective-permute-start(bf16[2,4,104,640]{3,2,1,0:T(8,128)(2,1)S(1)} %copy-done.9), channel_id=1, source_target_pairs={{0,7},{1,0},{2,1},{3,2},{4,3},{5,4},{6,5},{7,6},{8,15},{9,8},{10,9... | collective-permute-start | bytes 3194888 | tf_op jit(solution)/shard_map/ppermute | solution.py:270
  124.7 99.0 %all-to-all-start.1 = ((bf16[32,4,4,1,2,16,128]{6,5,4,2,1,3,0:T(8,128)(2,1)}), bf16[32,4,4,1,2,16,128]{6,5,4,2,1,3,0:T(8,128)(2,1)}, u32[]{:S(2)}, u32[]{:S(2)}) async-start(bf16[32,4,4,1,2,16,128]{6,5,4,2,1,3,0:T(8,128)(2,1)} %bitcast.245), calls=%async_computation.1 | async-start | bytes 8388608 | tf_op jit(solution)/shard_map/all_to_all | solution.py:337
  138.2 22.9 %copy-start.8 = (f32[2,64,1,5,128]{4,1,3,0,2:T(8,128)S(1)}, f32[2,64,1,5,128]{4,1,3,0,2:T(8,128)}, u32[]{:S(2)}) copy-start(f32[2,64,1,5,128]{4,1,3,0,2:T(8,128)} %convolution_bitcast_fusion.1) | copy-start | bytes 983044
  167.1 7.5 %collective-permute-start.10 = (bf16[1,64,640]{2,1,0:T(8,128)(2,1)S(1)}, bf16[1,64,640]{2,1,0:T(8,128)(2,1)S(1)}, u32[]{:S(2)}, u32[]{:S(2)}) collective-permute-start(bf16[1,64,640]{2,1,0:T(8,128)(2,1)S(1)} %bitcast.274), channel_id=1, source_target_pairs={{0,4},{1,5},{2,6},{3,7},{4,0},{5,1},{6,2},{7,3},{8,12},{9,13},{10,... | collective-permute-start | bytes 245768 | tf_op jit(solution)/shard_map/ppermute | solution.py:375
  168.9 6.7 %collective-permute-start.11 = (bf16[1,64,640]{2,1,0:T(8,128)(2,1)S(1)}, bf16[1,64,640]{2,1,0:T(8,128)(2,1)S(1)}, u32[]{:S(2)}, u32[]{:S(2)}) collective-permute-start(bf16[1,64,640]{2,1,0:T(8,128)(2,1)S(1)} %bitcast.271), channel_id=1, source_target_pairs={{0,5},{1,6},{2,7},{3,0},{4,1},{5,2},{6,3},{7,4},{8,13},{9,14},{10,... | collective-permute-start | bytes 245768 | tf_op jit(solution)/shard_map/ppermute | solution.py:375
  172.1 9.8 %collective-permute-start.12 = (bf16[1,64,640]{2,1,0:T(8,128)(2,1)S(1)}, bf16[1,64,640]{2,1,0:T(8,128)(2,1)S(1)}, u32[]{:S(2)}, u32[]{:S(2)}) collective-permute-start(bf16[1,64,640]{2,1,0:T(8,128)(2,1)S(1)} %bitcast.269), channel_id=1, source_target_pairs={{0,6},{1,7},{2,0},{3,1},{4,2},{5,3},{6,4},{7,5},{8,14},{9,15},{10,... | collective-permute-start | bytes 245768 | tf_op jit(solution)/shard_map/ppermute | solution.py:375
  172.8 9.1 %collective-permute-start.13 = (bf16[1,64,640]{2,1,0:T(8,128)(2,1)S(1)}, bf16[1,64,640]{2,1,0:T(8,128)(2,1)S(1)}, u32[]{:S(2)}, u32[]{:S(2)}) collective-permute-start(bf16[1,64,640]{2,1,0:T(8,128)(2,1)S(1)} %bitcast.270), channel_id=1, source_target_pairs={{0,7},{1,0},{2,1},{3,2},{4,3},{5,4},{6,5},{7,6},{8,15},{9,8},{10,9... | collective-permute-start | bytes 245768 | tf_op jit(solution)/shard_map/ppermute | solution.py:375
  172.8 9.1 %collective-permute-start.7 = (bf16[1,64,640]{2,1,0:T(8,128)(2,1)S(1)}, bf16[1,64,640]{2,1,0:T(8,128)(2,1)S(1)}, u32[]{:S(2)}, u32[]{:S(2)}) collective-permute-start(bf16[1,64,640]{2,1,0:T(8,128)(2,1)S(1)} %bitcast.272), channel_id=1, source_target_pairs={{0,1},{1,2},{2,3},{3,4},{4,5},{5,6},{6,7},{7,0},{8,9},{9,10},{10,1... | collective-permute-start | bytes 245768 | tf_op jit(solution)/shard_map/ppermute | solution.py:375
  174.6 7.3 %collective-permute-start.8 = (bf16[1,64,640]{2,1,0:T(8,128)(2,1)S(1)}, bf16[1,64,640]{2,1,0:T(8,128)(2,1)S(1)}, u32[]{:S(2)}, u32[]{:S(2)}) collective-permute-start(bf16[1,64,640]{2,1,0:T(8,128)(2,1)S(1)} %bitcast.275), channel_id=1, source_target_pairs={{0,2},{1,3},{2,4},{3,5},{4,6},{5,7},{6,0},{7,1},{8,10},{9,11},{10,... | collective-permute-start | bytes 245768 | tf_op jit(solution)/shard_map/ppermute | solution.py:375
  175.6 6.6 %collective-permute-start.9 = (bf16[1,64,640]{2,1,0:T(8,128)(2,1)S(1)}, bf16[1,64,640]{2,1,0:T(8,128)(2,1)S(1)}, u32[]{:S(2)}, u32[]{:S(2)}) collective-permute-start(bf16[1,64,640]{2,1,0:T(8,128)(2,1)S(1)} %bitcast.273), channel_id=1, source_target_pairs={{0,3},{1,4},{2,5},{3,6},{4,7},{5,0},{6,1},{7,2},{8,11},{9,12},{10,... | collective-permute-start | bytes 245768 | tf_op jit(solution)/shard_map/ppermute | solution.py:375
  246.9 23.6 %copy-start.1 = (bf16[256,1,2,16,128]{4,3,2,1,0:T(8,128)(2,1)S(1)}, bf16[256,1,2,16,128]{4,3,2,1,0:T(8,128)(2,1)}, u32[]{:S(2)}) copy-start(bf16[256,1,2,16,128]{4,3,2,1,0:T(8,128)(2,1)} %param.11) | copy-start | bytes 6291460
  (10 other events, 55.2 us)

commit v11 on v10

--- a/solution.py
+++ b/solution.py
@@ -221,11 +221,10 @@
             for k in range(1, tp_count)
         ]
     )
-    weights = jnp.stack(
-        [
-            lax.dynamic_slice_in_dim(w_kv, ((rank - k) % tp_count) * width, width, axis=0)
-            for k in range(tp_count)
-        ]
+    weights = jnp.take(
+        w_kv.reshape((tp_count, width) + w_kv.shape[1:]),
+        (rank - jnp.arange(tp_count, dtype=jnp.int32)) % tp_count,
+        axis=0,
     )
     widened = hidden.astype(jnp.float32)
     square_mean = jnp.sum(widened * widened, axis=(0, 4)) / (tp_count * width)
@@ -271,11 +270,10 @@
             for k in range(1, tp_count)
         ]
     )
-    weights = jnp.stack(
-        [
-            lax.dynamic_slice_in_dim(w_kv, ((rank - k) % tp_count) * width, width, axis=0)
-            for k in range(tp_count)
-        ]
+    weights = jnp.take(
+        w_kv.reshape((tp_count, width) + w_kv.shape[1:]),
+        (rank - jnp.arange(tp_count, dtype=jnp.int32)) % tp_count,
+        axis=0,
     )
     widened = hidden.astype(jnp.float32)
     square_mean = jnp.sum(widened * widened, axis=(0, 4)) / (tp_count * width)
@@ -370,12 +368,12 @@
         partial_out = jnp.einsum("rqh,hm->rqm", attn, w_out, preferred_element_type=jnp.float32)
         pieces = partial_out.astype(jnp.bfloat16).reshape(1, qlen, tp_count, -1)
         if r < req_dev - 1:
-            own = lax.dynamic_index_in_dim(pieces, rank, axis=2, keepdims=False)
-            received = [own] + [
+            rolled = jnp.take(
+                pieces, (rank + jnp.arange(tp_count, dtype=jnp.int32)) % tp_count, axis=2
+            )
+            received = [rolled[:, :, 0]] + [
                 lax.ppermute(
-                    lax.dynamic_index_in_dim(pieces, (rank + k) % tp_count, axis=2, keepdims=False),
-                    "tp",
-                    [(i, (i + k) % tp_count) for i in range(tp_count)],
+                    rolled[:, :, k], "tp", [(i, (i + k) % tp_count) for i in range(tp_count)]
                 )
                 for k in range(1, tp_count)
             ]

time: 276 us -> 271 us (0.982); the launches traced: 271 us -> 270 us
  waiting for transfers between devices: 76.4 us -> 81 us
  local copies, waits for them, and re-layouts: 48.2 us -> 44.6 us
    dynamic_slice x2 -> x0, local copies, waits for them, and re-layouts: 5.56 us -> none  [the longest x1 4.19 us: shards(): lax.dynamic_slice_in_dim(w_kv, (rank - k) % tp_count * width, width, axis=0)]
    gather x0 -> x2, local copies, waits for them, and re-layouts: none -> 4.85 us  [the longest x1 4.18 us: shards(): jnp.take(w_kv.reshape((tp_count, width) + w_kv.shape[1:]), (rank - jnp.ar...]
    unnamed x59 -> x48, local copies, waits for them, and re-layouts: 11.6 us -> 7.46 us
    ppermute x7, waiting for transfers between devices: 34.6 us -> 38.3 us  [shards(): lax.ppermute(recompute_hidden, 'tp', [(i, (i + k) % tp_count) for i in ra...]
  transfers between devices with their start and end apart: 16 -> 16, of which waited for: 4 -> 4; matrix products, arithmetic and copies ran while one was open for 33% -> 32% of each run, Pallas kernels for 7% -> 7%
where the time goes in v11:
time: 271 us; the launch traced here: 270 us
  waiting for transfers between devices  81 us (30%)
  local copies, waits for them, and re-layouts  44.6 us (16%)
  Pallas kernels  39.9 us (15%)
  other arithmetic  38.1 us (14%)
  starting transfers between devices  34.2 us (13%)
  blocking collectives  18.4 us (7%)
  matrix products  12.9 us (5%)
    all_to_all x2, waiting for transfers between devices, shards(): lax.all_to_all(outgoing, 'pool', split_axis=0, concat_axis=0, tiled=True)  42.2 us
    pallas_call x2, Pallas kernels, cached_attention(): pl.pallas_call(functools.partial(cached_kernel, scale), grid=(req_dev, po...  39.9 us
    ppermute x7, waiting for transfers between devices, shards(): lax.ppermute(recompute_hidden, 'tp', [(i, (i + k) % tp_count) for i in ra...  38.3 us
    reduce_or x1, other arithmetic, shards(): jnp.any(row_ids[..., None] == own_rows[:, :, None, None, None, :], axis=-1)  20.4 us
    all_to_all x1, blocking collectives, shards(): lax.all_to_all(pieces.transpose(2, 0, 1, 3), 'tp', split_axis=0, concat_a...  18.4 us
    all_to_all x2, starting transfers between devices, shards(): lax.all_to_all(outgoing, 'pool', split_axis=0, concat_axis=0, tiled=True)  15.3 us
    ppermute x7, starting transfers between devices, shards(): lax.ppermute(recompute_hidden, 'tp', [(i, (i + k) % tp_count) for i in ra...  10.5 us
    broadcast_in_dim x3, local copies, waits for them, and re-layouts, cached_attention(): valid = valid[..., None]  9.08 us
  transfers between devices with their start and end apart: 16, of which 4 were waited for; matrix products, arithmetic and copies ran while one was open for 32% of the time, Pallas kernels for 7%

profile of v11, /device:TPU:1, one launch (start us, length us, event | category | flops | bytes accessed | tf_op | source)
XLA Modules:
  0.0 270.0 jit_solution(17181193994948158588)
XLA Ops:
  0.0 2.6 collective-permute-start
  7.0 2.6 collective-permute-start.4
  14.4 3.5 %gather_fusion.1 = bf16[512,2,16,128]{3,2,1,0:T(8,128)(2,1)} fusion(bf16[256,2,16,128]{3,2,1,0:T(8,128)(2,1)S(1)} %bitcast.224, s32[1024]{0:T(1024)S(1)} %get-tuple-element.96), kind=kCustom, calls=%fused_computation.1 | custom fusion | bytes 8390656 | tf_op jit(solution)/shard_map/gather | solution.py:332
  17.9 9.8 %all-to-all-start = ((bf16[32,4,4,1,2,16,128]{6,5,4,2,1,3,0:T(8,128)(2,1)}), bf16[32,4,4,1,2,16,128]{6,5,4,2,1,3,0:T(8,128)(2,1)}, u32[]{:S(2)}, u32[]{:S(2)}) async-start(bf16[32,4,4,1,2,16,128]{6,5,4,2,1,3,0:T(8,128)(2,1)} %bitcast.227), calls=%async_computation | async-start | bytes 8388608 | tf_op jit(solution)/shard_map/all_to_all | solution.py:335
  28.9 2.3 reduce_window_sum.23
  34.0 20.4 %compare_reduce_fusion = pred[2,4,32,4,16]{4,3,2,1,0:T(4,128)(4,1)S(1)} fusion(s32[2,4,104]{2,1,0:T(4,128)S(1)} %get-tuple-element.42, s32[2,4,32,4,16]{4,3,2,1,0:T(4,128)S(1)} %iota_add_fusion), kind=kLoop, calls=%fused_computation.13 | loop fusion | flops 3391488 | bytes 85248 | tf_op jit(solution)/shard_map/reduce_or | solution.py:314
  55.2 2.0 copy.187
  58.1 3.5 %gather_fusion.2 = bf16[512,2,16,128]{3,2,1,0:T(8,128)(2,1)} fusion(bf16[256,2,16,128]{3,2,1,0:T(8,128)(2,1)S(1)} %bitcast.225, s32[1024]{0:T(1024)S(1)} %get-tuple-element.95), kind=kCustom, calls=%fused_computation.2 | custom fusion | bytes 8390656 | tf_op jit(solution)/shard_map/gather | solution.py:332
  61.6 4.2 %gather_fusion.3 = bf16[8,640,2,128]{3,1,2,0:T(8,128)(2,1)} fusion(bf16[8,640,2,128]{3,1,2,0:T(8,128)(2,1)} %copy.187, s32[1024]{0:T(1024)S(1)} %pad_clamp_fusion.2), kind=kCustom, calls=%fused_computation.3 | custom fusion | bytes 5242912 | tf_op jit(solution)/shard_map/jit(_take)/gather | solution.py:273
  68.6 29.4 %collective-permute-done.1 = bf16[2,4,104,640]{3,2,1,0:T(8,128)(2,1)} collective-permute-done((bf16[2,4,104,640]{3,2,1,0:T(8,128)(2,1)}, bf16[2,4,104,640]{3,2,1,0:T(8,128)(2,1)}, u32[]{:S(2)}, u32[]{:S(2)}) %collective-permute-start.1) | collective-permute-done | bytes 1064992 | tf_op jit(solution)/shard_map/ppermute | solution.py:269
  103.9 8.9 %collective-permute-done.6 = bf16[2,4,104,640]{3,2,1,0:T(8,128)(2,1)S(1)} collective-permute-done((bf16[2,4,104,640]{3,2,1,0:T(8,128)(2,1)S(1)}, bf16[2,4,104,640]{3,2,1,0:T(8,128)(2,1)S(1)}, u32[]{:S(2)}, u32[]{:S(2)}) %collective-permute-start.6) | collective-permute-done | bytes 1064992 | tf_op jit(solution)/shard_map/ppermute | solution.py:269
  114.8 3.0 %fusion.7 = f32[2,4,104,2,1,128]{5,2,3,1,0,4:T(8,128)S(1)} fusion(bf16[8,2,4,104,640]{4,3,2,1,0:T(8,128)(2,1)S(1)} %bitcast_dynamic-update-slice_fusion, f32[2,4,104]{2,1,0:T(4,128)S(1)} %add_rsqrt_fusion, bf16[8,640,2,128]{3,1,2,0:T(8,128)(2,1)S(1)} %copy-done.8, pred[8]{0:T(512)(128)(4,1)S(1)} %compare_and_fusion.1), kind=kOutput, calls=%fused_computation.20 | convolution fusion | flops 2195128320 | bytes 11996424 | tf_op jit(solution)/shard_map/trcnd,tdskh->rcnskh/dot_general | solution.py:281
  120.2 2.0 copy.191
  122.2 1.9 reshape.676
  124.9 5.5 %all-to-all-start.1 = ((bf16[32,4,4,1,2,16,128]{6,5,4,2,1,3,0:T(8,128)(2,1)}), bf16[32,4,4,1,2,16,128]{6,5,4,2,1,3,0:T(8,128)(2,1)}, u32[]{:S(2)}, u32[]{:S(2)}) async-start(bf16[32,4,4,1,2,16,128]{6,5,4,2,1,3,0:T(8,128)(2,1)} %bitcast.226), calls=%async_computation.1 | async-start | bytes 8388608 | tf_op jit(solution)/shard_map/all_to_all | solution.py:335
  132.6 4.5 %copy.202.valid_ref = f32[1,32,256,1]{3,2,1,0:T(8,128)} copy(f32[1,32,256,1]{1,2,3,0:T(8,128)S(1)} %get-tuple-element.59) | data formatting | bytes 65536 | tf_op jit(solution)/shard_map/broadcast_in_dim | solution.py:142
  137.8 19.9 %shard_map.109 = (f32[1,1,320]{2,1,0:T(1,128)}, f32[1,1,320]{2,1,0:T(1,128)}, f32[1,128,320]{2,1,0:T(8,128)}) custom-call(bf16[1,320,128]{2,1,0:T(8,128)(2,1)} %slice.141.q_ref, bf16[32,1,16,2,16,128]{5,4,3,2,1,0:T(8,128)(2,1)} %bitcast.64.kv_ref, f32[1,32,256,1]{3,2,1,0:T(8,128)} %copy.202.valid_ref, f32[1,8,128]{2,1,0:T(8,128)} %get-tuple-element.77.table_ref), custom_call_target="tpu_custom_call" | custom-call | tf_op jit(solution)/shard_map/pallas_call | solution.py:143
  161.0 4.1 %convolution_convert_fusion.1 = bf16[64,5120]{1,0:T(8,128)(2,1)S(1)} fusion(bf16[640,5120]{1,0:T(8,128)(2,1)} %param.21, bf16[8,8,5,128]{3,2,1,0:T(8,128)(2,1)S(1)} %bitcast.240), kind=kOutput, calls=%fused_computation.15 | convolution fusion | flops 419758080 | bytes 7290880 | tf_op jit(solution)/shard_map/rqh,hm->rqm/dot_general | solution.py:368
  167.7 2.4 collective-permute-start.11
  175.9 4.5 %copy.212.valid_ref = f32[1,32,256,1]{3,2,1,0:T(8,128)} copy(f32[1,32,256,1]{1,2,3,0:T(8,128)S(1)} %get-tuple-element.58) | data formatting | bytes 65536 | tf_op jit(solution)/shard_map/broadcast_in_dim | solution.py:142
  180.9 42.2 %all-to-all-done.1 = bf16[32,4,4,1,2,16,128]{6,5,4,2,1,3,0:T(8,128)(2,1)} async-done(((bf16[32,4,4,1,2,16,128]{6,5,4,2,1,3,0:T(8,128)(2,1)}), bf16[32,4,4,1,2,16,128]{6,5,4,2,1,3,0:T(8,128)(2,1)}, u32[]{:S(2)}, u32[]{:S(2)}) %all-to-all-start.1) | async-done | bytes 4194336 | tf_op jit(solution)/shard_map/all_to_all | solution.py:335
  223.1 20.0 %shard_map.110 = (f32[1,1,320]{2,1,0:T(1,128)}, f32[1,1,320]{2,1,0:T(1,128)}, f32[1,128,320]{2,1,0:T(8,128)}) custom-call(bf16[1,320,128]{2,1,0:T(8,128)(2,1)} %slice.160.q_ref, bf16[32,1,16,2,16,128]{5,4,3,2,1,0:T(8,128)(2,1)} %bitcast.85.kv_ref, f32[1,32,256,1]{3,2,1,0:T(8,128)} %copy.212.valid_ref, f32[1,8,128]{2,1,0:T(8,128)} %get-tuple-element.76.table_ref), custom_call_target="tpu_custom_call" | custom-call | tf_op jit(solution)/shard_map/pallas_call | solution.py:143
  246.4 4.3 %convolution_convert_fusion = bf16[64,5120]{1,0:T(8,128)(2,1)S(1)} fusion(bf16[640,5120]{1,0:T(8,128)(2,1)} %param.21, bf16[8,8,5,128]{3,2,1,0:T(8,128)(2,1)S(1)} %bitcast.241), kind=kOutput, calls=%fused_computation.14 | convolution fusion | flops 419758080 | bytes 7290880 | tf_op jit(solution)/shard_map/rqh,hm->rqm/dot_general | solution.py:368
  250.9 18.4 %all_to_all.15 = bf16[8,1,64,640]{3,2,1,0:T(8,128)(2,1)S(1)} all-to-all(bf16[8,1,64,640]{3,2,1,0:T(8,128)(2,1)S(1)} %bitcast.233), channel_id=1, replica_groups=mesh['pool'=32,'tp'=8] {'tp'}, dimensions={0} | all-to-all | bytes 1310720 | tf_op jit(solution)/shard_map/all_to_all | solution.py:382
  (178 shorter events, 47.3 us)
Async XLA Ops:
  0.0 66.3 %collective-permute-start = (bf16[2,4,104,640]{3,2,1,0:T(8,128)(2,1)}, bf16[2,4,104,640]{3,2,1,0:T(8,128)(2,1)}, u32[]{:S(2)}, u32[]{:S(2)}) collective-permute-start(bf16[2,4,104,640]{3,2,1,0:T(8,128)(2,1)} %param.19), channel_id=1, source_target_pairs={{0,1},{1,2},{2,3},{3,4},{4,5},{5,6},{6,7},{7,0},{8,9},{9,10},{10,1... | collective-permute-start | bytes 3194888 | tf_op jit(solution)/shard_map/ppermute | solution.py:269
  2.6 95.4 %collective-permute-start.1 = (bf16[2,4,104,640]{3,2,1,0:T(8,128)(2,1)}, bf16[2,4,104,640]{3,2,1,0:T(8,128)(2,1)}, u32[]{:S(2)}, u32[]{:S(2)}) collective-permute-start(bf16[2,4,104,640]{3,2,1,0:T(8,128)(2,1)} %param.19), channel_id=1, source_target_pairs={{0,2},{1,3},{2,4},{3,5},{4,6},{5,7},{6,0},{7,1},{8,10},{9,11},{10,... | collective-permute-start | bytes 3194888 | tf_op jit(solution)/shard_map/ppermute | solution.py:269
  3.8 95.6 %collective-permute-start.2 = (bf16[2,4,104,640]{3,2,1,0:T(8,128)(2,1)}, bf16[2,4,104,640]{3,2,1,0:T(8,128)(2,1)}, u32[]{:S(2)}, u32[]{:S(2)}) collective-permute-start(bf16[2,4,104,640]{3,2,1,0:T(8,128)(2,1)} %param.19), channel_id=1, source_target_pairs={{0,3},{1,4},{2,5},{3,6},{4,7},{5,0},{6,1},{7,2},{8,11},{9,12},{10,... | collective-permute-start | bytes 3194888 | tf_op jit(solution)/shard_map/ppermute | solution.py:269
  5.4 95.5 %collective-permute-start.3 = (bf16[2,4,104,640]{3,2,1,0:T(8,128)(2,1)}, bf16[2,4,104,640]{3,2,1,0:T(8,128)(2,1)}, u32[]{:S(2)}, u32[]{:S(2)}) collective-permute-start(bf16[2,4,104,640]{3,2,1,0:T(8,128)(2,1)} %param.19), channel_id=1, source_target_pairs={{0,4},{1,5},{2,6},{3,7},{4,0},{5,1},{6,2},{7,3},{8,12},{9,13},{10,... | collective-permute-start | bytes 3194888 | tf_op jit(solution)/shard_map/ppermute | solution.py:269
  7.0 95.3 %collective-permute-start.4 = (bf16[2,4,104,640]{3,2,1,0:T(8,128)(2,1)}, bf16[2,4,104,640]{3,2,1,0:T(8,128)(2,1)}, u32[]{:S(2)}, u32[]{:S(2)}) collective-permute-start(bf16[2,4,104,640]{3,2,1,0:T(8,128)(2,1)} %param.19), channel_id=1, source_target_pairs={{0,5},{1,6},{2,7},{3,0},{4,1},{5,2},{6,3},{7,4},{8,13},{9,14},{10,... | collective-permute-start | bytes 3194888 | tf_op jit(solution)/shard_map/ppermute | solution.py:269
  17.9 107.0 %all-to-all-start = ((bf16[32,4,4,1,2,16,128]{6,5,4,2,1,3,0:T(8,128)(2,1)}), bf16[32,4,4,1,2,16,128]{6,5,4,2,1,3,0:T(8,128)(2,1)}, u32[]{:S(2)}, u32[]{:S(2)}) async-start(bf16[32,4,4,1,2,16,128]{6,5,4,2,1,3,0:T(8,128)(2,1)} %bitcast.227), calls=%async_computation | async-start | bytes 8388608 | tf_op jit(solution)/shard_map/all_to_all | solution.py:335
  32.0 23.2 %copy-start.3 = (bf16[5120,2,1,128]{3,1,2,0:T(2,128)(2,1)S(1)}, bf16[5120,2,1,128]{3,1,2,0:T(2,128)(2,1)}, u32[]{:S(2)}) copy-start(bf16[5120,2,1,128]{3,1,2,0:T(2,128)(2,1)} %param.20) | copy-start | bytes 7864324
  54.8 64.9 %copy-start.4 = (bf16[2,64,5,64]{3,1,2,0:T(8,128)(2,1)}, bf16[2,64,5,64]{3,1,2,0:T(8,128)(2,1)S(1)}, u32[]{:S(2)}) copy-start(bf16[2,64,5,64]{3,1,2,0:T(8,128)(2,1)S(1)} %get-tuple-element.54) | copy-start | bytes 245764
  54.8 64.9 %copy-start.6 = (bf16[2,64,5,64]{3,1,2,0:T(8,128)(2,1)}, bf16[2,64,5,64]{3,1,2,0:T(8,128)(2,1)S(1)}, u32[]{:S(2)}) copy-start(bf16[2,64,5,64]{3,1,2,0:T(8,128)(2,1)S(1)} %get-tuple-element.55) | copy-start | bytes 245764
  66.2 94.4 %copy-start.11 = (f32[2,64,1,5,128]{4,1,3,0,2:T(8,128)}, f32[2,64,1,5,128]{4,1,3,0,2:T(8,128)S(1)}, u32[]{:S(2)}) copy-start(f32[2,64,1,5,128]{4,1,3,0,2:T(8,128)S(1)} %convolution_bitcast_fusion.1) | copy-start | bytes 983044
  66.3 37.4 %collective-permute-start.5 = (bf16[2,4,104,640]{3,2,1,0:T(8,128)(2,1)S(1)}, bf16[2,4,104,640]{3,2,1,0:T(8,128)(2,1)S(1)}, u32[]{:S(2)}, u32[]{:S(2)}) collective-permute-start(bf16[2,4,104,640]{3,2,1,0:T(8,128)(2,1)S(1)} %copy-done.13), channel_id=1, source_target_pairs={{0,6},{1,7},{2,0},{3,1},{4,2},{5,3},{6,4},{7,5},{8,14},{9,15},{10,... | collective-permute-start | bytes 3194888 | tf_op jit(solution)/shard_map/ppermute | solution.py:269
  98.0 14.8 %collective-permute-start.6 = (bf16[2,4,104,640]{3,2,1,0:T(8,128)(2,1)S(1)}, bf16[2,4,104,640]{3,2,1,0:T(8,128)(2,1)S(1)}, u32[]{:S(2)}, u32[]{:S(2)}) collective-permute-start(bf16[2,4,104,640]{3,2,1,0:T(8,128)(2,1)S(1)} %copy-done.13), channel_id=1, source_target_pairs={{0,7},{1,0},{2,1},{3,2},{4,3},{5,4},{6,5},{7,6},{8,15},{9,8},{10,9... | collective-permute-start | bytes 3194888 | tf_op jit(solution)/shard_map/ppermute | solution.py:269
  124.9 35.7 %copy-start.9 = (f32[2,64,1,5,128]{4,1,3,0,2:T(8,128)}, f32[2,64,1,5,128]{4,1,3,0,2:T(8,128)S(1)}, u32[]{:S(2)}) copy-start(f32[2,64,1,5,128]{4,1,3,0,2:T(8,128)S(1)} %convolution_bitcast_fusion) | copy-start | bytes 983044
  124.9 98.2 %all-to-all-start.1 = ((bf16[32,4,4,1,2,16,128]{6,5,4,2,1,3,0:T(8,128)(2,1)}), bf16[32,4,4,1,2,16,128]{6,5,4,2,1,3,0:T(8,128)(2,1)}, u32[]{:S(2)}, u32[]{:S(2)}) async-start(bf16[32,4,4,1,2,16,128]{6,5,4,2,1,3,0:T(8,128)(2,1)} %bitcast.226), calls=%async_computation.1 | async-start | bytes 8388608 | tf_op jit(solution)/shard_map/all_to_all | solution.py:335
  166.1 7.3 %collective-permute-start.10 = (bf16[1,64,640]{2,1,0:T(8,128)(2,1)S(1)}, bf16[1,64,640]{2,1,0:T(8,128)(2,1)S(1)}, u32[]{:S(2)}, u32[]{:S(2)}) collective-permute-start(bf16[1,64,640]{2,1,0:T(8,128)(2,1)S(1)} %get-tuple-element.49), channel_id=1, source_target_pairs={{0,4},{1,5},{2,6},{3,7},{4,0},{5,1},{6,2},{7,3},{8,12},{9,13},{10,... | collective-permute-start | bytes 245768 | tf_op jit(solution)/shard_map/ppermute | solution.py:375
  167.7 6.3 %collective-permute-start.11 = (bf16[1,64,640]{2,1,0:T(8,128)(2,1)S(1)}, bf16[1,64,640]{2,1,0:T(8,128)(2,1)S(1)}, u32[]{:S(2)}, u32[]{:S(2)}) collective-permute-start(bf16[1,64,640]{2,1,0:T(8,128)(2,1)S(1)} %get-tuple-element.48), channel_id=1, source_target_pairs={{0,5},{1,6},{2,7},{3,0},{4,1},{5,2},{6,3},{7,4},{8,13},{9,14},{10,... | collective-permute-start | bytes 245768 | tf_op jit(solution)/shard_map/ppermute | solution.py:375
  170.8 9.6 %collective-permute-start.12 = (bf16[1,64,640]{2,1,0:T(8,128)(2,1)S(1)}, bf16[1,64,640]{2,1,0:T(8,128)(2,1)S(1)}, u32[]{:S(2)}, u32[]{:S(2)}) collective-permute-start(bf16[1,64,640]{2,1,0:T(8,128)(2,1)S(1)} %get-tuple-element.47), channel_id=1, source_target_pairs={{0,6},{1,7},{2,0},{3,1},{4,2},{5,3},{6,4},{7,5},{8,14},{9,15},{10,... | collective-permute-start | bytes 245768 | tf_op jit(solution)/shard_map/ppermute | solution.py:375
  171.6 8.9 %collective-permute-start.13 = (bf16[1,64,640]{2,1,0:T(8,128)(2,1)S(1)}, bf16[1,64,640]{2,1,0:T(8,128)(2,1)S(1)}, u32[]{:S(2)}, u32[]{:S(2)}) collective-permute-start(bf16[1,64,640]{2,1,0:T(8,128)(2,1)S(1)} %get-tuple-element.46), channel_id=1, source_target_pairs={{0,7},{1,0},{2,1},{3,2},{4,3},{5,4},{6,5},{7,6},{8,15},{9,8},{10,9... | collective-permute-start | bytes 245768 | tf_op jit(solution)/shard_map/ppermute | solution.py:375
  171.6 8.9 %collective-permute-start.7 = (bf16[1,64,640]{2,1,0:T(8,128)(2,1)S(1)}, bf16[1,64,640]{2,1,0:T(8,128)(2,1)S(1)}, u32[]{:S(2)}, u32[]{:S(2)}) collective-permute-start(bf16[1,64,640]{2,1,0:T(8,128)(2,1)S(1)} %get-tuple-element.45), channel_id=1, source_target_pairs={{0,1},{1,2},{2,3},{3,4},{4,5},{5,6},{6,7},{7,0},{8,9},{9,10},{10,1... | collective-permute-start | bytes 245768 | tf_op jit(solution)/shard_map/ppermute | solution.py:375
  173.3 7.1 %collective-permute-start.8 = (bf16[1,64,640]{2,1,0:T(8,128)(2,1)S(1)}, bf16[1,64,640]{2,1,0:T(8,128)(2,1)S(1)}, u32[]{:S(2)}, u32[]{:S(2)}) collective-permute-start(bf16[1,64,640]{2,1,0:T(8,128)(2,1)S(1)} %get-tuple-element.51), channel_id=1, source_target_pairs={{0,2},{1,3},{2,4},{3,5},{4,6},{5,7},{6,0},{7,1},{8,10},{9,11},{10,... | collective-permute-start | bytes 245768 | tf_op jit(solution)/shard_map/ppermute | solution.py:375
  174.0 6.8 %collective-permute-start.9 = (bf16[1,64,640]{2,1,0:T(8,128)(2,1)S(1)}, bf16[1,64,640]{2,1,0:T(8,128)(2,1)S(1)}, u32[]{:S(2)}, u32[]{:S(2)}) collective-permute-start(bf16[1,64,640]{2,1,0:T(8,128)(2,1)S(1)} %get-tuple-element.50), channel_id=1, source_target_pairs={{0,3},{1,4},{2,5},{3,6},{4,7},{5,0},{6,1},{7,2},{8,11},{9,12},{10,... | collective-permute-start | bytes 245768 | tf_op jit(solution)/shard_map/ppermute | solution.py:375
  223.1 22.9 %copy-start.10 = (f32[2,64,1,5,128]{4,1,3,0,2:T(8,128)S(1)}, f32[2,64,1,5,128]{4,1,3,0,2:T(8,128)}, u32[]{:S(2)}) copy-start(f32[2,64,1,5,128]{4,1,3,0,2:T(8,128)} %copy-done.9) | copy-start | bytes 983044
  223.1 22.9 %copy-start.12 = (f32[2,64,1,5,128]{4,1,3,0,2:T(8,128)S(1)}, f32[2,64,1,5,128]{4,1,3,0,2:T(8,128)}, u32[]{:S(2)}) copy-start(f32[2,64,1,5,128]{4,1,3,0,2:T(8,128)} %copy-done.11) | copy-start | bytes 983044
  246.4 23.6 %copy-start.1 = (bf16[256,1,2,16,128]{4,3,2,1,0:T(8,128)(2,1)S(1)}, bf16[256,1,2,16,128]{4,3,2,1,0:T(8,128)(2,1)}, u32[]{:S(2)}) copy-start(bf16[256,1,2,16,128]{4,3,2,1,0:T(8,128)(2,1)} %param.11) | copy-start | bytes 6291460
  (12 other events, 105.4 us)

commit v12 on v11

--- a/solution.py
+++ b/solution.py
@@ -214,18 +214,20 @@
     tp_count = lax.axis_size("tp")
     rank = lax.axis_index("tp")
     width = recompute_hidden.shape[3]
-    hidden = jnp.stack(
-        [recompute_hidden]
+    partner = lax.ppermute(recompute_hidden, "tp", [(i, i ^ 1) for i in range(tp_count)])
+    pair = jnp.stack([recompute_hidden, partner])
+    shifts = range(0, tp_count, 2)
+    hidden = jnp.concatenate(
+        [pair]
         + [
-            lax.ppermute(recompute_hidden, "tp", [(i, (i + k) % tp_count) for i in range(tp_count)])
-            for k in range(1, tp_count)
+            lax.ppermute(pair, "tp", [(i, (i + k) % tp_count) for i in range(tp_count)])
+            for k in shifts[1:]
         ]
     )
-    weights = jnp.take(
-        w_kv.reshape((tp_count, width) + w_kv.shape[1:]),
-        (rank - jnp.arange(tp_count, dtype=jnp.int32)) % tp_count,
-        axis=0,
-    )
+    sources = jnp.stack(
+        [jnp.stack([(rank - k) % tp_count, ((rank - k) % tp_count) ^ 1]) for k in shifts]
+    ).reshape(-1)
+    weights = jnp.take(w_kv.reshape((tp_count, width) + w_kv.shape[1:]), sources, axis=0)
     widened = hidden.astype(jnp.float32)
     square_mean = jnp.sum(widened * widened, axis=(0, 4)) / (tp_count * width)
     normed = (widened * lax.rsqrt(square_mean + 1e-06)[None, ..., None]).astype(jnp.bfloat16)
@@ -263,18 +265,20 @@
     tp_count = lax.axis_size("tp")
     rank = lax.axis_index("tp")
     width = recompute_hidden.shape[3]
-    hidden = jnp.stack(
-        [recompute_hidden]
+    partner = lax.ppermute(recompute_hidden, "tp", [(i, i ^ 1) for i in range(tp_count)])
+    pair = jnp.stack([recompute_hidden, partner])
+    shifts = range(0, tp_count, 2)
+    hidden = jnp.concatenate(
+        [pair]
         + [
-            lax.ppermute(recompute_hidden, "tp", [(i, (i + k) % tp_count) for i in range(tp_count)])
-            for k in range(1, tp_count)
+            lax.ppermute(pair, "tp", [(i, (i + k) % tp_count) for i in range(tp_count)])
+            for k in shifts[1:]
         ]
     )
-    weights = jnp.take(
-        w_kv.reshape((tp_count, width) + w_kv.shape[1:]),
-        (rank - jnp.arange(tp_count, dtype=jnp.int32)) % tp_count,
-        axis=0,
-    )
+    sources = jnp.stack(
+        [jnp.stack([(rank - k) % tp_count, ((rank - k) % tp_count) ^ 1]) for k in shifts]
+    ).reshape(-1)
+    weights = jnp.take(w_kv.reshape((tp_count, width) + w_kv.shape[1:]), sources, axis=0)
     widened = hidden.astype(jnp.float32)
     square_mean = jnp.sum(widened * widened, axis=(0, 4)) / (tp_count * width)
     normed = (widened * lax.rsqrt(square_mean + 1e-06)[None, ..., None]).astype(jnp.bfloat16)

time: 271 us -> 322 us (1.19)
  waiting for transfers between devices: 81 us -> 117 us
  other arithmetic: 38.1 us -> 48.3 us
  local copies, waits for them, and re-layouts: 44.6 us -> 50 us
  blocking collectives: 18.4 us -> 14.7 us
    ppermute x7 -> x4, waiting for transfers between devices: 38.3 us -> 70.4 us  [the longest x3 70.4 us: shards(): lax.ppermute(pair, 'tp', [(i, (i + k) % tp_count) for i in range(tp_count)])]
    all_to_all x2, waiting for transfers between devices: 42.2 us -> 46.8 us  [shards(): lax.all_to_all(outgoing, 'pool', split_axis=0, concat_axis=0, tiled=True)]
    all_to_all x2, starting transfers between devices: 15.3 us -> 18.9 us  [shards(): lax.all_to_all(outgoing, 'pool', split_axis=0, concat_axis=0, tiled=True)]
    all_to_all x1, blocking collectives: 18.4 us -> 14.7 us  [shards(): lax.all_to_all(pieces.transpose(2, 0, 1, 3), 'tp', split_axis=0, concat_a...]
    ppermute x7 -> x4, starting transfers between devices: 10.5 us -> 8.3 us  [the longest x3 5.1 us: shards(): lax.ppermute(pair, 'tp', [(i, (i + k) % tp_count) for i in range(tp_count)])]
    unnamed x48 -> x51, local copies, waits for them, and re-layouts: 7.46 us -> 5.6 us
  transfers between devices with their start and end apart: 16 -> 13, of which waited for: 4 -> 3; matrix products, arithmetic and copies ran while one was open for 32% -> 33% of each run, Pallas kernels for 7% -> 6%
where the time goes in v12:
time: 322 us; the launch traced here: 321 us
  waiting for transfers between devices  117 us (36%)
  local copies, waits for them, and re-layouts  50 us (16%)
  other arithmetic  48.3 us (15%)
  Pallas kernels  40 us (12%)
  starting transfers between devices  35.5 us (11%)
  blocking collectives  14.7 us (5%)
  matrix products  14.6 us (5%)
    ppermute x3, waiting for transfers between devices, shards(): lax.ppermute(pair, 'tp', [(i, (i + k) % tp_count) for i in range(tp_count)])  70.4 us
    all_to_all x2, waiting for transfers between devices, shards(): lax.all_to_all(outgoing, 'pool', split_axis=0, concat_axis=0, tiled=True)  46.8 us
    pallas_call x2, Pallas kernels, cached_attention(): pl.pallas_call(functools.partial(cached_kernel, scale), grid=(req_dev, po...  40 us
    reduce_or x1, other arithmetic, shards(): jnp.any(row_ids[..., None] == own_rows[:, :, None, None, None, :], axis=-1)  20.4 us
    all_to_all x2, starting transfers between devices, shards(): lax.all_to_all(outgoing, 'pool', split_axis=0, concat_axis=0, tiled=True)  18.9 us
    all_to_all x1, blocking collectives, shards(): lax.all_to_all(pieces.transpose(2, 0, 1, 3), 'tp', split_axis=0, concat_a...  14.7 us
    broadcast_in_dim x3, local copies, waits for them, and re-layouts, cached_attention(): valid = valid[..., None]  9.11 us
    dot_general x2, matrix products, shards(): jnp.einsum('rqh,hm->rqm', attn, w_out, preferred_element_type=jnp.float32)  8.41 us
  transfers between devices with their start and end apart: 13, of which 3 were waited for; matrix products, arithmetic and copies ran while one was open for 33% of the time, Pallas kernels for 6%

profile of v12, /device:TPU:1, one launch (start us, length us, event | category | flops | bytes accessed | tf_op | source)
XLA Modules:
  0.0 321.0 jit_solution(8519339413905039864)
XLA Ops:
  0.0 3.2 collective-permute-start
  8.0 3.5 %gather_fusion.1 = bf16[512,2,16,128]{3,2,1,0:T(8,128)(2,1)} fusion(bf16[256,2,16,128]{3,2,1,0:T(8,128)(2,1)S(1)} %bitcast.228, s32[1024]{0:T(1024)S(1)} %get-tuple-element.96), kind=kCustom, calls=%fused_computation.1 | custom fusion | bytes 8390656 | tf_op jit(solution)/shard_map/gather | solution.py:336
  11.5 9.8 %all-to-all-start = ((bf16[32,4,4,1,2,16,128]{6,5,4,2,1,3,0:T(8,128)(2,1)}), bf16[32,4,4,1,2,16,128]{6,5,4,2,1,3,0:T(8,128)(2,1)}, u32[]{:S(2)}, u32[]{:S(2)}) async-start(bf16[32,4,4,1,2,16,128]{6,5,4,2,1,3,0:T(8,128)(2,1)} %bitcast.230), calls=%async_computation | async-start | bytes 8388608 | tf_op jit(solution)/shard_map/all_to_all | solution.py:339
  24.5 2.3 reduce_window_sum.23
  34.7 20.4 %compare_reduce_fusion = pred[2,4,32,4,16]{4,3,2,1,0:T(4,128)(4,1)S(1)} fusion(s32[2,4,104]{2,1,0:T(4,128)S(1)} %get-tuple-element.42, s32[2,4,32,4,16]{4,3,2,1,0:T(4,128)S(1)} %iota_add_fusion), kind=kLoop, calls=%fused_computation.13 | loop fusion | flops 3391488 | bytes 85248 | tf_op jit(solution)/shard_map/reduce_or | solution.py:318
  56.1 2.8 pad_maximum_fusion
  60.3 2.5 collective-permute-start.2
  65.4 3.8 %copy.187 = bf16[8,640,2,128]{3,1,2,0:T(8,128)(2,1)} copy(bf16[8,640,2,128]{3,2,1,0:T(2,128)(2,1)} %bitcast.235) | data formatting | bytes 5242880 | tf_op jit(solution)/shard_map/reshape | solution.py:281
  71.2 3.5 %gather_fusion.2 = bf16[512,2,16,128]{3,2,1,0:T(8,128)(2,1)} fusion(bf16[256,2,16,128]{3,2,1,0:T(8,128)(2,1)S(1)} %bitcast.229, s32[1024]{0:T(1024)S(1)} %get-tuple-element.95), kind=kCustom, calls=%fused_computation.2 | custom fusion | bytes 8390656 | tf_op jit(solution)/shard_map/gather | solution.py:336
  74.6 4.3 %gather_fusion.3 = bf16[8,640,2,128]{3,1,2,0:T(8,128)(2,1)} fusion(bf16[8,640,2,128]{3,1,2,0:T(8,128)(2,1)} %copy.187, s32[1024]{0:T(1024)} %pad_clamp_fusion.2), kind=kCustom, calls=%fused_computation.3 | custom fusion | bytes 5242912 | tf_op jit(solution)/shard_map/jit(_take)/gather | solution.py:281
  82.1 25.7 %collective-permute-done.1 = bf16[2,2,4,104,640]{4,3,2,1,0:T(8,128)(2,1)} collective-permute-done((bf16[2,2,4,104,640]{4,3,2,1,0:T(8,128)(2,1)}, bf16[2,2,4,104,640]{4,3,2,1,0:T(8,128)(2,1)}, u32[]{:S(2)}, u32[]{:S(2)}) %collective-permute-start.1) | collective-permute-done | bytes 2129952 | tf_op jit(solution)/shard_map/ppermute | solution.py:274
  109.8 44.7 %collective-permute-done.2 = bf16[2,2,4,104,640]{4,3,2,1,0:T(8,128)(2,1)} collective-permute-done((bf16[2,2,4,104,640]{4,3,2,1,0:T(8,128)(2,1)}, bf16[2,2,4,104,640]{4,3,2,1,0:T(8,128)(2,1)}, u32[]{:S(2)}, u32[]{:S(2)}) %collective-permute-start.2) | collective-permute-done | bytes 2129952 | tf_op jit(solution)/shard_map/ppermute | solution.py:274
  156.5 2.0 constant_dynamic-update-slice_fusion
  160.2 3.0 fusion.7
  172.0 9.1 %all-to-all-start.1 = ((bf16[32,4,4,1,2,16,128]{6,5,4,2,1,3,0:T(8,128)(2,1)}), bf16[32,4,4,1,2,16,128]{6,5,4,2,1,3,0:T(8,128)(2,1)}, u32[]{:S(2)}, u32[]{:S(2)}) async-start(bf16[32,4,4,1,2,16,128]{6,5,4,2,1,3,0:T(8,128)(2,1)} %bitcast.231), calls=%async_computation.1 | async-start | bytes 8388608 | tf_op jit(solution)/shard_map/all_to_all | solution.py:339
  183.3 4.5 %copy.202.valid_ref = f32[1,32,256,1]{3,2,1,0:T(8,128)} copy(f32[1,32,256,1]{1,2,3,0:T(8,128)S(1)} %get-tuple-element.59) | data formatting | bytes 65536 | tf_op jit(solution)/shard_map/broadcast_in_dim | solution.py:142
  188.5 20.0 %shard_map.109 = (f32[1,1,320]{2,1,0:T(1,128)}, f32[1,1,320]{2,1,0:T(1,128)}, f32[1,128,320]{2,1,0:T(8,128)}) custom-call(bf16[1,320,128]{2,1,0:T(8,128)(2,1)} %slice.141.q_ref, bf16[32,1,16,2,16,128]{5,4,3,2,1,0:T(8,128)(2,1)} %bitcast.70.kv_ref, f32[1,32,256,1]{3,2,1,0:T(8,128)} %copy.202.valid_ref, f32[1,8,128]{2,1,0:T(8,128)} %get-tuple-element.77.table_ref), custom_call_target="tpu_custom_call" | custom-call | tf_op jit(solution)/shard_map/pallas_call | solution.py:143
  211.7 4.1 %convolution_convert_fusion.1 = bf16[64,5120]{1,0:T(8,128)(2,1)S(1)} fusion(bf16[640,5120]{1,0:T(8,128)(2,1)} %param.21, bf16[8,8,5,128]{3,2,1,0:T(8,128)(2,1)S(1)} %bitcast.245), kind=kOutput, calls=%fused_computation.15 | convolution fusion | flops 419758080 | bytes 7290880 | tf_op jit(solution)/shard_map/rqh,hm->rqm/dot_general | solution.py:372
  223.2 2.6 collective-permute-start.8
  226.4 4.6 %copy.212.valid_ref = f32[1,32,256,1]{3,2,1,0:T(8,128)} copy(f32[1,32,256,1]{1,2,3,0:T(8,128)S(1)} %get-tuple-element.58) | data formatting | bytes 65536 | tf_op jit(solution)/shard_map/broadcast_in_dim | solution.py:142
  231.1 46.8 %all-to-all-done.1 = bf16[32,4,4,1,2,16,128]{6,5,4,2,1,3,0:T(8,128)(2,1)} async-done(((bf16[32,4,4,1,2,16,128]{6,5,4,2,1,3,0:T(8,128)(2,1)}), bf16[32,4,4,1,2,16,128]{6,5,4,2,1,3,0:T(8,128)(2,1)}, u32[]{:S(2)}, u32[]{:S(2)}) %all-to-all-start.1) | async-done | bytes 4194336 | tf_op jit(solution)/shard_map/all_to_all | solution.py:339
  277.8 20.0 %shard_map.110 = (f32[1,1,320]{2,1,0:T(1,128)}, f32[1,1,320]{2,1,0:T(1,128)}, f32[1,128,320]{2,1,0:T(8,128)}) custom-call(bf16[1,320,128]{2,1,0:T(8,128)(2,1)} %slice.160.q_ref, bf16[32,1,16,2,16,128]{5,4,3,2,1,0:T(8,128)(2,1)} %bitcast.91.kv_ref, f32[1,32,256,1]{3,2,1,0:T(8,128)} %copy.212.valid_ref, f32[1,8,128]{2,1,0:T(8,128)} %get-tuple-element.76.table_ref), custom_call_target="tpu_custom_call" | custom-call | tf_op jit(solution)/shard_map/pallas_call | solution.py:143
  301.1 4.3 %convolution_convert_fusion = bf16[64,5120]{1,0:T(8,128)(2,1)S(1)} fusion(bf16[640,5120]{1,0:T(8,128)(2,1)} %param.21, bf16[8,8,5,128]{3,2,1,0:T(8,128)(2,1)S(1)} %bitcast.246), kind=kOutput, calls=%fused_computation.14 | convolution fusion | flops 419758080 | bytes 7290880 | tf_op jit(solution)/shard_map/rqh,hm->rqm/dot_general | solution.py:372
  305.5 14.7 %all_to_all.15 = bf16[8,1,64,640]{3,2,1,0:T(8,128)(2,1)S(1)} all-to-all(bf16[8,1,64,640]{3,2,1,0:T(8,128)(2,1)S(1)} %bitcast.238), channel_id=1, replica_groups=mesh['pool'=32,'tp'=8] {'tp'}, dimensions={0} | all-to-all | bytes 1310720 | tf_op jit(solution)/shard_map/all_to_all | solution.py:386
  (183 shorter events, 58.2 us)
Async XLA Ops:
  0.0 56.1 %collective-permute-start = (bf16[2,4,104,640]{3,2,1,0:T(8,128)(2,1)}, bf16[2,4,104,640]{3,2,1,0:T(8,128)(2,1)}, u32[]{:S(2)}, u32[]{:S(2)}) collective-permute-start(bf16[2,4,104,640]{3,2,1,0:T(8,128)(2,1)} %param.19), channel_id=1, source_target_pairs={{0,1},{1,0},{2,3},{3,2},{4,5},{5,4},{6,7},{7,6},{8,9},{9,8},{10,11... | collective-permute-start | bytes 3194888 | tf_op jit(solution)/shard_map/ppermute | solution.py:268
  11.5 11.4 %copy-start.15 = (s32[64,4]{0,1:T(4,128)S(1)}, s32[64,4]{0,1:T(4,128)}, u32[]{:S(2)}) copy-start(s32[64,4]{0,1:T(4,128)} %param.13) | copy-start | bytes 3076
  11.5 11.4 %copy-start.17 = (s32[64,4]{0,1:T(4,128)S(1)}, s32[64,4]{0,1:T(4,128)}, u32[]{:S(2)}) copy-start(s32[64,4]{0,1:T(4,128)} %param.14) | copy-start | bytes 3076
  11.5 11.5 %copy-start.22 = (s32[64]{0:T(128)S(1)}, s32[64]{0:T(128)}, u32[]{:S(2)}) copy-start(s32[64]{0:T(128)} %param.16) | copy-start | bytes 772
  11.5 12.4 %copy-start.2 = (s32[64,128]{1,0:T(8,128)S(1)}, s32[64,128]{1,0:T(8,128)}, u32[]{:S(2)}) copy-start(s32[64,128]{1,0:T(8,128)} %param.12) | copy-start | bytes 98308
  11.5 20.2 %copy-start.11 = (bf16[2,64,2,1,128]{4,2,3,1,0:T(2,128)(2,1)S(1)}, bf16[2,64,2,1,128]{4,2,3,1,0:T(2,128)(2,1)}, u32[]{:S(2)}) copy-start(bf16[2,64,2,1,128]{4,2,3,1,0:T(2,128)(2,1)} %param.18) | copy-start | bytes 196612
  11.5 160.5 %all-to-all-start = ((bf16[32,4,4,1,2,16,128]{6,5,4,2,1,3,0:T(8,128)(2,1)}), bf16[32,4,4,1,2,16,128]{6,5,4,2,1,3,0:T(8,128)(2,1)}, u32[]{:S(2)}, u32[]{:S(2)}) async-start(bf16[32,4,4,1,2,16,128]{6,5,4,2,1,3,0:T(8,128)(2,1)} %bitcast.230), calls=%async_computation | async-start | bytes 8388608 | tf_op jit(solution)/shard_map/all_to_all | solution.py:339
  21.3 34.8 %copy-start.3 = (bf16[2,4,104,640]{3,2,1,0:T(8,128)(2,1)S(1)}, bf16[2,4,104,640]{3,2,1,0:T(8,128)(2,1)}, u32[]{:S(2)}) copy-start(bf16[2,4,104,640]{3,2,1,0:T(8,128)(2,1)} %param.19) | copy-start | bytes 3194884
  58.9 49.0 %collective-permute-start.1 = (bf16[2,2,4,104,640]{4,3,2,1,0:T(8,128)(2,1)}, bf16[2,2,4,104,640]{4,3,2,1,0:T(8,128)(2,1)}, u32[]{:S(2)}, u32[]{:S(2)}) collective-permute-start(bf16[2,2,4,104,640]{4,3,2,1,0:T(8,128)(2,1)} %pad_maximum_fusion), channel_id=1, source_target_pairs={{0,2},{1,3},{2,4},{3,5},{4,6},{5,7},{6,0},{7,1},{8,10},{9,11},{10,... | collective-permute-start | bytes 6389768 | tf_op jit(solution)/shard_map/ppermute | solution.py:274
  60.3 94.2 %collective-permute-start.2 = (bf16[2,2,4,104,640]{4,3,2,1,0:T(8,128)(2,1)}, bf16[2,2,4,104,640]{4,3,2,1,0:T(8,128)(2,1)}, u32[]{:S(2)}, u32[]{:S(2)}) collective-permute-start(bf16[2,2,4,104,640]{4,3,2,1,0:T(8,128)(2,1)} %pad_maximum_fusion), channel_id=1, source_target_pairs={{0,4},{1,5},{2,6},{3,7},{4,0},{5,1},{6,2},{7,3},{8,12},{9,13},{10,... | collective-permute-start | bytes 6389768 | tf_op jit(solution)/shard_map/ppermute | solution.py:274
  62.7 93.7 %collective-permute-start.3 = (bf16[2,2,4,104,640]{4,3,2,1,0:T(8,128)(2,1)}, bf16[2,2,4,104,640]{4,3,2,1,0:T(8,128)(2,1)}, u32[]{:S(2)}, u32[]{:S(2)}) collective-permute-start(bf16[2,2,4,104,640]{4,3,2,1,0:T(8,128)(2,1)} %pad_maximum_fusion), channel_id=1, source_target_pairs={{0,6},{1,7},{2,0},{3,1},{4,2},{5,3},{6,4},{7,5},{8,14},{9,15},{10,... | collective-permute-start | bytes 6389768 | tf_op jit(solution)/shard_map/ppermute | solution.py:274
  171.9 39.4 %copy-start.5 = (f32[2,64,1,5,128]{4,1,3,0,2:T(8,128)}, f32[2,64,1,5,128]{4,1,3,0,2:T(8,128)S(1)}, u32[]{:S(2)}) copy-start(f32[2,64,1,5,128]{4,1,3,0,2:T(8,128)S(1)} %convolution_bitcast_fusion) | copy-start | bytes 983044
  172.0 11.3 %copy-start.8 = (f32[2,32,4,4,16]{1,4,3,2,0:T(8,128)S(1)}, f32[2,32,4,4,16]{1,4,3,2,0:T(8,128)}, u32[]{:S(2)}) copy-start(f32[2,32,4,4,16]{1,4,3,2,0:T(8,128)} %copy.197) | copy-start | bytes 196612
  172.0 105.8 %all-to-all-start.1 = ((bf16[32,4,4,1,2,16,128]{6,5,4,2,1,3,0:T(8,128)(2,1)}), bf16[32,4,4,1,2,16,128]{6,5,4,2,1,3,0:T(8,128)(2,1)}, u32[]{:S(2)}, u32[]{:S(2)}) async-start(bf16[32,4,4,1,2,16,128]{6,5,4,2,1,3,0:T(8,128)(2,1)} %bitcast.231), calls=%async_computation.1 | async-start | bytes 8388608 | tf_op jit(solution)/shard_map/all_to_all | solution.py:339
  188.5 22.9 %copy-start.7 = (f32[2,64,1,5,128]{4,1,3,0,2:T(8,128)S(1)}, f32[2,64,1,5,128]{4,1,3,0,2:T(8,128)}, u32[]{:S(2)}) copy-start(f32[2,64,1,5,128]{4,1,3,0,2:T(8,128)} %convolution_bitcast_fusion.1) | copy-start | bytes 983044
  216.8 6.4 %collective-permute-start.10 = (bf16[1,64,640]{2,1,0:T(8,128)(2,1)S(1)}, bf16[1,64,640]{2,1,0:T(8,128)(2,1)S(1)}, u32[]{:S(2)}, u32[]{:S(2)}) collective-permute-start(bf16[1,64,640]{2,1,0:T(8,128)(2,1)S(1)} %get-tuple-element.46), channel_id=1, source_target_pairs={{0,7},{1,0},{2,1},{3,2},{4,3},{5,4},{6,5},{7,6},{8,15},{9,8},{10,9... | collective-permute-start | bytes 245768 | tf_op jit(solution)/shard_map/ppermute | solution.py:379
  218.7 7.2 %collective-permute-start.4 = (bf16[1,64,640]{2,1,0:T(8,128)(2,1)S(1)}, bf16[1,64,640]{2,1,0:T(8,128)(2,1)S(1)}, u32[]{:S(2)}, u32[]{:S(2)}) collective-permute-start(bf16[1,64,640]{2,1,0:T(8,128)(2,1)S(1)} %get-tuple-element.45), channel_id=1, source_target_pairs={{0,1},{1,2},{2,3},{3,4},{4,5},{5,6},{6,7},{7,0},{8,9},{9,10},{10,1... | collective-permute-start | bytes 245768 | tf_op jit(solution)/shard_map/ppermute | solution.py:379
  219.4 11.6 %collective-permute-start.5 = (bf16[1,64,640]{2,1,0:T(8,128)(2,1)S(1)}, bf16[1,64,640]{2,1,0:T(8,128)(2,1)S(1)}, u32[]{:S(2)}, u32[]{:S(2)}) collective-permute-start(bf16[1,64,640]{2,1,0:T(8,128)(2,1)S(1)} %get-tuple-element.51), channel_id=1, source_target_pairs={{0,2},{1,3},{2,4},{3,5},{4,6},{5,7},{6,0},{7,1},{8,10},{9,11},{10,... | collective-permute-start | bytes 245768 | tf_op jit(solution)/shard_map/ppermute | solution.py:379
  219.6 11.4 %collective-permute-start.6 = (bf16[1,64,640]{2,1,0:T(8,128)(2,1)S(1)}, bf16[1,64,640]{2,1,0:T(8,128)(2,1)S(1)}, u32[]{:S(2)}, u32[]{:S(2)}) collective-permute-start(bf16[1,64,640]{2,1,0:T(8,128)(2,1)S(1)} %get-tuple-element.50), channel_id=1, source_target_pairs={{0,3},{1,4},{2,5},{3,6},{4,7},{5,0},{6,1},{7,2},{8,11},{9,12},{10,... | collective-permute-start | bytes 245768 | tf_op jit(solution)/shard_map/ppermute | solution.py:379
  221.5 9.5 %collective-permute-start.7 = (bf16[1,64,640]{2,1,0:T(8,128)(2,1)S(1)}, bf16[1,64,640]{2,1,0:T(8,128)(2,1)S(1)}, u32[]{:S(2)}, u32[]{:S(2)}) collective-permute-start(bf16[1,64,640]{2,1,0:T(8,128)(2,1)S(1)} %get-tuple-element.49), channel_id=1, source_target_pairs={{0,4},{1,5},{2,6},{3,7},{4,0},{5,1},{6,2},{7,3},{8,12},{9,13},{10,... | collective-permute-start | bytes 245768 | tf_op jit(solution)/shard_map/ppermute | solution.py:379
  223.2 7.8 %collective-permute-start.8 = (bf16[1,64,640]{2,1,0:T(8,128)(2,1)S(1)}, bf16[1,64,640]{2,1,0:T(8,128)(2,1)S(1)}, u32[]{:S(2)}, u32[]{:S(2)}) collective-permute-start(bf16[1,64,640]{2,1,0:T(8,128)(2,1)S(1)} %get-tuple-element.48), channel_id=1, source_target_pairs={{0,5},{1,6},{2,7},{3,0},{4,1},{5,2},{6,3},{7,4},{8,13},{9,14},{10,... | collective-permute-start | bytes 245768 | tf_op jit(solution)/shard_map/ppermute | solution.py:379
  225.8 5.2 %collective-permute-start.9 = (bf16[1,64,640]{2,1,0:T(8,128)(2,1)S(1)}, bf16[1,64,640]{2,1,0:T(8,128)(2,1)S(1)}, u32[]{:S(2)}, u32[]{:S(2)}) collective-permute-start(bf16[1,64,640]{2,1,0:T(8,128)(2,1)S(1)} %get-tuple-element.47), channel_id=1, source_target_pairs={{0,6},{1,7},{2,0},{3,1},{4,2},{5,3},{6,4},{7,5},{8,14},{9,15},{10,... | collective-permute-start | bytes 245768 | tf_op jit(solution)/shard_map/ppermute | solution.py:379
  277.8 22.8 %copy-start.6 = (f32[2,64,1,5,128]{4,1,3,0,2:T(8,128)S(1)}, f32[2,64,1,5,128]{4,1,3,0,2:T(8,128)}, u32[]{:S(2)}) copy-start(f32[2,64,1,5,128]{4,1,3,0,2:T(8,128)} %copy-done.5) | copy-start | bytes 983044
  301.1 20.0 %copy-start.1 = (bf16[256,1,2,16,128]{4,3,2,1,0:T(8,128)(2,1)S(1)}, bf16[256,1,2,16,128]{4,3,2,1,0:T(8,128)(2,1)}, u32[]{:S(2)}) copy-start(bf16[256,1,2,16,128]{4,3,2,1,0:T(8,128)(2,1)} %param.11) | copy-start | bytes 6291460
  (12 other events, 58.4 us)

commit v13 on v11

--- a/solution.py
+++ b/solution.py
@@ -72,7 +72,7 @@
     return THETA ** (-(jnp.arange(halfway, dtype=jnp.float32) * 2.0) / head_dim)
 
 
-SET_BLOCK = 8
+SET_BLOCK = 16
 
 
 def cached_kernel(scale, q_ref, kv_ref, valid_ref, table_ref, peak_ref, sum_ref, num_ref, m_acc, w_acc, n_acc):

time: 271 us -> 271 us (level)
  transfers between devices with their start and end apart: 16 -> 16, of which waited for: 4 -> 4; matrix products, arithmetic and copies ran while one was open for 32% -> 32% of each run, Pallas kernels for 7% -> 8%
where the time goes in v13:
time: 271 us
  waiting for transfers between devices  80.4 us (30%)
  local copies, waits for them, and re-layouts  44.6 us (16%)
  Pallas kernels  41.1 us (15%)
  other arithmetic  38.1 us (14%)
  starting transfers between devices  34.2 us (13%)
  blocking collectives  18.4 us (7%)
  matrix products  12.9 us (5%)
    all_to_all x2, waiting for transfers between devices, shards(): lax.all_to_all(outgoing, 'pool', split_axis=0, concat_axis=0, tiled=True)  41.7 us
    pallas_call x2, Pallas kernels, cached_attention(): pl.pallas_call(functools.partial(cached_kernel, scale), grid=(req_dev, po...  41.1 us
    ppermute x7, waiting for transfers between devices, shards(): lax.ppermute(recompute_hidden, 'tp', [(i, (i + k) % tp_count) for i in ra...  38.3 us
    reduce_or x1, other arithmetic, shards(): jnp.any(row_ids[..., None] == own_rows[:, :, None, None, None, :], axis=-1)  20.4 us
    all_to_all x1, blocking collectives, shards(): lax.all_to_all(pieces.transpose(2, 0, 1, 3), 'tp', split_axis=0, concat_a...  18.4 us
    all_to_all x2, starting transfers between devices, shards(): lax.all_to_all(outgoing, 'pool', split_axis=0, concat_axis=0, tiled=True)  15.3 us
    ppermute x7, starting transfers between devices, shards(): lax.ppermute(recompute_hidden, 'tp', [(i, (i + k) % tp_count) for i in ra...  10.5 us
    broadcast_in_dim x3, local copies, waits for them, and re-layouts, cached_attention(): valid = valid[..., None]  9.08 us
  transfers between devices with their start and end apart: 16, of which 4 were waited for; matrix products, arithmetic and copies ran while one was open for 32% of the time, Pallas kernels for 8%

profile of v13, /device:TPU:1, one launch (start us, length us, event | category | flops | bytes accessed | tf_op | source)
XLA Modules:
  0.0 270.6 jit_solution(17384035934244309609)
XLA Ops:
  0.0 2.6 collective-permute-start
  7.0 2.6 collective-permute-start.4
  14.4 3.5 %gather_fusion.1 = bf16[512,2,16,128]{3,2,1,0:T(8,128)(2,1)} fusion(bf16[256,2,16,128]{3,2,1,0:T(8,128)(2,1)S(1)} %bitcast.224, s32[1024]{0:T(1024)S(1)} %get-tuple-element.96), kind=kCustom, calls=%fused_computation.1 | custom fusion | bytes 8390656 | tf_op jit(solution)/shard_map/gather | solution.py:332
  17.9 9.8 %all-to-all-start = ((bf16[32,4,4,1,2,16,128]{6,5,4,2,1,3,0:T(8,128)(2,1)}), bf16[32,4,4,1,2,16,128]{6,5,4,2,1,3,0:T(8,128)(2,1)}, u32[]{:S(2)}, u32[]{:S(2)}) async-start(bf16[32,4,4,1,2,16,128]{6,5,4,2,1,3,0:T(8,128)(2,1)} %bitcast.227), calls=%async_computation | async-start | bytes 8388608 | tf_op jit(solution)/shard_map/all_to_all | solution.py:335
  28.9 2.3 reduce_window_sum.23
  34.0 20.4 %compare_reduce_fusion = pred[2,4,32,4,16]{4,3,2,1,0:T(4,128)(4,1)S(1)} fusion(s32[2,4,104]{2,1,0:T(4,128)S(1)} %get-tuple-element.42, s32[2,4,32,4,16]{4,3,2,1,0:T(4,128)S(1)} %iota_add_fusion), kind=kLoop, calls=%fused_computation.13 | loop fusion | flops 3391488 | bytes 85248 | tf_op jit(solution)/shard_map/reduce_or | solution.py:314
  55.2 2.0 copy.187
  58.1 3.5 %gather_fusion.2 = bf16[512,2,16,128]{3,2,1,0:T(8,128)(2,1)} fusion(bf16[256,2,16,128]{3,2,1,0:T(8,128)(2,1)S(1)} %bitcast.225, s32[1024]{0:T(1024)S(1)} %get-tuple-element.95), kind=kCustom, calls=%fused_computation.2 | custom fusion | bytes 8390656 | tf_op jit(solution)/shard_map/gather | solution.py:332
  61.6 4.2 %gather_fusion.3 = bf16[8,640,2,128]{3,1,2,0:T(8,128)(2,1)} fusion(bf16[8,640,2,128]{3,1,2,0:T(8,128)(2,1)} %copy.187, s32[1024]{0:T(1024)S(1)} %pad_clamp_fusion.2), kind=kCustom, calls=%fused_computation.3 | custom fusion | bytes 5242912 | tf_op jit(solution)/shard_map/jit(_take)/gather | solution.py:273
  68.6 29.4 %collective-permute-done.1 = bf16[2,4,104,640]{3,2,1,0:T(8,128)(2,1)} collective-permute-done((bf16[2,4,104,640]{3,2,1,0:T(8,128)(2,1)}, bf16[2,4,104,640]{3,2,1,0:T(8,128)(2,1)}, u32[]{:S(2)}, u32[]{:S(2)}) %collective-permute-start.1) | collective-permute-done | bytes 1064992 | tf_op jit(solution)/shard_map/ppermute | solution.py:269
  103.9 8.9 %collective-permute-done.6 = bf16[2,4,104,640]{3,2,1,0:T(8,128)(2,1)S(1)} collective-permute-done((bf16[2,4,104,640]{3,2,1,0:T(8,128)(2,1)S(1)}, bf16[2,4,104,640]{3,2,1,0:T(8,128)(2,1)S(1)}, u32[]{:S(2)}, u32[]{:S(2)}) %collective-permute-start.6) | collective-permute-done | bytes 1064992 | tf_op jit(solution)/shard_map/ppermute | solution.py:269
  114.8 3.0 %fusion.7 = f32[2,4,104,2,1,128]{5,2,3,1,0,4:T(8,128)S(1)} fusion(bf16[8,2,4,104,640]{4,3,2,1,0:T(8,128)(2,1)S(1)} %bitcast_dynamic-update-slice_fusion, f32[2,4,104]{2,1,0:T(4,128)S(1)} %add_rsqrt_fusion, bf16[8,640,2,128]{3,1,2,0:T(8,128)(2,1)S(1)} %copy-done.8, pred[8]{0:T(512)(128)(4,1)S(1)} %compare_and_fusion.1), kind=kOutput, calls=%fused_computation.20 | convolution fusion | flops 2195128320 | bytes 11996424 | tf_op jit(solution)/shard_map/trcnd,tdskh->rcnskh/dot_general | solution.py:281
  120.2 2.0 copy.191
  122.2 1.9 reshape.676
  124.9 5.5 %all-to-all-start.1 = ((bf16[32,4,4,1,2,16,128]{6,5,4,2,1,3,0:T(8,128)(2,1)}), bf16[32,4,4,1,2,16,128]{6,5,4,2,1,3,0:T(8,128)(2,1)}, u32[]{:S(2)}, u32[]{:S(2)}) async-start(bf16[32,4,4,1,2,16,128]{6,5,4,2,1,3,0:T(8,128)(2,1)} %bitcast.226), calls=%async_computation.1 | async-start | bytes 8388608 | tf_op jit(solution)/shard_map/all_to_all | solution.py:335
  132.6 4.5 %copy.202.valid_ref = f32[1,32,256,1]{3,2,1,0:T(8,128)} copy(f32[1,32,256,1]{1,2,3,0:T(8,128)S(1)} %get-tuple-element.59) | data formatting | bytes 65536 | tf_op jit(solution)/shard_map/broadcast_in_dim | solution.py:142
  137.8 20.5 %shard_map.109 = (f32[1,1,320]{2,1,0:T(1,128)}, f32[1,1,320]{2,1,0:T(1,128)}, f32[1,128,320]{2,1,0:T(8,128)}) custom-call(bf16[1,320,128]{2,1,0:T(8,128)(2,1)} %slice.141.q_ref, bf16[32,1,16,2,16,128]{5,4,3,2,1,0:T(8,128)(2,1)} %bitcast.64.kv_ref, f32[1,32,256,1]{3,2,1,0:T(8,128)} %copy.202.valid_ref, f32[1,8,128]{2,1,0:T(8,128)} %get-tuple-element.77.table_ref), custom_call_target="tpu_custom_call" | custom-call | tf_op jit(solution)/shard_map/pallas_call | solution.py:143
  161.6 4.1 %convolution_convert_fusion.1 = bf16[64,5120]{1,0:T(8,128)(2,1)S(1)} fusion(bf16[640,5120]{1,0:T(8,128)(2,1)} %param.21, bf16[8,8,5,128]{3,2,1,0:T(8,128)(2,1)S(1)} %bitcast.240), kind=kOutput, calls=%fused_computation.15 | convolution fusion | flops 419758080 | bytes 7290880 | tf_op jit(solution)/shard_map/rqh,hm->rqm/dot_general | solution.py:368
  168.3 2.4 collective-permute-start.11
  176.5 4.5 %copy.212.valid_ref = f32[1,32,256,1]{3,2,1,0:T(8,128)} copy(f32[1,32,256,1]{1,2,3,0:T(8,128)S(1)} %get-tuple-element.58) | data formatting | bytes 65536 | tf_op jit(solution)/shard_map/broadcast_in_dim | solution.py:142
  181.5 41.7 %all-to-all-done.1 = bf16[32,4,4,1,2,16,128]{6,5,4,2,1,3,0:T(8,128)(2,1)} async-done(((bf16[32,4,4,1,2,16,128]{6,5,4,2,1,3,0:T(8,128)(2,1)}), bf16[32,4,4,1,2,16,128]{6,5,4,2,1,3,0:T(8,128)(2,1)}, u32[]{:S(2)}, u32[]{:S(2)}) %all-to-all-start.1) | async-done | bytes 4194336 | tf_op jit(solution)/shard_map/all_to_all | solution.py:335
  223.1 20.6 %shard_map.110 = (f32[1,1,320]{2,1,0:T(1,128)}, f32[1,1,320]{2,1,0:T(1,128)}, f32[1,128,320]{2,1,0:T(8,128)}) custom-call(bf16[1,320,128]{2,1,0:T(8,128)(2,1)} %slice.160.q_ref, bf16[32,1,16,2,16,128]{5,4,3,2,1,0:T(8,128)(2,1)} %bitcast.85.kv_ref, f32[1,32,256,1]{3,2,1,0:T(8,128)} %copy.212.valid_ref, f32[1,8,128]{2,1,0:T(8,128)} %get-tuple-element.76.table_ref), custom_call_target="tpu_custom_call" | custom-call | tf_op jit(solution)/shard_map/pallas_call | solution.py:143
  247.0 4.3 %convolution_convert_fusion = bf16[64,5120]{1,0:T(8,128)(2,1)S(1)} fusion(bf16[640,5120]{1,0:T(8,128)(2,1)} %param.21, bf16[8,8,5,128]{3,2,1,0:T(8,128)(2,1)S(1)} %bitcast.241), kind=kOutput, calls=%fused_computation.14 | convolution fusion | flops 419758080 | bytes 7290880 | tf_op jit(solution)/shard_map/rqh,hm->rqm/dot_general | solution.py:368
  251.4 18.4 %all_to_all.15 = bf16[8,1,64,640]{3,2,1,0:T(8,128)(2,1)S(1)} all-to-all(bf16[8,1,64,640]{3,2,1,0:T(8,128)(2,1)S(1)} %bitcast.233), channel_id=1, replica_groups=mesh['pool'=32,'tp'=8] {'tp'}, dimensions={0} | all-to-all | bytes 1310720 | tf_op jit(solution)/shard_map/all_to_all | solution.py:382
  (178 shorter events, 47.3 us)
Async XLA Ops:
  0.0 66.3 %collective-permute-start = (bf16[2,4,104,640]{3,2,1,0:T(8,128)(2,1)}, bf16[2,4,104,640]{3,2,1,0:T(8,128)(2,1)}, u32[]{:S(2)}, u32[]{:S(2)}) collective-permute-start(bf16[2,4,104,640]{3,2,1,0:T(8,128)(2,1)} %param.19), channel_id=1, source_target_pairs={{0,1},{1,2},{2,3},{3,4},{4,5},{5,6},{6,7},{7,0},{8,9},{9,10},{10,1... | collective-permute-start | bytes 3194888 | tf_op jit(solution)/shard_map/ppermute | solution.py:269
  2.6 95.4 %collective-permute-start.1 = (bf16[2,4,104,640]{3,2,1,0:T(8,128)(2,1)}, bf16[2,4,104,640]{3,2,1,0:T(8,128)(2,1)}, u32[]{:S(2)}, u32[]{:S(2)}) collective-permute-start(bf16[2,4,104,640]{3,2,1,0:T(8,128)(2,1)} %param.19), channel_id=1, source_target_pairs={{0,2},{1,3},{2,4},{3,5},{4,6},{5,7},{6,0},{7,1},{8,10},{9,11},{10,... | collective-permute-start | bytes 3194888 | tf_op jit(solution)/shard_map/ppermute | solution.py:269
  3.8 95.6 %collective-permute-start.2 = (bf16[2,4,104,640]{3,2,1,0:T(8,128)(2,1)}, bf16[2,4,104,640]{3,2,1,0:T(8,128)(2,1)}, u32[]{:S(2)}, u32[]{:S(2)}) collective-permute-start(bf16[2,4,104,640]{3,2,1,0:T(8,128)(2,1)} %param.19), channel_id=1, source_target_pairs={{0,3},{1,4},{2,5},{3,6},{4,7},{5,0},{6,1},{7,2},{8,11},{9,12},{10,... | collective-permute-start | bytes 3194888 | tf_op jit(solution)/shard_map/ppermute | solution.py:269
  5.4 95.5 %collective-permute-start.3 = (bf16[2,4,104,640]{3,2,1,0:T(8,128)(2,1)}, bf16[2,4,104,640]{3,2,1,0:T(8,128)(2,1)}, u32[]{:S(2)}, u32[]{:S(2)}) collective-permute-start(bf16[2,4,104,640]{3,2,1,0:T(8,128)(2,1)} %param.19), channel_id=1, source_target_pairs={{0,4},{1,5},{2,6},{3,7},{4,0},{5,1},{6,2},{7,3},{8,12},{9,13},{10,... | collective-permute-start | bytes 3194888 | tf_op jit(solution)/shard_map/ppermute | solution.py:269
  7.0 95.3 %collective-permute-start.4 = (bf16[2,4,104,640]{3,2,1,0:T(8,128)(2,1)}, bf16[2,4,104,640]{3,2,1,0:T(8,128)(2,1)}, u32[]{:S(2)}, u32[]{:S(2)}) collective-permute-start(bf16[2,4,104,640]{3,2,1,0:T(8,128)(2,1)} %param.19), channel_id=1, source_target_pairs={{0,5},{1,6},{2,7},{3,0},{4,1},{5,2},{6,3},{7,4},{8,13},{9,14},{10,... | collective-permute-start | bytes 3194888 | tf_op jit(solution)/shard_map/ppermute | solution.py:269
  17.9 107.0 %all-to-all-start = ((bf16[32,4,4,1,2,16,128]{6,5,4,2,1,3,0:T(8,128)(2,1)}), bf16[32,4,4,1,2,16,128]{6,5,4,2,1,3,0:T(8,128)(2,1)}, u32[]{:S(2)}, u32[]{:S(2)}) async-start(bf16[32,4,4,1,2,16,128]{6,5,4,2,1,3,0:T(8,128)(2,1)} %bitcast.227), calls=%async_computation | async-start | bytes 8388608 | tf_op jit(solution)/shard_map/all_to_all | solution.py:335
  32.0 23.2 %copy-start.3 = (bf16[5120,2,1,128]{3,1,2,0:T(2,128)(2,1)S(1)}, bf16[5120,2,1,128]{3,1,2,0:T(2,128)(2,1)}, u32[]{:S(2)}) copy-start(bf16[5120,2,1,128]{3,1,2,0:T(2,128)(2,1)} %param.20) | copy-start | bytes 7864324
  54.8 64.9 %copy-start.4 = (bf16[2,64,5,64]{3,1,2,0:T(8,128)(2,1)}, bf16[2,64,5,64]{3,1,2,0:T(8,128)(2,1)S(1)}, u32[]{:S(2)}) copy-start(bf16[2,64,5,64]{3,1,2,0:T(8,128)(2,1)S(1)} %get-tuple-element.54) | copy-start | bytes 245764
  54.8 64.9 %copy-start.6 = (bf16[2,64,5,64]{3,1,2,0:T(8,128)(2,1)}, bf16[2,64,5,64]{3,1,2,0:T(8,128)(2,1)S(1)}, u32[]{:S(2)}) copy-start(bf16[2,64,5,64]{3,1,2,0:T(8,128)(2,1)S(1)} %get-tuple-element.55) | copy-start | bytes 245764
  66.2 95.0 %copy-start.11 = (f32[2,64,1,5,128]{4,1,3,0,2:T(8,128)}, f32[2,64,1,5,128]{4,1,3,0,2:T(8,128)S(1)}, u32[]{:S(2)}) copy-start(f32[2,64,1,5,128]{4,1,3,0,2:T(8,128)S(1)} %convolution_bitcast_fusion.1) | copy-start | bytes 983044
  66.3 37.4 %collective-permute-start.5 = (bf16[2,4,104,640]{3,2,1,0:T(8,128)(2,1)S(1)}, bf16[2,4,104,640]{3,2,1,0:T(8,128)(2,1)S(1)}, u32[]{:S(2)}, u32[]{:S(2)}) collective-permute-start(bf16[2,4,104,640]{3,2,1,0:T(8,128)(2,1)S(1)} %copy-done.13), channel_id=1, source_target_pairs={{0,6},{1,7},{2,0},{3,1},{4,2},{5,3},{6,4},{7,5},{8,14},{9,15},{10,... | collective-permute-start | bytes 3194888 | tf_op jit(solution)/shard_map/ppermute | solution.py:269
  98.0 14.8 %collective-permute-start.6 = (bf16[2,4,104,640]{3,2,1,0:T(8,128)(2,1)S(1)}, bf16[2,4,104,640]{3,2,1,0:T(8,128)(2,1)S(1)}, u32[]{:S(2)}, u32[]{:S(2)}) collective-permute-start(bf16[2,4,104,640]{3,2,1,0:T(8,128)(2,1)S(1)} %copy-done.13), channel_id=1, source_target_pairs={{0,7},{1,0},{2,1},{3,2},{4,3},{5,4},{6,5},{7,6},{8,15},{9,8},{10,9... | collective-permute-start | bytes 3194888 | tf_op jit(solution)/shard_map/ppermute | solution.py:269
  124.9 36.3 %copy-start.9 = (f32[2,64,1,5,128]{4,1,3,0,2:T(8,128)}, f32[2,64,1,5,128]{4,1,3,0,2:T(8,128)S(1)}, u32[]{:S(2)}) copy-start(f32[2,64,1,5,128]{4,1,3,0,2:T(8,128)S(1)} %convolution_bitcast_fusion) | copy-start | bytes 983044
  124.9 98.2 %all-to-all-start.1 = ((bf16[32,4,4,1,2,16,128]{6,5,4,2,1,3,0:T(8,128)(2,1)}), bf16[32,4,4,1,2,16,128]{6,5,4,2,1,3,0:T(8,128)(2,1)}, u32[]{:S(2)}, u32[]{:S(2)}) async-start(bf16[32,4,4,1,2,16,128]{6,5,4,2,1,3,0:T(8,128)(2,1)} %bitcast.226), calls=%async_computation.1 | async-start | bytes 8388608 | tf_op jit(solution)/shard_map/all_to_all | solution.py:335
  166.6 7.3 %collective-permute-start.10 = (bf16[1,64,640]{2,1,0:T(8,128)(2,1)S(1)}, bf16[1,64,640]{2,1,0:T(8,128)(2,1)S(1)}, u32[]{:S(2)}, u32[]{:S(2)}) collective-permute-start(bf16[1,64,640]{2,1,0:T(8,128)(2,1)S(1)} %get-tuple-element.49), channel_id=1, source_target_pairs={{0,4},{1,5},{2,6},{3,7},{4,0},{5,1},{6,2},{7,3},{8,12},{9,13},{10,... | collective-permute-start | bytes 245768 | tf_op jit(solution)/shard_map/ppermute | solution.py:375
  168.3 6.3 %collective-permute-start.11 = (bf16[1,64,640]{2,1,0:T(8,128)(2,1)S(1)}, bf16[1,64,640]{2,1,0:T(8,128)(2,1)S(1)}, u32[]{:S(2)}, u32[]{:S(2)}) collective-permute-start(bf16[1,64,640]{2,1,0:T(8,128)(2,1)S(1)} %get-tuple-element.48), channel_id=1, source_target_pairs={{0,5},{1,6},{2,7},{3,0},{4,1},{5,2},{6,3},{7,4},{8,13},{9,14},{10,... | collective-permute-start | bytes 245768 | tf_op jit(solution)/shard_map/ppermute | solution.py:375
  171.4 9.6 %collective-permute-start.12 = (bf16[1,64,640]{2,1,0:T(8,128)(2,1)S(1)}, bf16[1,64,640]{2,1,0:T(8,128)(2,1)S(1)}, u32[]{:S(2)}, u32[]{:S(2)}) collective-permute-start(bf16[1,64,640]{2,1,0:T(8,128)(2,1)S(1)} %get-tuple-element.47), channel_id=1, source_target_pairs={{0,6},{1,7},{2,0},{3,1},{4,2},{5,3},{6,4},{7,5},{8,14},{9,15},{10,... | collective-permute-start | bytes 245768 | tf_op jit(solution)/shard_map/ppermute | solution.py:375
  172.2 8.9 %collective-permute-start.13 = (bf16[1,64,640]{2,1,0:T(8,128)(2,1)S(1)}, bf16[1,64,640]{2,1,0:T(8,128)(2,1)S(1)}, u32[]{:S(2)}, u32[]{:S(2)}) collective-permute-start(bf16[1,64,640]{2,1,0:T(8,128)(2,1)S(1)} %get-tuple-element.46), channel_id=1, source_target_pairs={{0,7},{1,0},{2,1},{3,2},{4,3},{5,4},{6,5},{7,6},{8,15},{9,8},{10,9... | collective-permute-start | bytes 245768 | tf_op jit(solution)/shard_map/ppermute | solution.py:375
  172.2 8.9 %collective-permute-start.7 = (bf16[1,64,640]{2,1,0:T(8,128)(2,1)S(1)}, bf16[1,64,640]{2,1,0:T(8,128)(2,1)S(1)}, u32[]{:S(2)}, u32[]{:S(2)}) collective-permute-start(bf16[1,64,640]{2,1,0:T(8,128)(2,1)S(1)} %get-tuple-element.45), channel_id=1, source_target_pairs={{0,1},{1,2},{2,3},{3,4},{4,5},{5,6},{6,7},{7,0},{8,9},{9,10},{10,1... | collective-permute-start | bytes 245768 | tf_op jit(solution)/shard_map/ppermute | solution.py:375
  173.9 7.1 %collective-permute-start.8 = (bf16[1,64,640]{2,1,0:T(8,128)(2,1)S(1)}, bf16[1,64,640]{2,1,0:T(8,128)(2,1)S(1)}, u32[]{:S(2)}, u32[]{:S(2)}) collective-permute-start(bf16[1,64,640]{2,1,0:T(8,128)(2,1)S(1)} %get-tuple-element.51), channel_id=1, source_target_pairs={{0,2},{1,3},{2,4},{3,5},{4,6},{5,7},{6,0},{7,1},{8,10},{9,11},{10,... | collective-permute-start | bytes 245768 | tf_op jit(solution)/shard_map/ppermute | solution.py:375
  174.6 6.8 %collective-permute-start.9 = (bf16[1,64,640]{2,1,0:T(8,128)(2,1)S(1)}, bf16[1,64,640]{2,1,0:T(8,128)(2,1)S(1)}, u32[]{:S(2)}, u32[]{:S(2)}) collective-permute-start(bf16[1,64,640]{2,1,0:T(8,128)(2,1)S(1)} %get-tuple-element.50), channel_id=1, source_target_pairs={{0,3},{1,4},{2,5},{3,6},{4,7},{5,0},{6,1},{7,2},{8,11},{9,12},{10,... | collective-permute-start | bytes 245768 | tf_op jit(solution)/shard_map/ppermute | solution.py:375
  223.1 23.5 %copy-start.10 = (f32[2,64,1,5,128]{4,1,3,0,2:T(8,128)S(1)}, f32[2,64,1,5,128]{4,1,3,0,2:T(8,128)}, u32[]{:S(2)}) copy-start(f32[2,64,1,5,128]{4,1,3,0,2:T(8,128)} %copy-done.9) | copy-start | bytes 983044
  223.1 23.5 %copy-start.12 = (f32[2,64,1,5,128]{4,1,3,0,2:T(8,128)S(1)}, f32[2,64,1,5,128]{4,1,3,0,2:T(8,128)}, u32[]{:S(2)}) copy-start(f32[2,64,1,5,128]{4,1,3,0,2:T(8,128)} %copy-done.11) | copy-start | bytes 983044
  247.0 23.6 %copy-start.1 = (bf16[256,1,2,16,128]{4,3,2,1,0:T(8,128)(2,1)S(1)}, bf16[256,1,2,16,128]{4,3,2,1,0:T(8,128)(2,1)}, u32[]{:S(2)}) copy-start(bf16[256,1,2,16,128]{4,3,2,1,0:T(8,128)(2,1)} %param.11) | copy-start | bytes 6291460
  (12 other events, 105.4 us)

commit v14 on v11

--- a/solution.py
+++ b/solution.py
@@ -132,7 +132,7 @@
     def _():
         peak_ref[0] = m_acc[...]
         sum_ref[0] = w_acc[...]
-        num_ref[0] = n_acc[...]
+        num_ref[0] = n_acc[...].T
 
 
 def cached_attention(queries, arrived, valid, tables, scale):
@@ -152,12 +152,12 @@
         out_specs=[
             pl.BlockSpec((1, 1, rows), lambda r, j: (r, 0, 0)),
             pl.BlockSpec((1, 1, rows), lambda r, j: (r, 0, 0)),
-            pl.BlockSpec((1, head_dim, rows), lambda r, j: (r, 0, 0)),
+            pl.BlockSpec((1, rows, head_dim), lambda r, j: (r, 0, 0)),
         ],
         out_shape=[
             jax.ShapeDtypeStruct((req_dev, 1, rows), jnp.float32),
             jax.ShapeDtypeStruct((req_dev, 1, rows), jnp.float32),
-            jax.ShapeDtypeStruct((req_dev, head_dim, rows), jnp.float32),
+            jax.ShapeDtypeStruct((req_dev, rows, head_dim), jnp.float32),
         ],
         scratch_shapes=[
             pltpu.VMEM((1, rows), jnp.float32),
@@ -166,7 +166,7 @@
         ],
         compiler_params=pltpu.CompilerParams(dimension_semantics=("parallel", "arbitrary")),
     )(queries, arrived, valid, tables)
-    return (peak, total, jnp.swapaxes(num, 1, 2))
+    return (peak, total, num)
 
 def shards(
     pool_kv,

time: 271 us -> 271 us (level)
  no operation moved by 1% of the time
where the time goes in v14:
time: 271 us; the launch traced here: 270 us
  waiting for transfers between devices  81 us (30%)
  local copies, waits for them, and re-layouts  42.5 us (16%)
  Pallas kernels  40.1 us (15%)
  other arithmetic  40 us (15%)
  starting transfers between devices  34.2 us (13%)
  blocking collectives  18.4 us (7%)
  matrix products  12.9 us (5%)
    all_to_all x2, waiting for transfers between devices, shards(): lax.all_to_all(outgoing, 'pool', split_axis=0, concat_axis=0, tiled=True)  42.2 us
    pallas_call x2, Pallas kernels, cached_attention(): pl.pallas_call(functools.partial(cached_kernel, scale), grid=(req_dev, po...  40.1 us
    ppermute x7, waiting for transfers between devices, shards(): lax.ppermute(recompute_hidden, 'tp', [(i, (i + k) % tp_count) for i in ra...  38.3 us
    reduce_or x1, other arithmetic, shards(): jnp.any(row_ids[..., None] == own_rows[:, :, None, None, None, :], axis=-1)  20.4 us
    all_to_all x1, blocking collectives, shards(): lax.all_to_all(pieces.transpose(2, 0, 1, 3), 'tp', split_axis=0, concat_a...  18.4 us
    all_to_all x2, starting transfers between devices, shards(): lax.all_to_all(outgoing, 'pool', split_axis=0, concat_axis=0, tiled=True)  15.3 us
    ppermute x7, starting transfers between devices, shards(): lax.ppermute(recompute_hidden, 'tp', [(i, (i + k) % tp_count) for i in ra...  10.5 us
    broadcast_in_dim x3, local copies, waits for them, and re-layouts, cached_attention(): valid = valid[..., None]  9.08 us
  transfers between devices with their start and end apart: 16, of which 4 were waited for; matrix products, arithmetic and copies ran while one was open for 32% of the time, Pallas kernels for 7%

profile of v14, /device:TPU:1, one launch (start us, length us, event | category | flops | bytes accessed | tf_op | source)
XLA Modules:
  0.0 270.0 jit_solution(9018373047462130737)
XLA Ops:
  0.0 2.6 collective-permute-start
  7.0 2.6 collective-permute-start.4
  14.4 3.5 %gather_fusion.1 = bf16[512,2,16,128]{3,2,1,0:T(8,128)(2,1)} fusion(bf16[256,2,16,128]{3,2,1,0:T(8,128)(2,1)S(1)} %bitcast.222, s32[1024]{0:T(1024)S(1)} %get-tuple-element.96), kind=kCustom, calls=%fused_computation.1 | custom fusion | bytes 8390656 | tf_op jit(solution)/shard_map/gather | solution.py:332
  17.9 9.8 %all-to-all-start = ((bf16[32,4,4,1,2,16,128]{6,5,4,2,1,3,0:T(8,128)(2,1)}), bf16[32,4,4,1,2,16,128]{6,5,4,2,1,3,0:T(8,128)(2,1)}, u32[]{:S(2)}, u32[]{:S(2)}) async-start(bf16[32,4,4,1,2,16,128]{6,5,4,2,1,3,0:T(8,128)(2,1)} %bitcast.225), calls=%async_computation | async-start | bytes 8388608 | tf_op jit(solution)/shard_map/all_to_all | solution.py:335
  28.9 2.3 reduce_window_sum.23
  34.0 20.4 %compare_reduce_fusion = pred[2,4,32,4,16]{4,3,2,1,0:T(4,128)(4,1)S(1)} fusion(s32[2,4,104]{2,1,0:T(4,128)S(1)} %get-tuple-element.42, s32[2,4,32,4,16]{4,3,2,1,0:T(4,128)S(1)} %iota_add_fusion), kind=kLoop, calls=%fused_computation.13 | loop fusion | flops 3391488 | bytes 85248 | tf_op jit(solution)/shard_map/reduce_or | solution.py:314
  55.2 2.0 copy.181
  58.1 3.5 %gather_fusion.2 = bf16[512,2,16,128]{3,2,1,0:T(8,128)(2,1)} fusion(bf16[256,2,16,128]{3,2,1,0:T(8,128)(2,1)S(1)} %bitcast.223, s32[1024]{0:T(1024)S(1)} %get-tuple-element.95), kind=kCustom, calls=%fused_computation.2 | custom fusion | bytes 8390656 | tf_op jit(solution)/shard_map/gather | solution.py:332
  61.6 4.2 %gather_fusion.3 = bf16[8,640,2,128]{3,1,2,0:T(8,128)(2,1)} fusion(bf16[8,640,2,128]{3,1,2,0:T(8,128)(2,1)} %copy.181, s32[1024]{0:T(1024)S(1)} %pad_clamp_fusion.2), kind=kCustom, calls=%fused_computation.3 | custom fusion | bytes 5242912 | tf_op jit(solution)/shard_map/jit(_take)/gather | solution.py:273
  68.6 29.4 %collective-permute-done.1 = bf16[2,4,104,640]{3,2,1,0:T(8,128)(2,1)} collective-permute-done((bf16[2,4,104,640]{3,2,1,0:T(8,128)(2,1)}, bf16[2,4,104,640]{3,2,1,0:T(8,128)(2,1)}, u32[]{:S(2)}, u32[]{:S(2)}) %collective-permute-start.1) | collective-permute-done | bytes 1064992 | tf_op jit(solution)/shard_map/ppermute | solution.py:269
  103.9 8.9 %collective-permute-done.6 = bf16[2,4,104,640]{3,2,1,0:T(8,128)(2,1)S(1)} collective-permute-done((bf16[2,4,104,640]{3,2,1,0:T(8,128)(2,1)S(1)}, bf16[2,4,104,640]{3,2,1,0:T(8,128)(2,1)S(1)}, u32[]{:S(2)}, u32[]{:S(2)}) %collective-permute-start.6) | collective-permute-done | bytes 1064992 | tf_op jit(solution)/shard_map/ppermute | solution.py:269
  114.8 3.0 %fusion.7 = f32[2,4,104,2,1,128]{5,2,3,1,0,4:T(8,128)S(1)} fusion(bf16[8,2,4,104,640]{4,3,2,1,0:T(8,128)(2,1)S(1)} %bitcast_dynamic-update-slice_fusion, f32[2,4,104]{2,1,0:T(4,128)S(1)} %add_rsqrt_fusion, bf16[8,640,2,128]{3,1,2,0:T(8,128)(2,1)S(1)} %copy-done.8, pred[8]{0:T(512)(128)(4,1)S(1)} %compare_and_fusion.1), kind=kOutput, calls=%fused_computation.20 | convolution fusion | flops 2195128320 | bytes 11996424 | tf_op jit(solution)/shard_map/trcnd,tdskh->rcnskh/dot_general | solution.py:281
  120.2 2.0 copy.185
  122.2 1.9 reshape.676
  124.9 5.5 %all-to-all-start.1 = ((bf16[32,4,4,1,2,16,128]{6,5,4,2,1,3,0:T(8,128)(2,1)}), bf16[32,4,4,1,2,16,128]{6,5,4,2,1,3,0:T(8,128)(2,1)}, u32[]{:S(2)}, u32[]{:S(2)}) async-start(bf16[32,4,4,1,2,16,128]{6,5,4,2,1,3,0:T(8,128)(2,1)} %bitcast.224), calls=%async_computation.1 | async-start | bytes 8388608 | tf_op jit(solution)/shard_map/all_to_all | solution.py:335
  132.7 4.5 %copy.196.valid_ref = f32[1,32,256,1]{3,2,1,0:T(8,128)} copy(f32[1,32,256,1]{1,2,3,0:T(8,128)S(1)} %get-tuple-element.59) | data formatting | bytes 65536 | tf_op jit(solution)/shard_map/broadcast_in_dim | solution.py:142
  137.8 20.0 %shard_map.109 = (f32[1,1,320]{2,1,0:T(1,128)}, f32[1,1,320]{2,1,0:T(1,128)}, f32[1,320,128]{2,1,0:T(8,128)}) custom-call(bf16[1,320,128]{2,1,0:T(8,128)(2,1)} %slice.141.q_ref, bf16[32,1,16,2,16,128]{5,4,3,2,1,0:T(8,128)(2,1)} %bitcast.64.kv_ref, f32[1,32,256,1]{3,2,1,0:T(8,128)} %copy.196.valid_ref, f32[1,8,128]{2,1,0:T(8,128)} %get-tuple-element.77.table_ref), custom_call_target="tpu_custom_call" | custom-call | tf_op jit(solution)/shard_map/pallas_call | solution.py:143
  161.0 4.1 %convolution_convert_fusion.1 = bf16[64,5120]{1,0:T(8,128)(2,1)S(1)} fusion(bf16[640,5120]{1,0:T(8,128)(2,1)} %param.21, bf16[8,8,5,128]{3,2,1,0:T(8,128)(2,1)S(1)} %bitcast.236), kind=kOutput, calls=%fused_computation.15 | convolution fusion | flops 419758080 | bytes 7290880 | tf_op jit(solution)/shard_map/rqh,hm->rqm/dot_general | solution.py:368
  167.7 2.4 collective-permute-start.11
  175.9 4.5 %copy.205.valid_ref = f32[1,32,256,1]{3,2,1,0:T(8,128)} copy(f32[1,32,256,1]{1,2,3,0:T(8,128)S(1)} %get-tuple-element.58) | data formatting | bytes 65536 | tf_op jit(solution)/shard_map/broadcast_in_dim | solution.py:142
  180.9 42.2 %all-to-all-done.1 = bf16[32,4,4,1,2,16,128]{6,5,4,2,1,3,0:T(8,128)(2,1)} async-done(((bf16[32,4,4,1,2,16,128]{6,5,4,2,1,3,0:T(8,128)(2,1)}), bf16[32,4,4,1,2,16,128]{6,5,4,2,1,3,0:T(8,128)(2,1)}, u32[]{:S(2)}, u32[]{:S(2)}) %all-to-all-start.1) | async-done | bytes 4194336 | tf_op jit(solution)/shard_map/all_to_all | solution.py:335
  223.1 20.1 %shard_map.110 = (f32[1,1,320]{2,1,0:T(1,128)}, f32[1,1,320]{2,1,0:T(1,128)}, f32[1,320,128]{2,1,0:T(8,128)}) custom-call(bf16[1,320,128]{2,1,0:T(8,128)(2,1)} %slice.160.q_ref, bf16[32,1,16,2,16,128]{5,4,3,2,1,0:T(8,128)(2,1)} %bitcast.84.kv_ref, f32[1,32,256,1]{3,2,1,0:T(8,128)} %copy.205.valid_ref, f32[1,8,128]{2,1,0:T(8,128)} %get-tuple-element.76.table_ref), custom_call_target="tpu_custom_call" | custom-call | tf_op jit(solution)/shard_map/pallas_call | solution.py:143
  246.4 4.3 %convolution_convert_fusion = bf16[64,5120]{1,0:T(8,128)(2,1)S(1)} fusion(bf16[640,5120]{1,0:T(8,128)(2,1)} %param.21, bf16[8,8,5,128]{3,2,1,0:T(8,128)(2,1)S(1)} %bitcast.237), kind=kOutput, calls=%fused_computation.14 | convolution fusion | flops 419758080 | bytes 7290880 | tf_op jit(solution)/shard_map/rqh,hm->rqm/dot_general | solution.py:368
  250.8 18.4 %all_to_all.15 = bf16[8,1,64,640]{3,2,1,0:T(8,128)(2,1)S(1)} all-to-all(bf16[8,1,64,640]{3,2,1,0:T(8,128)(2,1)S(1)} %bitcast.231), channel_id=1, replica_groups=mesh['pool'=32,'tp'=8] {'tp'}, dimensions={0} | all-to-all | bytes 1310720 | tf_op jit(solution)/shard_map/all_to_all | solution.py:382
  (176 shorter events, 47.0 us)
Async XLA Ops:
  0.0 66.3 %collective-permute-start = (bf16[2,4,104,640]{3,2,1,0:T(8,128)(2,1)}, bf16[2,4,104,640]{3,2,1,0:T(8,128)(2,1)}, u32[]{:S(2)}, u32[]{:S(2)}) collective-permute-start(bf16[2,4,104,640]{3,2,1,0:T(8,128)(2,1)} %param.19), channel_id=1, source_target_pairs={{0,1},{1,2},{2,3},{3,4},{4,5},{5,6},{6,7},{7,0},{8,9},{9,10},{10,1... | collective-permute-start | bytes 3194888 | tf_op jit(solution)/shard_map/ppermute | solution.py:269
  2.6 95.4 %collective-permute-start.1 = (bf16[2,4,104,640]{3,2,1,0:T(8,128)(2,1)}, bf16[2,4,104,640]{3,2,1,0:T(8,128)(2,1)}, u32[]{:S(2)}, u32[]{:S(2)}) collective-permute-start(bf16[2,4,104,640]{3,2,1,0:T(8,128)(2,1)} %param.19), channel_id=1, source_target_pairs={{0,2},{1,3},{2,4},{3,5},{4,6},{5,7},{6,0},{7,1},{8,10},{9,11},{10,... | collective-permute-start | bytes 3194888 | tf_op jit(solution)/shard_map/ppermute | solution.py:269
  3.8 95.6 %collective-permute-start.2 = (bf16[2,4,104,640]{3,2,1,0:T(8,128)(2,1)}, bf16[2,4,104,640]{3,2,1,0:T(8,128)(2,1)}, u32[]{:S(2)}, u32[]{:S(2)}) collective-permute-start(bf16[2,4,104,640]{3,2,1,0:T(8,128)(2,1)} %param.19), channel_id=1, source_target_pairs={{0,3},{1,4},{2,5},{3,6},{4,7},{5,0},{6,1},{7,2},{8,11},{9,12},{10,... | collective-permute-start | bytes 3194888 | tf_op jit(solution)/shard_map/ppermute | solution.py:269
  5.4 95.5 %collective-permute-start.3 = (bf16[2,4,104,640]{3,2,1,0:T(8,128)(2,1)}, bf16[2,4,104,640]{3,2,1,0:T(8,128)(2,1)}, u32[]{:S(2)}, u32[]{:S(2)}) collective-permute-start(bf16[2,4,104,640]{3,2,1,0:T(8,128)(2,1)} %param.19), channel_id=1, source_target_pairs={{0,4},{1,5},{2,6},{3,7},{4,0},{5,1},{6,2},{7,3},{8,12},{9,13},{10,... | collective-permute-start | bytes 3194888 | tf_op jit(solution)/shard_map/ppermute | solution.py:269
  7.0 95.3 %collective-permute-start.4 = (bf16[2,4,104,640]{3,2,1,0:T(8,128)(2,1)}, bf16[2,4,104,640]{3,2,1,0:T(8,128)(2,1)}, u32[]{:S(2)}, u32[]{:S(2)}) collective-permute-start(bf16[2,4,104,640]{3,2,1,0:T(8,128)(2,1)} %param.19), channel_id=1, source_target_pairs={{0,5},{1,6},{2,7},{3,0},{4,1},{5,2},{6,3},{7,4},{8,13},{9,14},{10,... | collective-permute-start | bytes 3194888 | tf_op jit(solution)/shard_map/ppermute | solution.py:269
  17.9 107.0 %all-to-all-start = ((bf16[32,4,4,1,2,16,128]{6,5,4,2,1,3,0:T(8,128)(2,1)}), bf16[32,4,4,1,2,16,128]{6,5,4,2,1,3,0:T(8,128)(2,1)}, u32[]{:S(2)}, u32[]{:S(2)}) async-start(bf16[32,4,4,1,2,16,128]{6,5,4,2,1,3,0:T(8,128)(2,1)} %bitcast.225), calls=%async_computation | async-start | bytes 8388608 | tf_op jit(solution)/shard_map/all_to_all | solution.py:335
  32.0 23.2 %copy-start.3 = (bf16[5120,2,1,128]{3,1,2,0:T(2,128)(2,1)S(1)}, bf16[5120,2,1,128]{3,1,2,0:T(2,128)(2,1)}, u32[]{:S(2)}) copy-start(bf16[5120,2,1,128]{3,1,2,0:T(2,128)(2,1)} %param.20) | copy-start | bytes 7864324
  54.8 64.9 %copy-start.4 = (bf16[2,64,5,64]{3,1,2,0:T(8,128)(2,1)}, bf16[2,64,5,64]{3,1,2,0:T(8,128)(2,1)S(1)}, u32[]{:S(2)}) copy-start(bf16[2,64,5,64]{3,1,2,0:T(8,128)(2,1)S(1)} %get-tuple-element.54) | copy-start | bytes 245764
  54.8 64.9 %copy-start.6 = (bf16[2,64,5,64]{3,1,2,0:T(8,128)(2,1)}, bf16[2,64,5,64]{3,1,2,0:T(8,128)(2,1)S(1)}, u32[]{:S(2)}) copy-start(bf16[2,64,5,64]{3,1,2,0:T(8,128)(2,1)S(1)} %get-tuple-element.55) | copy-start | bytes 245764
  66.2 93.5 %copy-start.11 = (f32[2,64,1,5,128]{4,1,3,0,2:T(8,128)}, f32[2,64,1,5,128]{4,1,3,0,2:T(8,128)S(1)}, u32[]{:S(2)}) copy-start(f32[2,64,1,5,128]{4,1,3,0,2:T(8,128)S(1)} %convolution_bitcast_fusion.1) | copy-start | bytes 983044
  66.3 37.4 %collective-permute-start.5 = (bf16[2,4,104,640]{3,2,1,0:T(8,128)(2,1)S(1)}, bf16[2,4,104,640]{3,2,1,0:T(8,128)(2,1)S(1)}, u32[]{:S(2)}, u32[]{:S(2)}) collective-permute-start(bf16[2,4,104,640]{3,2,1,0:T(8,128)(2,1)S(1)} %copy-done.13), channel_id=1, source_target_pairs={{0,6},{1,7},{2,0},{3,1},{4,2},{5,3},{6,4},{7,5},{8,14},{9,15},{10,... | collective-permute-start | bytes 3194888 | tf_op jit(solution)/shard_map/ppermute | solution.py:269
  98.0 14.8 %collective-permute-start.6 = (bf16[2,4,104,640]{3,2,1,0:T(8,128)(2,1)S(1)}, bf16[2,4,104,640]{3,2,1,0:T(8,128)(2,1)S(1)}, u32[]{:S(2)}, u32[]{:S(2)}) collective-permute-start(bf16[2,4,104,640]{3,2,1,0:T(8,128)(2,1)S(1)} %copy-done.13), channel_id=1, source_target_pairs={{0,7},{1,0},{2,1},{3,2},{4,3},{5,4},{6,5},{7,6},{8,15},{9,8},{10,9... | collective-permute-start | bytes 3194888 | tf_op jit(solution)/shard_map/ppermute | solution.py:269
  124.9 34.8 %copy-start.9 = (f32[2,64,1,5,128]{4,1,3,0,2:T(8,128)}, f32[2,64,1,5,128]{4,1,3,0,2:T(8,128)S(1)}, u32[]{:S(2)}) copy-start(f32[2,64,1,5,128]{4,1,3,0,2:T(8,128)S(1)} %convolution_bitcast_fusion) | copy-start | bytes 983044
  124.9 98.2 %all-to-all-start.1 = ((bf16[32,4,4,1,2,16,128]{6,5,4,2,1,3,0:T(8,128)(2,1)}), bf16[32,4,4,1,2,16,128]{6,5,4,2,1,3,0:T(8,128)(2,1)}, u32[]{:S(2)}, u32[]{:S(2)}) async-start(bf16[32,4,4,1,2,16,128]{6,5,4,2,1,3,0:T(8,128)(2,1)} %bitcast.224), calls=%async_computation.1 | async-start | bytes 8388608 | tf_op jit(solution)/shard_map/all_to_all | solution.py:335
  166.1 7.2 %collective-permute-start.10 = (bf16[1,64,640]{2,1,0:T(8,128)(2,1)S(1)}, bf16[1,64,640]{2,1,0:T(8,128)(2,1)S(1)}, u32[]{:S(2)}, u32[]{:S(2)}) collective-permute-start(bf16[1,64,640]{2,1,0:T(8,128)(2,1)S(1)} %get-tuple-element.49), channel_id=1, source_target_pairs={{0,4},{1,5},{2,6},{3,7},{4,0},{5,1},{6,2},{7,3},{8,12},{9,13},{10,... | collective-permute-start | bytes 245768 | tf_op jit(solution)/shard_map/ppermute | solution.py:375
  167.7 6.3 %collective-permute-start.11 = (bf16[1,64,640]{2,1,0:T(8,128)(2,1)S(1)}, bf16[1,64,640]{2,1,0:T(8,128)(2,1)S(1)}, u32[]{:S(2)}, u32[]{:S(2)}) collective-permute-start(bf16[1,64,640]{2,1,0:T(8,128)(2,1)S(1)} %get-tuple-element.48), channel_id=1, source_target_pairs={{0,5},{1,6},{2,7},{3,0},{4,1},{5,2},{6,3},{7,4},{8,13},{9,14},{10,... | collective-permute-start | bytes 245768 | tf_op jit(solution)/shard_map/ppermute | solution.py:375
  170.8 9.6 %collective-permute-start.12 = (bf16[1,64,640]{2,1,0:T(8,128)(2,1)S(1)}, bf16[1,64,640]{2,1,0:T(8,128)(2,1)S(1)}, u32[]{:S(2)}, u32[]{:S(2)}) collective-permute-start(bf16[1,64,640]{2,1,0:T(8,128)(2,1)S(1)} %get-tuple-element.47), channel_id=1, source_target_pairs={{0,6},{1,7},{2,0},{3,1},{4,2},{5,3},{6,4},{7,5},{8,14},{9,15},{10,... | collective-permute-start | bytes 245768 | tf_op jit(solution)/shard_map/ppermute | solution.py:375
  171.6 8.9 %collective-permute-start.13 = (bf16[1,64,640]{2,1,0:T(8,128)(2,1)S(1)}, bf16[1,64,640]{2,1,0:T(8,128)(2,1)S(1)}, u32[]{:S(2)}, u32[]{:S(2)}) collective-permute-start(bf16[1,64,640]{2,1,0:T(8,128)(2,1)S(1)} %get-tuple-element.46), channel_id=1, source_target_pairs={{0,7},{1,0},{2,1},{3,2},{4,3},{5,4},{6,5},{7,6},{8,15},{9,8},{10,9... | collective-permute-start | bytes 245768 | tf_op jit(solution)/shard_map/ppermute | solution.py:375
  171.6 8.9 %collective-permute-start.7 = (bf16[1,64,640]{2,1,0:T(8,128)(2,1)S(1)}, bf16[1,64,640]{2,1,0:T(8,128)(2,1)S(1)}, u32[]{:S(2)}, u32[]{:S(2)}) collective-permute-start(bf16[1,64,640]{2,1,0:T(8,128)(2,1)S(1)} %get-tuple-element.45), channel_id=1, source_target_pairs={{0,1},{1,2},{2,3},{3,4},{4,5},{5,6},{6,7},{7,0},{8,9},{9,10},{10,1... | collective-permute-start | bytes 245768 | tf_op jit(solution)/shard_map/ppermute | solution.py:375
  173.3 7.2 %collective-permute-start.8 = (bf16[1,64,640]{2,1,0:T(8,128)(2,1)S(1)}, bf16[1,64,640]{2,1,0:T(8,128)(2,1)S(1)}, u32[]{:S(2)}, u32[]{:S(2)}) collective-permute-start(bf16[1,64,640]{2,1,0:T(8,128)(2,1)S(1)} %get-tuple-element.51), channel_id=1, source_target_pairs={{0,2},{1,3},{2,4},{3,5},{4,6},{5,7},{6,0},{7,1},{8,10},{9,11},{10,... | collective-permute-start | bytes 245768 | tf_op jit(solution)/shard_map/ppermute | solution.py:375
  174.0 6.8 %collective-permute-start.9 = (bf16[1,64,640]{2,1,0:T(8,128)(2,1)S(1)}, bf16[1,64,640]{2,1,0:T(8,128)(2,1)S(1)}, u32[]{:S(2)}, u32[]{:S(2)}) collective-permute-start(bf16[1,64,640]{2,1,0:T(8,128)(2,1)S(1)} %get-tuple-element.50), channel_id=1, source_target_pairs={{0,3},{1,4},{2,5},{3,6},{4,7},{5,0},{6,1},{7,2},{8,11},{9,12},{10,... | collective-permute-start | bytes 245768 | tf_op jit(solution)/shard_map/ppermute | solution.py:375
  223.1 21.9 %copy-start.10 = (f32[2,64,1,5,128]{4,1,3,0,2:T(8,128)S(1)}, f32[2,64,1,5,128]{4,1,3,0,2:T(8,128)}, u32[]{:S(2)}) copy-start(f32[2,64,1,5,128]{4,1,3,0,2:T(8,128)} %copy-done.9) | copy-start | bytes 983044
  223.1 21.9 %copy-start.12 = (f32[2,64,1,5,128]{4,1,3,0,2:T(8,128)S(1)}, f32[2,64,1,5,128]{4,1,3,0,2:T(8,128)}, u32[]{:S(2)}) copy-start(f32[2,64,1,5,128]{4,1,3,0,2:T(8,128)} %copy-done.11) | copy-start | bytes 983044
  246.4 23.6 %copy-start.1 = (bf16[256,1,2,16,128]{4,3,2,1,0:T(8,128)(2,1)S(1)}, bf16[256,1,2,16,128]{4,3,2,1,0:T(8,128)(2,1)}, u32[]{:S(2)}) copy-start(bf16[256,1,2,16,128]{4,3,2,1,0:T(8,128)(2,1)} %param.11) | copy-start | bytes 6291460
  (12 other events, 105.4 us)
